TPU v7x, 256 devices: a whole 4x4x8 slice. The times are simulated.
256 devices in a mesh: dp: 8 (over x, core), expert: 32 (over y, z).
Axes of the slice: x: 4, y: 4, z: 8, core: 2. Of those that a mesh axis runs over, the one named last changes fastest.
Arguments:
- tokens: bfloat16 [12288, 2048], P(('dp', 'expert')), may hold values from -6 to 6
- routes: int32 [12288, 6], P(('dp', 'expert')), may hold values from 0 to 31, all different within a row; in each aligned block of 48 rows (0 to 47, 48 to 95, ...) at most 12 rows name the same one
- gates: float32 [12288, 6], P(('dp', 'expert')), may hold values from 0.02 to 0.5
- cotangent: bfloat16 [12288, 2048], P(('dp', 'expert')), may hold values from -6 to 6
- swap_flag: int32 [32], replicated, may hold values from 0 to 1, as said below
- w_up: bfloat16 [32, 2048, 1408], P('expert', 'dp'), may hold values from -0.125 to 0.125
- w_down: bfloat16 [32, 1408, 2048], P('expert', 'dp'), may hold values from -0.15625 to 0.15625
- m_up: bfloat16 [32, 2048, 1408], P('expert', 'dp'), may hold values from -12 to 12
- v_up: bfloat16 [32, 2048, 1408], P('expert', 'dp'), may hold values from 1 to 50
- m_down: bfloat16 [32, 1408, 2048], P('expert', 'dp'), may hold values from -12 to 12
- v_down: bfloat16 [32, 1408, 2048], P('expert', 'dp'), may hold values from 1 to 50
Outputs:
- mixed: bfloat16 [12288, 2048], P(('dp', 'expert'))
- input_grad: bfloat16 [12288, 2048], P(('dp', 'expert'))
- new_w_up: bfloat16 [32, 2048, 1408], P('expert', 'dp')
- new_w_down: bfloat16 [32, 1408, 2048], P('expert', 'dp')
- new_m_up: bfloat16 [32, 2048, 1408], P('expert', 'dp')
- new_v_up: bfloat16 [32, 2048, 1408], P('expert', 'dp')
- new_m_down: bfloat16 [32, 1408, 2048], P('expert', 'dp')
- new_v_down: bfloat16 [32, 1408, 2048], P('expert', 'dp')
Inputs may be any that keep to these rules, and one draw needn't show every extreme that they name: `routes`: in each aligned block of 48 rows (the tokens of one device) no expert is chosen by more than 12 rows, a bound that some block reaches; the 6 experts of a row differ. swap_flag[e] == swap_flag[e xor 1] for every e; the pairs of experts 0 and 2 * (8) trade places in every draw, and some other pair stays.
All inputs are finite; a program needn't handle non-finite values.
Results may differ from a plain program's by a relative error of at most 0.015.
Values may be sent and summed in bfloat16 or wider, within the bound.
No kernel may reach another device: no remote copies, remote signals or barrier semaphores. Data moves between devices by JAX's collectives and lax.ppermute only.
A program may use at most 128 MiB of HBM per device.

v0:
```python
import jax
import jax.numpy as jnp
from jax import lax
from jax.sharding import PartitionSpec as P

ADAM_STEP = 10


beta_one = 0.9
beta_two = 0.95
learn_rate = 0.001
adam_eps = 1e-08


def partner(value, axis, distance):
    mask = 2**distance
    pairs = [(source, source ^ mask) for source in range(lax.axis_size(axis))]
    return lax.ppermute(value, axis, pairs)


def silu_slope(value):
    sigma = jax.nn.sigmoid(value)
    return sigma * (1.0 + value * (1.0 - sigma))


def adam_update(weight, first_moment, second_moment, gradient):
    first_new = beta_one * first_moment.astype(jnp.float32) + (1.0 - beta_one) * gradient
    second_new = (
        beta_two * second_moment.astype(jnp.float32) + (1.0 - beta_two) * gradient * gradient
    )
    correct_one = 1.0 - beta_one**ADAM_STEP
    correct_two = 1.0 - beta_two**ADAM_STEP
    weight_new = weight.astype(jnp.float32) - learn_rate * (first_new / correct_one) / (
        jnp.sqrt(second_new / correct_two) + adam_eps
    )
    return (
        weight_new.astype(jnp.bfloat16),
        first_new.astype(jnp.bfloat16),
        second_new.astype(jnp.bfloat16),
    )


def contract_rows(left, right):
    return lax.dot_general(
        left, right, (((0,), (0,)), ((), ())), preferred_element_type=jnp.float32
    )


def contract_cols(left, right):
    return lax.dot_general(
        left, right, (((1,), (1,)), ((), ())), preferred_element_type=jnp.float32
    )


def stack_state(members):
    return jnp.stack([member.reshape(-1) for member in members])


def unstack_state(stacked, member_shapes):
    return tuple(
        (stacked[number].reshape(member_shape) for number, member_shape in enumerate(member_shapes))
    )


def body(tokens, routes, gates, cotangent, swap_flag, w_up, w_down, m_up, v_up, m_down, v_down):
    experts = lax.axis_size("expert")
    my_slot = lax.axis_index("expert")
    tok_count, model_width = tokens.shape
    chosen = routes.shape[1]
    pair_count = tok_count * chosen
    capacity = pair_count * 4 // (3 * experts)
    row_total = experts * capacity
    my_flag = swap_flag[my_slot]
    swapped = my_flag == 1
    w_up_in = partner(w_up, "expert", 0)
    w_down_in = partner(w_down, "expert", 0)
    up_moments = partner(jnp.concatenate([m_up, v_up], axis=0), "expert", 0)
    down_moments = partner(jnp.concatenate([m_down, v_down], axis=0), "expert", 0)
    w_up_use = jnp.where(swapped, w_up_in, w_up)
    w_down_use = jnp.where(swapped, w_down_in, w_down)
    m_up_use = jnp.where(swapped, up_moments[0:1], m_up)
    v_up_use = jnp.where(swapped, up_moments[1:2], v_up)
    m_down_use = jnp.where(swapped, down_moments[0:1], m_down)
    v_down_use = jnp.where(swapped, down_moments[1:2], v_down)
    flat_routes = routes.reshape(pair_count)
    dest_routes = jnp.bitwise_xor(flat_routes, swap_flag[flat_routes])
    one_hot = (dest_routes[:, None] == jnp.arange(experts, dtype=jnp.int32)[None, :]).astype(
        jnp.int32
    )
    position = jnp.sum(jnp.cumsum(one_hot, axis=0) * one_hot, axis=1) - 1
    slot_index = dest_routes * capacity + position
    source = (
        jnp.full((row_total,), -1, jnp.int32)
        .at[slot_index]
        .set(jnp.arange(pair_count, dtype=jnp.int32))
    )
    is_live = source >= 0
    safe_source = jnp.maximum(source, 0)
    token_ids = safe_source // chosen
    send_tokens = jnp.where(
        is_live[:, None], tokens[token_ids], jnp.zeros((), jnp.bfloat16)
    ).reshape(experts, capacity, model_width)
    live_gates = jnp.where(is_live, gates.reshape(pair_count)[safe_source], 0.0)
    send_grads = (
        (live_gates[:, None] * cotangent[token_ids].astype(jnp.float32))
        .astype(jnp.bfloat16)
        .reshape(experts, capacity, model_width)
    )
    up_full = lax.all_gather(w_up_use, "dp", axis=1, tiled=True)[0]
    down_full = lax.all_gather(w_down_use, "dp", axis=1, tiled=True)[0]
    got_both = lax.all_to_all(
        jnp.concatenate([send_tokens, send_grads], axis=1),
        "expert",
        split_axis=0,
        concat_axis=0,
        tiled=True,
    )
    expert_rows = got_both[:, :capacity].reshape(row_total, model_width)
    grad_rows = got_both[:, capacity:].reshape(row_total, model_width)
    up_act = jnp.dot(expert_rows, up_full, preferred_element_type=jnp.float32)
    hidden = jax.nn.silu(up_act).astype(jnp.bfloat16)
    expert_out = jnp.dot(hidden, down_full, preferred_element_type=jnp.float32).astype(jnp.bfloat16)
    returned = lax.all_to_all(
        expert_out.reshape(experts, capacity, model_width),
        "expert",
        split_axis=0,
        concat_axis=0,
        tiled=True,
    )
    picked = returned.reshape(row_total, model_width)[slot_index].reshape(
        tok_count, chosen, model_width
    )
    mixed = jnp.sum(gates[:, :, None] * picked.astype(jnp.float32), axis=1).astype(jnp.bfloat16)
    hidden_grad = contract_cols(grad_rows, down_full)
    up_grad = (hidden_grad * silu_slope(up_act)).astype(jnp.bfloat16)
    input_part = contract_cols(up_grad, up_full).astype(jnp.bfloat16)
    back_grads = lax.all_to_all(
        input_part.reshape(experts, capacity, model_width),
        "expert",
        split_axis=0,
        concat_axis=0,
        tiled=True,
    )
    picked_grad = back_grads.reshape(row_total, model_width)[slot_index].reshape(
        tok_count, chosen, model_width
    )
    input_grad = jnp.sum(picked_grad.astype(jnp.float32), axis=1).astype(jnp.bfloat16)
    up_gradient = lax.psum_scatter(
        contract_rows(expert_rows, up_grad).astype(jnp.bfloat16),
        "dp",
        scatter_dimension=0,
        tiled=True,
    ).astype(jnp.float32)
    down_gradient = lax.psum_scatter(
        contract_rows(hidden, grad_rows).astype(jnp.bfloat16),
        "dp",
        scatter_dimension=0,
        tiled=True,
    ).astype(jnp.float32)
    up_new = adam_update(w_up_use[0], m_up_use[0], v_up_use[0], up_gradient)
    down_new = adam_update(w_down_use[0], m_down_use[0], v_down_use[0], down_gradient)
    return (
        mixed,
        input_grad,
        up_new[0][None],
        down_new[0][None],
        up_new[1][None],
        up_new[2][None],
        down_new[1][None],
        down_new[2][None],
    )


def solution(mesh):
    return jax.shard_map(
        body,
        mesh=mesh,
        in_specs=(
            P(("dp", "expert"), None),
            P(("dp", "expert"), None),
            P(("dp", "expert"), None),
            P(("dp", "expert"), None),
            P(),
            P("expert", "dp", None),
            P("expert", "dp", None),
            P("expert", "dp", None),
            P("expert", "dp", None),
            P("expert", "dp", None),
            P("expert", "dp", None),
        ),
        out_specs=(
            P(("dp", "expert"), None),
            P(("dp", "expert"), None),
            P("expert", "dp", None),
            P("expert", "dp", None),
            P("expert", "dp", None),
            P("expert", "dp", None),
            P("expert", "dp", None),
            P("expert", "dp", None),
        ),
        check_vma=False,
    )
```

profile of v0, /device:TPU:6, one launch (start us, length us, event | category | flops | bytes accessed | tf_op | source)
XLA Modules:
  0.0 441.1 jit_solution(2398692835408480219)
XLA Ops:
  14.7 4.3 fusion.38
  19.0 6.6 %collective-permute-done = bf16[1,256,1408]{2,1,0:T(8,128)(2,1)S(1)} collective-permute-done((bf16[1,256,1408]{2,1,0:T(8,128)(2,1)}, bf16[1,256,1408]{2,1,0:T(8,128)(2,1)S(1)}, u32[]{:S(2)}, u32[]{:S(2)}) %collective-permute-start) | collective-permute-done | bytes 720928 | tf_op jit(solution)/shard_map/ppermute | solution.py:18
  27.1 15.6 %fusion.42 = (s32[288]{0:T(512)S(1)}, s32[288]{0:T(512)S(1)}) fusion(s32[288]{0:T(512)S(1)} %reshape.168, pred[288]{0:T(512)(128)(4,1)S(1)} %get-tuple-element.32, pred[288]{0:T(512)(128)(4,1)S(1)} %get-tuple-element.31, pred[288]{0:T(512)(128)(4,1)S(1)} %get-tuple-element.30, pred[288]{0:T(512)(128)(4,1)S(1)} %get-tuple-element.29, ...), kind=kLoop, calls=%fused_computation.115 | loop fusion | flops 7488 | bytes 11908 | tf_op jit(solution)/shard_map/xor | solution.py:86
  44.1 2.9 scatter_custom_fusion
  47.0 2.8 gather_fusion.1
  50.1 3.1 gather_fusion.2
  53.2 3.2 gather_fusion
  56.4 2.4 gather.25
  58.8 3.9 reshape.180
  66.3 85.0 %all_to_all.15 = bf16[32,24,2048]{2,1,0:T(8,128)(2,1)S(1)} all-to-all(bf16[32,24,2048]{2,1,0:T(8,128)(2,1)S(1)} %pad_maximum_fusion), channel_id=1, replica_groups=mesh['dp'=8,'expert'=32] {'expert'}, dimensions={0} | all-to-all | bytes 6291456 | tf_op jit(solution)/shard_map/all_to_all | solution.py:111
  153.6 3.6 reshape.172
  158.7 5.8 %fusion.6 = f32[384,1408]{1,0:T(8,128)S(1)} fusion(bf16[384,2048]{1,0:T(8,128)(2,1)} %reshape.172, bf16[1,2048,1408]{2,1,0:T(8,128)(2,1)} %all-gather.3.cloned.1.call-done), kind=kOutput, calls=%fused_computation.14 | convolution fusion | flops 2214592512 | bytes 9502720 | tf_op jit(solution)/shard_map/dot_general | solution.py:120
  165.9 5.1 %convolution_convert_fusion = bf16[1408,2048]{1,0:T(8,128)(2,1)} fusion(bf16[384,2048]{1,0:T(8,128)(2,1)S(1)} %copy-done.9, f32[384,1408]{1,0:T(8,128)S(1)} %fusion.6), kind=kOutput, calls=%fused_computation.6 | convolution fusion | flops 2220179456 | bytes 9502720 | tf_op jit(solution)/shard_map/dot_general | solution.py:44
  174.9 43.2 %collective-permute-done.1 = bf16[1,176,2048]{2,1,0:T(8,128)(2,1)S(1)} collective-permute-done((bf16[1,176,2048]{2,1,0:T(8,128)(2,1)S(1)}, bf16[1,176,2048]{2,1,0:T(8,128)(2,1)S(1)}, u32[]{:S(2)}, u32[]{:S(2)}) %collective-permute-start.1) | collective-permute-done | bytes 720928 | tf_op jit(solution)/shard_map/ppermute | solution.py:18
  219.0 5.2 %fusion.35 = (bf16[1,176,2048]{2,1,0:T(8,128)(2,1)}, bf16[1,176,2048]{2,1,0:T(8,128)(2,1)}, bf16[1,176,2048]{2,1,0:T(8,128)(2,1)}, bf16[1,176,2048]{2,1,0:T(8,128)(2,1)}) fusion(bf16[176,2048]{1,0:T(8,128)(2,1)} %reduce-scatter.5.cloned.1.call-done, bf16[1,176,2048]{2,1,0:T(8,128)(2,1)S(1)} %copy-done.6, bf16[2,176,2048]{2,1,0:T(8,128)(2,1)} %collective-permute-done.3, ...), kind=kLoop, calls=%fused_computation.55 | loop fusion | flops 7929856 | bytes 7929857 | tf_op jit(solution)/shard_map/broadcast_in_dim | solution.py:166
  224.4 37.9 %all-gather.5.cloned.1.call-done = bf16[1,1408,2048]{2,1,0:T(8,128)(2,1)} async-done(((bf16[1,176,2048]{2,1,0:T(8,128)(2,1)}), bf16[1,1408,2048]{2,1,0:T(8,128)(2,1)}) %all-gather.5.cloned.1.call-update) | async-done | bytes 5767184 | tf_op jit(solution)/shard_map/all_gather | solution.py:110
  262.3 7.2 %fusion.11 = bf16[384,1408]{1,0:T(8,128)(2,1)S(1)} fusion(bf16[384,2048]{1,0:T(8,128)(2,1)S(1)} %copy-done.9, bf16[1,1408,2048]{2,1,0:T(8,128)(2,1)} %all-gather.5.cloned.1.call-done, f32[384,1408]{1,0:T(8,128)} %copy-done.15), kind=kOutput, calls=%fused_computation.20 | convolution fusion | flops 2219458560 | bytes 10584064 | tf_op jit(solution)/shard_map/dot_general | solution.py:50
  270.5 5.1 %convolution_convert_fusion.1 = bf16[2048,1408]{1,0:T(8,128)(2,1)} fusion(bf16[384,2048]{1,0:T(8,128)(2,1)S(1)} %copy-done.8, bf16[384,1408]{1,0:T(8,128)(2,1)S(1)} %fusion.11), kind=kOutput, calls=%fused_computation.7 | convolution fusion | flops 2217476096 | bytes 8421376 | tf_op jit(solution)/shard_map/dot_general | solution.py:44
  276.9 5.3 %fusion.14 = bf16[384,2048]{1,0:T(8,128)(2,1)S(1)} fusion(bf16[384,1408]{1,0:T(8,128)(2,1)S(1)} %copy-done.14, bf16[1,2048,1408]{2,1,0:T(8,128)(2,1)} %all-gather.3.cloned.1.call-done), kind=kOutput, calls=%fused_computation.21 | convolution fusion | flops 2215378944 | bytes 8421376 | tf_op jit(solution)/shard_map/dot_general | solution.py:50
  283.7 9.9 %all-to-all-start.2 = ((bf16[32,12,2048]{2,1,0:T(8,128)(2,1)}), bf16[32,12,2048]{2,1,0:T(8,128)(2,1)S(1)}, u32[]{:S(2)}, u32[]{:S(2)}) async-start(bf16[32,12,2048]{2,1,0:T(8,128)(2,1)} %reshape.176), calls=%async_computation.2 | async-start | bytes 4194304 | tf_op jit(solution)/shard_map/all_to_all | solution.py:137
  293.6 7.3 %fusion.17 = bf16[384,2048]{1,0:T(8,128)(2,1)} fusion(bf16[1,1408,2048]{2,1,0:T(8,128)(2,1)} %all-gather.5.cloned.1.call-done, f32[384,1408]{1,0:T(8,128)} %copy-done.15), kind=kOutput, calls=%fused_computation.22 | convolution fusion | flops 2218082304 | bytes 9502720 | tf_op jit(solution)/shard_map/dot_general | solution.py:122
  300.9 3.7 reshape.173
  304.5 39.5 %all-to-all-done.2 = bf16[32,12,2048]{2,1,0:T(8,128)(2,1)S(1)} async-done(((bf16[32,12,2048]{2,1,0:T(8,128)(2,1)}), bf16[32,12,2048]{2,1,0:T(8,128)(2,1)S(1)}, u32[]{:S(2)}, u32[]{:S(2)}) %all-to-all-start.2) | async-done | bytes 1572896 | tf_op jit(solution)/shard_map/all_to_all | solution.py:137
  345.3 6.6 %all-to-all-start.1 = ((bf16[32,12,2048]{2,1,0:T(8,128)(2,1)}), bf16[32,12,2048]{2,1,0:T(8,128)(2,1)}, u32[]{:S(2)}, u32[]{:S(2)}) async-start(bf16[32,12,2048]{2,1,0:T(8,128)(2,1)} %reshape.173), calls=%async_computation.1 | async-start | bytes 4194304 | tf_op jit(solution)/shard_map/all_to_all | solution.py:123
  356.0 2.5 reshape.177
  358.5 2.4 gather_fusion.4
  362.3 40.4 %all-to-all-done.1 = bf16[32,12,2048]{2,1,0:T(8,128)(2,1)} async-done(((bf16[32,12,2048]{2,1,0:T(8,128)(2,1)}), bf16[32,12,2048]{2,1,0:T(8,128)(2,1)}, u32[]{:S(2)}, u32[]{:S(2)}) %all-to-all-start.1) | async-done | bytes 1572896 | tf_op jit(solution)/shard_map/all_to_all | solution.py:123
  402.7 2.5 reshape.174
  405.2 3.0 gather_fusion.3
  410.3 3.1 reduce_sum.32
  415.2 14.6 %collective-permute-done.2 = bf16[2,256,1408]{2,1,0:T(8,128)(2,1)} collective-permute-done((bf16[2,256,1408]{2,1,0:T(8,128)(2,1)}, bf16[2,256,1408]{2,1,0:T(8,128)(2,1)}, u32[]{:S(2)}, u32[]{:S(2)}) %collective-permute-start.2) | collective-permute-done | bytes 1441824 | tf_op jit(solution)/shard_map/ppermute | solution.py:18
  429.8 4.8 %fusion.30 = (bf16[1,256,1408]{2,1,0:T(8,128)(2,1)}, bf16[1,256,1408]{2,1,0:T(8,128)(2,1)}, bf16[1,256,1408]{2,1,0:T(8,128)(2,1)}) fusion(bf16[256,1408]{1,0:T(8,128)(2,1)} %reduce-scatter.3.cloned.1.call-done, bf16[1,256,1408]{2,1,0:T(8,128)(2,1)} %param.19, bf16[2,256,1408]{2,1,0:T(8,128)(2,1)} %collective-permute-done.2, pred[]{:T(512)} %bitcast.33, ...), kind=kLoop, calls=%fused_computation.44 | loop fusion | flops 7569408 | bytes 6488065 | tf_op jit(solution)/shard_map/broadcast_in_dim | solution.py:168
  (84 shorter events, 38.2 us)
Async XLA Ops:
  7.2 42.9 %copy-start = (bf16[48,2048]{1,0:T(8,128)(2,1)S(1)}, bf16[48,2048]{1,0:T(8,128)(2,1)}, u32[]{:S(2)}) copy-start(bf16[48,2048]{1,0:T(8,128)(2,1)} %param.14) | copy-start | bytes 589828
  7.2 19.7 %copy-start.12 = (f32[48,6]{0,1:T(8,128)S(1)}, f32[48,6]{0,1:T(8,128)}, u32[]{:S(2)}) copy-start(f32[48,6]{0,1:T(8,128)} %param.13) | copy-start | bytes 3460
  7.2 151.5 %all-gather.3.cloned.1.call-start = ((), (), s32[]{:S(2)}) async-start(), calls=%async_computation.5 | async-start | bytes 6488064 | tf_op jit(solution)/shard_map/all_gather | solution.py:109
  7.2 18.4 %collective-permute-start = (bf16[1,256,1408]{2,1,0:T(8,128)(2,1)}, bf16[1,256,1408]{2,1,0:T(8,128)(2,1)S(1)}, u32[]{:S(2)}, u32[]{:S(2)}) collective-permute-start(bf16[1,256,1408]{2,1,0:T(8,128)(2,1)} %param.16), channel_id=1, source_target_pairs={{0,1},{1,0},{2,3},{3,2},{4,5},{5,4},{6,7},{7,6},{8,9},{9,8},{10,11... | collective-permute-start | bytes 2162696 | tf_op jit(solution)/shard_map/ppermute | solution.py:18
  26.6 192.4 %reduce-scatter.5.cloned.1.call-start = ((), (), s32[]{:S(2)}) async-start(), calls=%async_computation.8 | async-start | bytes 6488064 | tf_op jit(solution)/shard_map/reduce_scatter | solution.py:154
  50.1 3.1 copy-start.2
  62.7 2.3 copy-start.3
  158.6 7.2 %copy-start.9 = (bf16[384,2048]{1,0:T(8,128)(2,1)S(1)}, bf16[384,2048]{1,0:T(8,128)(2,1)}, u32[]{:S(2)}) copy-start(bf16[384,2048]{1,0:T(8,128)(2,1)} %reshape.175) | copy-start | bytes 4718596
  164.5 1.4 copy-start.15
  171.0 1.1 copy-start.6
  171.0 1.3 copy-start.7
  171.0 91.3 %all-gather.5.cloned.1.call-start = ((), (), s32[]{:S(2)}) async-start(), calls=%async_computation.6 | async-start | bytes 6488064 | tf_op jit(solution)/shard_map/all_gather | solution.py:110
  172.3 1.7 copy-start.10
  172.5 46.5 %collective-permute-start.3 = (bf16[2,176,2048]{2,1,0:T(8,128)(2,1)S(1)}, bf16[2,176,2048]{2,1,0:T(8,128)(2,1)}, u32[]{:S(2)}, u32[]{:S(2)}) collective-permute-start(bf16[2,176,2048]{2,1,0:T(8,128)(2,1)S(1)} %pad_maximum_fusion.2), channel_id=1, source_target_pairs={{0,1},{1,0},{2,3},{3,2},{4,5},{5,4},{6,7},{7,6},{8,9},{9,8},{10,11... | collective-permute-start | bytes 4325384 | tf_op jit(solution)/shard_map/ppermute | solution.py:18
  174.0 44.1 %collective-permute-start.1 = (bf16[1,176,2048]{2,1,0:T(8,128)(2,1)S(1)}, bf16[1,176,2048]{2,1,0:T(8,128)(2,1)S(1)}, u32[]{:S(2)}, u32[]{:S(2)}) collective-permute-start(bf16[1,176,2048]{2,1,0:T(8,128)(2,1)S(1)} %copy-done.10), channel_id=1, source_target_pairs={{0,1},{1,0},{2,3},{3,2},{4,5},{5,4},{6,7},{7,6},{8,9},{9,8},{10,11... | collective-permute-start | bytes 2162696 | tf_op jit(solution)/shard_map/ppermute | solution.py:18
  218.1 0.9 copy-start.11
  224.1 46.4 %copy-start.8 = (bf16[384,2048]{1,0:T(8,128)(2,1)S(1)}, bf16[384,2048]{1,0:T(8,128)(2,1)}, u32[]{:S(2)}) copy-start(bf16[384,2048]{1,0:T(8,128)(2,1)} %reshape.172) | copy-start | bytes 4718596
  224.1 205.7 %reduce-scatter.3.cloned.1.call-start = ((), (), s32[]{:S(2)}) async-start(), calls=%async_computation.7 | async-start | bytes 6488064 | tf_op jit(solution)/shard_map/reduce_scatter | solution.py:148
  269.5 1.0 copy-start.13
  275.7 1.2 copy-start.14
  283.7 60.3 %all-to-all-start.2 = ((bf16[32,12,2048]{2,1,0:T(8,128)(2,1)}), bf16[32,12,2048]{2,1,0:T(8,128)(2,1)S(1)}, u32[]{:S(2)}, u32[]{:S(2)}) async-start(bf16[32,12,2048]{2,1,0:T(8,128)(2,1)} %reshape.176), calls=%async_computation.2 | async-start | bytes 4194304 | tf_op jit(solution)/shard_map/all_to_all | solution.py:137
  304.5 47.4 %copy-start.5 = (bf16[1,256,1408]{2,1,0:T(8,128)(2,1)S(1)}, bf16[1,256,1408]{2,1,0:T(8,128)(2,1)}, u32[]{:S(2)}) copy-start(bf16[1,256,1408]{2,1,0:T(8,128)(2,1)} %param.19) | copy-start | bytes 2162692
  344.0 1.3 copy-start.4
  345.3 57.3 %all-to-all-start.1 = ((bf16[32,12,2048]{2,1,0:T(8,128)(2,1)}), bf16[32,12,2048]{2,1,0:T(8,128)(2,1)}, u32[]{:S(2)}, u32[]{:S(2)}) async-start(bf16[32,12,2048]{2,1,0:T(8,128)(2,1)} %reshape.173), calls=%async_computation.1 | async-start | bytes 4194304 | tf_op jit(solution)/shard_map/all_to_all | solution.py:123
  354.3 75.5 %collective-permute-start.2 = (bf16[2,256,1408]{2,1,0:T(8,128)(2,1)}, bf16[2,256,1408]{2,1,0:T(8,128)(2,1)}, u32[]{:S(2)}, u32[]{:S(2)}) collective-permute-start(bf16[2,256,1408]{2,1,0:T(8,128)(2,1)} %pad_maximum_fusion.1), channel_id=1, source_target_pairs={{0,1},{1,0},{2,3},{3,2},{4,5},{5,4},{6,7},{7,6},{8,9},{9,8},{10,11... | collective-permute-start | bytes 4325384 | tf_op jit(solution)/shard_map/ppermute | solution.py:18
  429.8 4.8 %copy-start.1 = (bf16[48,2048]{1,0:T(8,128)(2,1)S(1)}, bf16[48,2048]{1,0:T(8,128)(2,1)}, u32[]{:S(2)}) copy-start(bf16[48,2048]{1,0:T(8,128)(2,1)} %param.14) | copy-start | bytes 589828
Sparse Core Ops, SparseCore 0:
  26.7 43.0 all-gather.2
  171.1 36.9 reduce-scatter.4
  224.3 38.0 all-gather.4
  275.8 42.7 reduce-scatter.2
where the time goes:
time: 445 us; the launch traced here: 441 us
  waiting for transfers between devices  182 us (41%)
  blocking collectives  85 us (19%)
  local copies, waits for them, and re-layouts  59.6 us (13%)
  other arithmetic  40.9 us (9%)
  matrix products  35.7 us (8%)
  starting transfers between devices  23 us (5%)
  between operations  14.7 us (3%)
    all_to_all x1, blocking collectives, body(): lax.all_to_all(jnp.concatenate([send_tokens, send_grads], axis=1), 'exper...  85 us
    ppermute x4, waiting for transfers between devices, partner(): return lax.ppermute(value, axis, pairs)  64.4 us
    all_to_all x1, waiting for transfers between devices, body(): lax.all_to_all(expert_out.reshape(experts, capacity, model_width), 'exper...  40.4 us
    all_to_all x1, waiting for transfers between devices, body(): lax.all_to_all(input_part.reshape(experts, capacity, model_width), 'exper...  39.5 us
    all_gather x1, waiting for transfers between devices, body(): down_full = lax.all_gather(w_down_use, 'dp', axis=1, tiled=True)[0]  37.9 us
    xor x1, other arithmetic, body(): dest_routes = jnp.bitwise_xor(flat_routes, swap_flag[flat_routes])  15.6 us
    dot_general x2, matrix products, contract_cols(): lax.dot_general(left, right, (((1,), (1,)), ((), ())), preferred_element_...  12.4 us
    dot_general x2, matrix products, contract_rows(): lax.dot_general(left, right, (((0,), (0,)), ((), ())), preferred_element_...  10.2 us
  transfers between devices with their start and end apart: 10, of which 6 were waited for; matrix products, arithmetic and copies ran while one was open for 21% of the time, Pallas kernels for 0%

commit v1 on v0

--- a/solution.py
+++ b/solution.py
@@ -70,46 +70,50 @@
     pair_count = tok_count * chosen
     capacity = pair_count * 4 // (3 * experts)
     row_total = experts * capacity
-    my_flag = swap_flag[my_slot]
-    swapped = my_flag == 1
+    swapped = swap_flag[my_slot] == 1
     w_up_in = partner(w_up, "expert", 0)
     w_down_in = partner(w_down, "expert", 0)
-    up_moments = partner(jnp.concatenate([m_up, v_up], axis=0), "expert", 0)
-    down_moments = partner(jnp.concatenate([m_down, v_down], axis=0), "expert", 0)
+    w_up_in, w_down_in, up_local, down_local = lax.optimization_barrier(
+        (
+            w_up_in,
+            w_down_in,
+            jnp.concatenate([m_up, v_up], axis=0),
+            jnp.concatenate([m_down, v_down], axis=0),
+        )
+    )
+    up_moments = partner(up_local, "expert", 0)
+    down_moments = partner(down_local, "expert", 0)
     w_up_use = jnp.where(swapped, w_up_in, w_up)
     w_down_use = jnp.where(swapped, w_down_in, w_down)
-    m_up_use = jnp.where(swapped, up_moments[0:1], m_up)
-    v_up_use = jnp.where(swapped, up_moments[1:2], v_up)
-    m_down_use = jnp.where(swapped, down_moments[0:1], m_down)
-    v_down_use = jnp.where(swapped, down_moments[1:2], v_down)
-    flat_routes = routes.reshape(pair_count)
-    dest_routes = jnp.bitwise_xor(flat_routes, swap_flag[flat_routes])
-    one_hot = (dest_routes[:, None] == jnp.arange(experts, dtype=jnp.int32)[None, :]).astype(
-        jnp.int32
-    )
-    position = jnp.sum(jnp.cumsum(one_hot, axis=0) * one_hot, axis=1) - 1
-    slot_index = dest_routes * capacity + position
-    source = (
-        jnp.full((row_total,), -1, jnp.int32)
-        .at[slot_index]
-        .set(jnp.arange(pair_count, dtype=jnp.int32))
-    )
-    is_live = source >= 0
-    safe_source = jnp.maximum(source, 0)
-    token_ids = safe_source // chosen
-    send_tokens = jnp.where(
-        is_live[:, None], tokens[token_ids], jnp.zeros((), jnp.bfloat16)
-    ).reshape(experts, capacity, model_width)
-    live_gates = jnp.where(is_live, gates.reshape(pair_count)[safe_source], 0.0)
-    send_grads = (
-        (live_gates[:, None] * cotangent[token_ids].astype(jnp.float32))
-        .astype(jnp.bfloat16)
-        .reshape(experts, capacity, model_width)
-    )
     up_full = lax.all_gather(w_up_use, "dp", axis=1, tiled=True)[0]
     down_full = lax.all_gather(w_down_use, "dp", axis=1, tiled=True)[0]
+    expert_ids = jnp.arange(experts, dtype=jnp.int32)
+    route_hot = (routes.reshape(pair_count)[:, None] == expert_ids[None, :]).astype(jnp.int32)
+    paired_hot = route_hot.reshape(pair_count, experts // 2, 2)[:, :, ::-1].reshape(
+        pair_count, experts
+    )
+    dest_hot = jnp.where(swap_flag[None, :] == 1, paired_hot, route_hot)
+    position = jnp.sum(jnp.cumsum(dest_hot, axis=0) * dest_hot, axis=1) - 1
+    slot_index = jnp.sum(dest_hot * (expert_ids * capacity)[None, :], axis=1) + position
+    pick = slot_index[:, None] == jnp.arange(row_total, dtype=jnp.int32)[None, :]
+    pick_bf = pick.astype(jnp.bfloat16)
+    gather_rows = jnp.sum(pick_bf.reshape(tok_count, chosen, row_total), axis=1).T
+    live_gates = jnp.sum(
+        jnp.where(pick, gates.reshape(pair_count)[:, None], 0.0), axis=0
+    )
+    send_tokens = jnp.dot(gather_rows, tokens, preferred_element_type=jnp.float32).astype(
+        jnp.bfloat16
+    )
+    send_cot = jnp.dot(gather_rows, cotangent, preferred_element_type=jnp.float32)
+    send_grads = (live_gates[:, None] * send_cot).astype(jnp.bfloat16)
     got_both = lax.all_to_all(
-        jnp.concatenate([send_tokens, send_grads], axis=1),
+        jnp.concatenate(
+            [
+                send_tokens.reshape(experts, capacity, model_width),
+                send_grads.reshape(experts, capacity, model_width),
+            ],
+            axis=1,
+        ),
         "expert",
         split_axis=0,
         concat_axis=0,
@@ -119,6 +123,9 @@
     grad_rows = got_both[:, capacity:].reshape(row_total, model_width)
     up_act = jnp.dot(expert_rows, up_full, preferred_element_type=jnp.float32)
     hidden = jax.nn.silu(up_act).astype(jnp.bfloat16)
+    down_full, hidden, up_moments, down_moments = lax.optimization_barrier(
+        (down_full, hidden, up_moments, down_moments)
+    )
     expert_out = jnp.dot(hidden, down_full, preferred_element_type=jnp.float32).astype(jnp.bfloat16)
     returned = lax.all_to_all(
         expert_out.reshape(experts, capacity, model_width),
@@ -127,10 +134,10 @@
         concat_axis=0,
         tiled=True,
     )
-    picked = returned.reshape(row_total, model_width)[slot_index].reshape(
-        tok_count, chosen, model_width
-    )
-    mixed = jnp.sum(gates[:, :, None] * picked.astype(jnp.float32), axis=1).astype(jnp.bfloat16)
+    picked = jnp.dot(
+        pick_bf, returned.reshape(row_total, model_width), preferred_element_type=jnp.float32
+    ).reshape(tok_count, chosen, model_width)
+    mixed = jnp.sum(gates[:, :, None] * picked, axis=1).astype(jnp.bfloat16)
     hidden_grad = contract_cols(grad_rows, down_full)
     up_grad = (hidden_grad * silu_slope(up_act)).astype(jnp.bfloat16)
     input_part = contract_cols(up_grad, up_full).astype(jnp.bfloat16)
@@ -141,10 +148,10 @@
         concat_axis=0,
         tiled=True,
     )
-    picked_grad = back_grads.reshape(row_total, model_width)[slot_index].reshape(
-        tok_count, chosen, model_width
-    )
-    input_grad = jnp.sum(picked_grad.astype(jnp.float32), axis=1).astype(jnp.bfloat16)
+    picked_grad = jnp.dot(
+        pick_bf, back_grads.reshape(row_total, model_width), preferred_element_type=jnp.float32
+    ).reshape(tok_count, chosen, model_width)
+    input_grad = jnp.sum(picked_grad, axis=1).astype(jnp.bfloat16)
     up_gradient = lax.psum_scatter(
         contract_rows(expert_rows, up_grad).astype(jnp.bfloat16),
         "dp",
@@ -157,6 +164,10 @@
         scatter_dimension=0,
         tiled=True,
     ).astype(jnp.float32)
+    m_up_use = jnp.where(swapped, up_moments[0:1], m_up)
+    v_up_use = jnp.where(swapped, up_moments[1:2], v_up)
+    m_down_use = jnp.where(swapped, down_moments[0:1], m_down)
+    v_down_use = jnp.where(swapped, down_moments[1:2], v_down)
     up_new = adam_update(w_up_use[0], m_up_use[0], v_up_use[0], up_gradient)
     down_new = adam_update(w_down_use[0], m_down_use[0], v_down_use[0], down_gradient)
     return (

time: 445 us -> 365 us (0.82)
  blocking collectives: 85 us -> 0 us
  waiting for transfers between devices: 182 us -> 227 us
  local copies, waits for them, and re-layouts: 59.6 us -> 26.8 us
  other arithmetic: 40.9 us -> 20.8 us
  starting transfers between devices: 23 us -> 31.1 us
  matrix products: 35.7 us -> 43.6 us
    all_to_all x1 -> x0, blocking collectives: 85 us -> none  [body(): lax.all_to_all(jnp.concatenate([send_tokens, send_grads], axis=1), 'exper...]
    all_to_all x0 -> x1, waiting for transfers between devices: none -> 71.5 us  [body(): lax.all_to_all(jnp.concatenate([send_tokens.reshape(experts, capacity, mo...]
    all_gather x1, waiting for transfers between devices: 37.9 us -> 0.01 us  [body(): down_full = lax.all_gather(w_down_use, 'dp', axis=1, tiled=True)[0]]
    gather x7 -> x0, local copies, waits for them, and re-layouts: 18.8 us -> none  [the longest x2 5.57 us: body(): tokens[token_ids]]
    xor x1 -> x0, other arithmetic: 15.6 us -> none  [body(): dest_routes = jnp.bitwise_xor(flat_routes, swap_flag[flat_routes])]
    all_to_all x0 -> x1, starting transfers between devices: none -> 11.3 us  [body(): lax.all_to_all(jnp.concatenate([send_tokens.reshape(experts, capacity, mo...]
    unnamed x34 -> x42, local copies, waits for them, and re-layouts: 10 us -> 0.27 us
    all_to_all x1, waiting for transfers between devices: 40.4 us -> 48.2 us  [body(): lax.all_to_all(expert_out.reshape(experts, capacity, model_width), 'exper...]
  transfers between devices with their start and end apart: 10 -> 11, of which waited for: 6 -> 7; matrix products, arithmetic and copies ran while one was open for 21% -> 22% of each run, Pallas kernels for 0% -> 0%
where the time goes in v1:
time: 365 us; the launch traced here: 364 us
  waiting for transfers between devices  227 us (62%)
  matrix products  43.6 us (12%)
  starting transfers between devices  31.1 us (9%)
  local copies, waits for them, and re-layouts  26.8 us (7%)
  other arithmetic  20.8 us (6%)
  between operations  14.7 us (4%)
    all_to_all x1, waiting for transfers between devices, body(): lax.all_to_all(jnp.concatenate([send_tokens.reshape(experts, capacity, mo...  71.5 us
    ppermute x4, waiting for transfers between devices, partner(): return lax.ppermute(value, axis, pairs)  67.3 us
    all_to_all x1, waiting for transfers between devices, body(): lax.all_to_all(expert_out.reshape(experts, capacity, model_width), 'exper...  48.2 us
    all_to_all x1, waiting for transfers between devices, body(): lax.all_to_all(input_part.reshape(experts, capacity, model_width), 'exper...  39.7 us
    dot_general x2, matrix products, contract_cols(): lax.dot_general(left, right, (((1,), (1,)), ((), ())), preferred_element_...  12.5 us
    all_to_all x1, starting transfers between devices, body(): lax.all_to_all(jnp.concatenate([send_tokens.reshape(experts, capacity, mo...  11.3 us
    dot_general x2, matrix products, contract_rows(): lax.dot_general(left, right, (((0,), (0,)), ((), ())), preferred_element_...  10.2 us
    all_to_all x1, starting transfers between devices, body(): lax.all_to_all(input_part.reshape(experts, capacity, model_width), 'exper...  8.72 us
  transfers between devices with their start and end apart: 11, of which 7 were waited for; matrix products, arithmetic and copies ran while one was open for 22% of the time, Pallas kernels for 0%

profile of v1, /device:TPU:6, one launch (start us, length us, event | category | flops | bytes accessed | tf_op | source)
XLA Modules:
  0.0 363.8 jit_solution(15417215184260463378)
XLA Ops:
  7.3 2.0 collective-permute-start
  11.3 2.6 pad_maximum_fusion.2
  15.1 11.4 %collective-permute-done = bf16[1,256,1408]{2,1,0:T(8,128)(2,1)S(1)} collective-permute-done((bf16[1,256,1408]{2,1,0:T(8,128)(2,1)}, bf16[1,256,1408]{2,1,0:T(8,128)(2,1)S(1)}, u32[]{:S(2)}, u32[]{:S(2)}) %collective-permute-start) | collective-permute-done | bytes 720928 | tf_op jit(solution)/shard_map/ppermute | solution.py:18
  26.6 14.5 %collective-permute-done.1 = bf16[1,176,2048]{2,1,0:T(8,128)(2,1)S(1)} collective-permute-done((bf16[1,176,2048]{2,1,0:T(8,128)(2,1)}, bf16[1,176,2048]{2,1,0:T(8,128)(2,1)S(1)}, u32[]{:S(2)}, u32[]{:S(2)}) %collective-permute-start.1) | collective-permute-done | bytes 720928 | tf_op jit(solution)/shard_map/ppermute | solution.py:18
  46.0 1.8 multiply_convert_fusion
  47.9 2.4 reshape.177
  50.3 1.8 convolution_convert_fusion.3
  52.1 3.6 reshape.176
  55.7 4.4 %pad_maximum_fusion = bf16[32,24,2048]{2,1,0:T(8,128)(2,1)} fusion(bf16[32,12,2048]{2,1,0:T(8,128)(2,1)S(1)} %reshape.177, bf16[32,12,2048]{2,1,0:T(8,128)(2,1)} %reshape.176), kind=kLoop, calls=%fused_computation.6 | loop fusion | flops 6291456 | bytes 6291456 | tf_op jit(solution)/shard_map/concatenate | solution.py:110
  60.1 11.3 %all-to-all-start = ((bf16[32,24,2048]{2,1,0:T(8,128)(2,1)}), bf16[32,24,2048]{2,1,0:T(8,128)(2,1)S(1)}, u32[]{:S(2)}, u32[]{:S(2)}) async-start(bf16[32,24,2048]{2,1,0:T(8,128)(2,1)} %pad_maximum_fusion), calls=%async_computation | async-start | bytes 6291456 | tf_op jit(solution)/shard_map/all_to_all | solution.py:109
  71.4 1.9 collective-permute-start.2
  73.5 71.5 %all-to-all-done = bf16[32,24,2048]{2,1,0:T(8,128)(2,1)S(1)} async-done(((bf16[32,24,2048]{2,1,0:T(8,128)(2,1)}), bf16[32,24,2048]{2,1,0:T(8,128)(2,1)S(1)}, u32[]{:S(2)}, u32[]{:S(2)}) %all-to-all-start) | async-done | bytes 3145760 | tf_op jit(solution)/shard_map/all_to_all | solution.py:109
  145.1 3.0 fusion.34
  148.1 3.8 %reshape.181 = bf16[384,2048]{1,0:T(8,128)(2,1)} reshape(bf16[32,12,2048]{2,1,0:T(8,128)(2,1)} %get-tuple-element.24) | data formatting | bytes 3145728 | tf_op jit(solution)/shard_map/reshape | solution.py:123
  153.2 7.3 %multiply_convert_fusion.1 = (bf16[384,1408]{1,0:T(8,128)(2,1)S(1)}, f32[384,1408]{1,0:T(8,128)}) fusion(bf16[384,2048]{1,0:T(8,128)(2,1)} %reshape.178, bf16[1,2048,1408]{2,1,0:T(8,128)(2,1)} %all-gather.5.cloned.1.call-done), kind=kOutput, calls=%fused_computation.14 | convolution fusion | flops 2217295872 | bytes 10584064 | tf_op jit(solution)/shard_map/dot_general | solution.py:124
  160.5 11.6 %collective-permute-done.2 = bf16[2,256,1408]{2,1,0:T(8,128)(2,1)} collective-permute-done((bf16[2,256,1408]{2,1,0:T(8,128)(2,1)}, bf16[2,256,1408]{2,1,0:T(8,128)(2,1)}, u32[]{:S(2)}, u32[]{:S(2)}) %collective-permute-start.2) | collective-permute-done | bytes 1441824 | tf_op jit(solution)/shard_map/ppermute | solution.py:18
  172.1 29.8 %collective-permute-done.3 = bf16[2,176,2048]{2,1,0:T(8,128)(2,1)} collective-permute-done((bf16[2,176,2048]{2,1,0:T(8,128)(2,1)}, bf16[2,176,2048]{2,1,0:T(8,128)(2,1)}, u32[]{:S(2)}, u32[]{:S(2)}) %collective-permute-start.3) | collective-permute-done | bytes 1441824 | tf_op jit(solution)/shard_map/ppermute | solution.py:18
  201.9 5.0 %convolution_convert_fusion = bf16[1408,2048]{1,0:T(8,128)(2,1)} fusion(bf16[384,1408]{1,0:T(8,128)(2,1)S(1)} %get-tuple-element.20, bf16[384,2048]{1,0:T(8,128)(2,1)S(1)} %copy-done.9), kind=kOutput, calls=%fused_computation | convolution fusion | flops 2217476096 | bytes 8421376 | tf_op jit(solution)/shard_map/dot_general | solution.py:44
  207.2 7.2 %fusion.4 = bf16[384,1408]{1,0:T(8,128)(2,1)S(1)} fusion(bf16[384,2048]{1,0:T(8,128)(2,1)S(1)} %copy-done.9, bf16[1408,2048]{1,0:T(8,128)(2,1)} %bitcast.111, f32[384,1408]{1,0:T(8,128)} %get-tuple-element.33), kind=kOutput, calls=%fused_computation.9 | convolution fusion | flops 2219458560 | bytes 10584064 | tf_op jit(solution)/shard_map/dot_general | solution.py:50
  214.5 5.2 %convolution_convert_fusion.1 = bf16[2048,1408]{1,0:T(8,128)(2,1)} fusion(bf16[384,2048]{1,0:T(8,128)(2,1)S(1)} %copy-done.10, bf16[384,1408]{1,0:T(8,128)(2,1)S(1)} %fusion.4), kind=kOutput, calls=%fused_computation.1 | convolution fusion | flops 2217476096 | bytes 8421376 | tf_op jit(solution)/shard_map/dot_general | solution.py:44
  219.7 5.3 %fusion.5 = bf16[384,2048]{1,0:T(8,128)(2,1)S(1)} fusion(bf16[384,1408]{1,0:T(8,128)(2,1)S(1)} %fusion.4, bf16[1,2048,1408]{2,1,0:T(8,128)(2,1)} %all-gather.5.cloned.1.call-done), kind=kOutput, calls=%fused_computation.10 | convolution fusion | flops 2215378944 | bytes 8421376 | tf_op jit(solution)/shard_map/dot_general | solution.py:50
  225.0 1.5 reshape.182
  226.5 8.7 %all-to-all-start.2 = ((bf16[32,12,2048]{2,1,0:T(8,128)(2,1)}), bf16[32,12,2048]{2,1,0:T(8,128)(2,1)S(1)}, u32[]{:S(2)}, u32[]{:S(2)}) async-start(bf16[32,12,2048]{2,1,0:T(8,128)(2,1)} %reshape.182), calls=%async_computation.2 | async-start | bytes 4194304 | tf_op jit(solution)/shard_map/all_to_all | solution.py:144
  235.2 6.9 %convolution_convert_fusion.2 = bf16[384,2048]{1,0:T(8,128)(2,1)} fusion(bf16[384,1408]{1,0:T(8,128)(2,1)} %copy-done.19, bf16[1408,2048]{1,0:T(8,128)(2,1)} %bitcast.112), kind=kOutput, calls=%fused_computation.11 | convolution fusion | flops 2215378944 | bytes 8421376 | tf_op jit(solution)/shard_map/dot_general | solution.py:129
  242.1 3.7 %reshape.179 = bf16[32,12,2048]{2,1,0:T(8,128)(2,1)} reshape(bf16[384,2048]{1,0:T(8,128)(2,1)} %convolution_convert_fusion.2) | data formatting | bytes 3145728 | tf_op jit(solution)/shard_map/reshape | solution.py:131
  245.7 39.7 %all-to-all-done.2 = bf16[32,12,2048]{2,1,0:T(8,128)(2,1)S(1)} async-done(((bf16[32,12,2048]{2,1,0:T(8,128)(2,1)}), bf16[32,12,2048]{2,1,0:T(8,128)(2,1)S(1)}, u32[]{:S(2)}, u32[]{:S(2)}) %all-to-all-start.2) | async-done | bytes 1572896 | tf_op jit(solution)/shard_map/all_to_all | solution.py:144
  285.5 6.5 %all-to-all-start.1 = ((bf16[32,12,2048]{2,1,0:T(8,128)(2,1)}), bf16[32,12,2048]{2,1,0:T(8,128)(2,1)}, u32[]{:S(2)}, u32[]{:S(2)}) async-start(bf16[32,12,2048]{2,1,0:T(8,128)(2,1)} %reshape.179), calls=%async_computation.1 | async-start | bytes 4194304 | tf_op jit(solution)/shard_map/all_to_all | solution.py:130
  293.3 48.2 %all-to-all-done.1 = bf16[32,12,2048]{2,1,0:T(8,128)(2,1)} async-done(((bf16[32,12,2048]{2,1,0:T(8,128)(2,1)}), bf16[32,12,2048]{2,1,0:T(8,128)(2,1)}, u32[]{:S(2)}, u32[]{:S(2)}) %all-to-all-start.1) | async-done | bytes 1572896 | tf_op jit(solution)/shard_map/all_to_all | solution.py:130
  341.6 3.6 reshape.186
  346.7 1.5 fusion.8
  348.3 4.5 %fusion.20 = (bf16[1,176,2048]{2,1,0:T(8,128)(2,1)}, bf16[1,176,2048]{2,1,0:T(8,128)(2,1)}, bf16[1,176,2048]{2,1,0:T(8,128)(2,1)}) fusion(bf16[176,2048]{1,0:T(8,128)(2,1)} %reduce-scatter.5.cloned.1.call-done, bf16[1,176,2048]{2,1,0:T(8,128)(2,1)S(1)} %copy-done.5, bf16[2,176,2048]{2,1,0:T(8,128)(2,1)} %collective-permute-done.3, pred[]{:T(512)} %bitcast.3, ...), kind=kLoop, calls=%fused_computation.37 | loop fusion | flops 7569408 | bytes 6488065 | tf_op jit(solution)/shard_map/broadcast_in_dim | solution.py:181
  352.7 4.5 %fusion.19 = (bf16[1,256,1408]{2,1,0:T(8,128)(2,1)}, bf16[1,256,1408]{2,1,0:T(8,128)(2,1)}, bf16[1,256,1408]{2,1,0:T(8,128)(2,1)}) fusion(bf16[256,1408]{1,0:T(8,128)(2,1)} %reduce-scatter.3.cloned.1.call-done, bf16[1,256,1408]{2,1,0:T(8,128)(2,1)} %param.19, bf16[2,256,1408]{2,1,0:T(8,128)(2,1)} %collective-permute-done.2, pred[]{:T(512)} %bitcast.3, ...), kind=kLoop, calls=%fused_computation.36 | loop fusion | flops 7569408 | bytes 6488065 | tf_op jit(solution)/shard_map/broadcast_in_dim | solution.py:179
  (84 shorter events, 12.3 us)
Async XLA Ops:
  7.2 38.9 %copy-start = (bf16[48,2048]{1,0:T(8,128)(2,1)S(1)}, bf16[48,2048]{1,0:T(8,128)(2,1)}, u32[]{:S(2)}) copy-start(bf16[48,2048]{1,0:T(8,128)(2,1)} %param.14) | copy-start | bytes 589828
  7.2 6.7 %copy-start.7 = (bf16[1,256,1408]{2,1,0:T(8,128)(2,1)S(1)}, bf16[1,256,1408]{2,1,0:T(8,128)(2,1)}, u32[]{:S(2)}) copy-start(bf16[1,256,1408]{2,1,0:T(8,128)(2,1)} %param.19) | copy-start | bytes 2162692
  7.2 6.7 %copy-start.8 = (bf16[1,256,1408]{2,1,0:T(8,128)(2,1)S(1)}, bf16[1,256,1408]{2,1,0:T(8,128)(2,1)}, u32[]{:S(2)}) copy-start(bf16[1,256,1408]{2,1,0:T(8,128)(2,1)} %param.18) | copy-start | bytes 2162692
  7.2 146.0 %all-gather.5.cloned.1.call-start = ((), (), s32[]{:S(2)}) async-start(), calls=%async_computation.6 | async-start | bytes 6488064 | tf_op jit(solution)/shard_map/all_gather | solution.py:88
  7.3 19.3 %collective-permute-start = (bf16[1,256,1408]{2,1,0:T(8,128)(2,1)}, bf16[1,256,1408]{2,1,0:T(8,128)(2,1)S(1)}, u32[]{:S(2)}, u32[]{:S(2)}) collective-permute-start(bf16[1,256,1408]{2,1,0:T(8,128)(2,1)} %param.16), channel_id=1, source_target_pairs={{0,1},{1,0},{2,3},{3,2},{4,5},{5,4},{6,7},{7,6},{8,9},{9,8},{10,11... | collective-permute-start | bytes 2162696 | tf_op jit(solution)/shard_map/ppermute | solution.py:18
  9.3 31.8 %collective-permute-start.1 = (bf16[1,176,2048]{2,1,0:T(8,128)(2,1)}, bf16[1,176,2048]{2,1,0:T(8,128)(2,1)S(1)}, u32[]{:S(2)}, u32[]{:S(2)}) collective-permute-start(bf16[1,176,2048]{2,1,0:T(8,128)(2,1)} %param.17), channel_id=1, source_target_pairs={{0,1},{1,0},{2,3},{3,2},{4,5},{5,4},{6,7},{7,6},{8,9},{9,8},{10,11... | collective-permute-start | bytes 2162696 | tf_op jit(solution)/shard_map/ppermute | solution.py:18
  13.9 27.2 %copy-start.13 = (bf16[1,256,1408]{2,1,0:T(8,128)(2,1)S(1)}, bf16[1,256,1408]{2,1,0:T(8,128)(2,1)}, u32[]{:S(2)}) copy-start(bf16[1,256,1408]{2,1,0:T(8,128)(2,1)} %param.16) | copy-start | bytes 2162692
  15.1 27.0 %copy-start.18 = (s32[32]{0:T(128)S(1)}, s32[32]{0:T(128)}, u32[]{:S(2)}) copy-start(s32[32]{0:T(128)} %param.15) | copy-start | bytes 388
  15.1 27.1 %copy-start.16 = (s32[48,6]{0,1:T(8,128)S(1)}, s32[48,6]{0,1:T(8,128)}, u32[]{:S(2)}) copy-start(s32[48,6]{0,1:T(8,128)} %param.12) | copy-start | bytes 3460
  15.1 27.3 %copy-start.17 = (f32[48,6]{0,1:T(8,128)S(1)}, f32[48,6]{0,1:T(8,128)}, u32[]{:S(2)}) copy-start(f32[48,6]{0,1:T(8,128)} %param.13) | copy-start | bytes 3460
  15.1 27.5 %copy-start.14 = (bf16[1,176,2048]{2,1,0:T(8,128)(2,1)S(1)}, bf16[1,176,2048]{2,1,0:T(8,128)(2,1)}, u32[]{:S(2)}) copy-start(bf16[1,176,2048]{2,1,0:T(8,128)(2,1)} %param.17) | copy-start | bytes 2162692
  42.0 159.9 %all-gather.3.cloned.1.call-start = ((), (), s32[]{:S(2)}) async-start(), calls=%async_computation.5 | async-start | bytes 6488064 | tf_op jit(solution)/shard_map/all_gather | solution.py:89
  47.9 2.4 copy-start.15
  60.1 85.0 %all-to-all-start = ((bf16[32,24,2048]{2,1,0:T(8,128)(2,1)}), bf16[32,24,2048]{2,1,0:T(8,128)(2,1)S(1)}, u32[]{:S(2)}, u32[]{:S(2)}) async-start(bf16[32,24,2048]{2,1,0:T(8,128)(2,1)} %pad_maximum_fusion), calls=%async_computation | async-start | bytes 6291456 | tf_op jit(solution)/shard_map/all_to_all | solution.py:109
  71.4 276.9 %reduce-scatter.5.cloned.1.call-start = ((), (), s32[]{:S(2)}) async-start(), calls=%async_computation.8 | async-start | bytes 6488064 | tf_op jit(solution)/shard_map/reduce_scatter | solution.py:161
  71.4 100.6 %collective-permute-start.2 = (bf16[2,256,1408]{2,1,0:T(8,128)(2,1)}, bf16[2,256,1408]{2,1,0:T(8,128)(2,1)}, u32[]{:S(2)}, u32[]{:S(2)}) collective-permute-start(bf16[2,256,1408]{2,1,0:T(8,128)(2,1)} %pad_maximum_fusion.1), channel_id=1, source_target_pairs={{0,1},{1,0},{2,3},{3,2},{4,5},{5,4},{6,7},{7,6},{8,9},{9,8},{10,11... | collective-permute-start | bytes 4325384 | tf_op jit(solution)/shard_map/ppermute | solution.py:18
  73.3 128.6 %collective-permute-start.3 = (bf16[2,176,2048]{2,1,0:T(8,128)(2,1)}, bf16[2,176,2048]{2,1,0:T(8,128)(2,1)}, u32[]{:S(2)}, u32[]{:S(2)}) collective-permute-start(bf16[2,176,2048]{2,1,0:T(8,128)(2,1)} %pad_maximum_fusion.2), channel_id=1, source_target_pairs={{0,1},{1,0},{2,3},{3,2},{4,5},{5,4},{6,7},{7,6},{8,9},{9,8},{10,11... | collective-permute-start | bytes 4325384 | tf_op jit(solution)/shard_map/ppermute | solution.py:18
  148.1 3.8 %copy-start.2 = (bf16[32,12,2048]{2,1,0:T(8,128)(2,1)S(1)}, bf16[32,12,2048]{2,1,0:T(8,128)(2,1)}, u32[]{:S(2)}) copy-start(bf16[32,12,2048]{2,1,0:T(8,128)(2,1)} %get-tuple-element.25) | copy-start | bytes 4718596
  153.2 48.7 %copy-start.9 = (bf16[384,2048]{1,0:T(8,128)(2,1)S(1)}, bf16[384,2048]{1,0:T(8,128)(2,1)}, u32[]{:S(2)}) copy-start(bf16[384,2048]{1,0:T(8,128)(2,1)} %reshape.181) | copy-start | bytes 4718596
  160.5 46.5 %copy-start.19 = (bf16[384,1408]{1,0:T(8,128)(2,1)}, bf16[384,1408]{1,0:T(8,128)(2,1)S(1)}, u32[]{:S(2)}) copy-start(bf16[384,1408]{1,0:T(8,128)(2,1)S(1)} %get-tuple-element.20) | copy-start | bytes 3244036
  207.0 145.8 %reduce-scatter.3.cloned.1.call-start = ((), (), s32[]{:S(2)}) async-start(), calls=%async_computation.7 | async-start | bytes 6488064 | tf_op jit(solution)/shard_map/reduce_scatter | solution.py:155
  207.2 7.3 %copy-start.10 = (bf16[384,2048]{1,0:T(8,128)(2,1)S(1)}, bf16[384,2048]{1,0:T(8,128)(2,1)}, u32[]{:S(2)}) copy-start(bf16[384,2048]{1,0:T(8,128)(2,1)} %reshape.178) | copy-start | bytes 4718596
  226.5 59.0 %all-to-all-start.2 = ((bf16[32,12,2048]{2,1,0:T(8,128)(2,1)}), bf16[32,12,2048]{2,1,0:T(8,128)(2,1)S(1)}, u32[]{:S(2)}, u32[]{:S(2)}) async-start(bf16[32,12,2048]{2,1,0:T(8,128)(2,1)} %reshape.182), calls=%async_computation.2 | async-start | bytes 4194304 | tf_op jit(solution)/shard_map/all_to_all | solution.py:144
  285.5 56.1 %all-to-all-start.1 = ((bf16[32,12,2048]{2,1,0:T(8,128)(2,1)}), bf16[32,12,2048]{2,1,0:T(8,128)(2,1)}, u32[]{:S(2)}, u32[]{:S(2)}) async-start(bf16[32,12,2048]{2,1,0:T(8,128)(2,1)} %reshape.179), calls=%async_computation.1 | async-start | bytes 4194304 | tf_op jit(solution)/shard_map/all_to_all | solution.py:130
  293.3 51.9 %copy-start.11 = (bf16[384,2048,1]{1,0,2:T(8,128)(2,1)S(1)}, bf16[384,2048,1]{1,0,2:T(8,128)(2,1)}, u32[]{:S(2)}) copy-start(bf16[384,2048,1]{1,0,2:T(8,128)(2,1)} %reshape.187) | copy-start | bytes 4718596
  345.2 1.5 copy-start.12
  346.7 1.5 copy-start.4
  346.7 1.5 copy-start.5
  346.7 1.6 copy-start.6
  348.2 4.5 %copy-start.3 = (bf16[1,256,1408]{2,1,0:T(8,128)(2,1)S(1)}, bf16[1,256,1408]{2,1,0:T(8,128)(2,1)}, u32[]{:S(2)}) copy-start(bf16[1,256,1408]{2,1,0:T(8,128)(2,1)} %broadcast_select_fusion) | copy-start | bytes 2162692
  352.7 4.6 %copy-start.1 = (bf16[48,2048]{1,0:T(8,128)(2,1)S(1)}, bf16[48,2048]{1,0:T(8,128)(2,1)}, u32[]{:S(2)}) copy-start(bf16[48,2048]{1,0:T(8,128)(2,1)} %param.14) | copy-start | bytes 589828
Sparse Core Ops, SparseCore 0:
  42.1 42.1 all-gather.4
  86.7 41.3 all-gather.2
  207.1 40.9 reduce-scatter.4
  250.5 43.6 reduce-scatter.2

commit v2 on v1

--- a/solution.py
+++ b/solution.py
@@ -71,8 +71,48 @@
     capacity = pair_count * 4 // (3 * experts)
     row_total = experts * capacity
     swapped = swap_flag[my_slot] == 1
+    expert_ids = jnp.arange(experts, dtype=jnp.int32)
+    route_hot = (routes.reshape(pair_count)[:, None] == expert_ids[None, :]).astype(jnp.int32)
+    paired_hot = route_hot.reshape(pair_count, experts // 2, 2)[:, :, ::-1].reshape(
+        pair_count, experts
+    )
+    dest_hot = jnp.where(swap_flag[None, :] == 1, paired_hot, route_hot)
+    position = jnp.sum(jnp.cumsum(dest_hot, axis=0) * dest_hot, axis=1) - 1
+    dest = jnp.sum(dest_hot * expert_ids[None, :], axis=1)
+    slot_index = dest * capacity + position
+    pick = slot_index[:, None] == jnp.arange(row_total, dtype=jnp.int32)[None, :]
+    pick_bf = pick.astype(jnp.bfloat16)
+    send_row = (dest * (2 * capacity) + position).reshape(tok_count, chosen)
+    row_ids = jnp.arange(2 * row_total, dtype=jnp.int32)
+    token_pick = jnp.sum(
+        (send_row[:, :, None] == row_ids[None, None, :]).astype(jnp.bfloat16), axis=1
+    )
+    grad_pick = jnp.sum(
+        (send_row[:, :, None] + capacity == row_ids[None, None, :]).astype(jnp.bfloat16), axis=1
+    )
+    row_scale = jnp.sum(
+        jnp.where(
+            send_row[:, :, None] + capacity == row_ids[None, None, :], gates[:, :, None], 0.0
+        ),
+        axis=(0, 1),
+    ) + jnp.sum(token_pick.astype(jnp.float32), axis=0)
+    picked_rows = lax.dot_general(
+        jnp.concatenate([token_pick, grad_pick], axis=0),
+        jnp.concatenate([tokens, cotangent], axis=0),
+        (((0,), (0,)), ((), ())),
+        preferred_element_type=jnp.float32,
+    )
+    send_both = (row_scale[:, None] * picked_rows).astype(jnp.bfloat16)
+    w_up, w_down, send_both = lax.optimization_barrier((w_up, w_down, send_both))
     w_up_in = partner(w_up, "expert", 0)
     w_down_in = partner(w_down, "expert", 0)
+    got_both = lax.all_to_all(
+        send_both.reshape(experts, 2 * capacity, model_width),
+        "expert",
+        split_axis=0,
+        concat_axis=0,
+        tiled=True,
+    )
     w_up_in, w_down_in, up_local, down_local = lax.optimization_barrier(
         (
             w_up_in,
@@ -87,69 +127,39 @@
     w_down_use = jnp.where(swapped, w_down_in, w_down)
     up_full = lax.all_gather(w_up_use, "dp", axis=1, tiled=True)[0]
     down_full = lax.all_gather(w_down_use, "dp", axis=1, tiled=True)[0]
-    expert_ids = jnp.arange(experts, dtype=jnp.int32)
-    route_hot = (routes.reshape(pair_count)[:, None] == expert_ids[None, :]).astype(jnp.int32)
-    paired_hot = route_hot.reshape(pair_count, experts // 2, 2)[:, :, ::-1].reshape(
-        pair_count, experts
-    )
-    dest_hot = jnp.where(swap_flag[None, :] == 1, paired_hot, route_hot)
-    position = jnp.sum(jnp.cumsum(dest_hot, axis=0) * dest_hot, axis=1) - 1
-    slot_index = jnp.sum(dest_hot * (expert_ids * capacity)[None, :], axis=1) + position
-    pick = slot_index[:, None] == jnp.arange(row_total, dtype=jnp.int32)[None, :]
-    pick_bf = pick.astype(jnp.bfloat16)
-    gather_rows = jnp.sum(pick_bf.reshape(tok_count, chosen, row_total), axis=1).T
-    live_gates = jnp.sum(
-        jnp.where(pick, gates.reshape(pair_count)[:, None], 0.0), axis=0
-    )
-    send_tokens = jnp.dot(gather_rows, tokens, preferred_element_type=jnp.float32).astype(
-        jnp.bfloat16
-    )
-    send_cot = jnp.dot(gather_rows, cotangent, preferred_element_type=jnp.float32)
-    send_grads = (live_gates[:, None] * send_cot).astype(jnp.bfloat16)
-    got_both = lax.all_to_all(
-        jnp.concatenate(
-            [
-                send_tokens.reshape(experts, capacity, model_width),
-                send_grads.reshape(experts, capacity, model_width),
-            ],
-            axis=1,
-        ),
-        "expert",
-        split_axis=0,
-        concat_axis=0,
-        tiled=True,
-    )
     expert_rows = got_both[:, :capacity].reshape(row_total, model_width)
     grad_rows = got_both[:, capacity:].reshape(row_total, model_width)
     up_act = jnp.dot(expert_rows, up_full, preferred_element_type=jnp.float32)
     hidden = jax.nn.silu(up_act).astype(jnp.bfloat16)
-    down_full, hidden, up_moments, down_moments = lax.optimization_barrier(
-        (down_full, hidden, up_moments, down_moments)
-    )
+    down_full, hidden, up_moments = lax.optimization_barrier((down_full, hidden, up_moments))
     expert_out = jnp.dot(hidden, down_full, preferred_element_type=jnp.float32).astype(jnp.bfloat16)
-    returned = lax.all_to_all(
-        expert_out.reshape(experts, capacity, model_width),
+    hidden_grad = contract_cols(grad_rows, down_full)
+    up_grad = (hidden_grad * silu_slope(up_act)).astype(jnp.bfloat16)
+    input_part = contract_cols(up_grad, up_full).astype(jnp.bfloat16)
+    both_back = lax.all_to_all(
+        jnp.concatenate(
+            [
+                expert_out.reshape(experts, capacity, model_width),
+                input_part.reshape(experts, capacity, model_width),
+            ],
+            axis=1,
+        ),
         "expert",
         split_axis=0,
         concat_axis=0,
         tiled=True,
     )
+    both_back, down_moments = lax.optimization_barrier((both_back, down_moments))
     picked = jnp.dot(
-        pick_bf, returned.reshape(row_total, model_width), preferred_element_type=jnp.float32
+        pick_bf,
+        both_back[:, :capacity].reshape(row_total, model_width),
+        preferred_element_type=jnp.float32,
     ).reshape(tok_count, chosen, model_width)
     mixed = jnp.sum(gates[:, :, None] * picked, axis=1).astype(jnp.bfloat16)
-    hidden_grad = contract_cols(grad_rows, down_full)
-    up_grad = (hidden_grad * silu_slope(up_act)).astype(jnp.bfloat16)
-    input_part = contract_cols(up_grad, up_full).astype(jnp.bfloat16)
-    back_grads = lax.all_to_all(
-        input_part.reshape(experts, capacity, model_width),
-        "expert",
-        split_axis=0,
-        concat_axis=0,
-        tiled=True,
-    )
     picked_grad = jnp.dot(
-        pick_bf, back_grads.reshape(row_total, model_width), preferred_element_type=jnp.float32
+        pick_bf,
+        both_back[:, capacity:].reshape(row_total, model_width),
+        preferred_element_type=jnp.float32,
     ).reshape(tok_count, chosen, model_width)
     input_grad = jnp.sum(picked_grad, axis=1).astype(jnp.bfloat16)
     up_gradient = lax.psum_scatter(

time: 365 us -> 346 us (0.948)
  waiting for transfers between devices: 227 us -> 209 us
  starting transfers between devices: 31.1 us -> 26.4 us
  matrix products: 43.6 us -> 47.7 us
    all_to_all x3 -> x2, waiting for transfers between devices: 159 us -> 71.8 us  [the longest x1 71.8 us: body(): lax.all_to_all(send_both.reshape(experts, 2 * capacity, model_width), 'ex...]
    ppermute x4, waiting for transfers between devices: 67.3 us -> 137 us  [partner(): return lax.ppermute(value, axis, pairs)]
    all_to_all x3 -> x2, starting transfers between devices: 26.5 us -> 20 us  [the longest x1 11.3 us: body(): lax.all_to_all(send_both.reshape(experts, 2 * capacity, model_width), 'ex...]
    reshape x5 -> x3, local copies, waits for them, and re-layouts: 11 us -> 5.14 us  [the longest x1 3.75 us: body(): both_back[:, capacity:].reshape(row_total, model_width)]
    dot_general x4 -> x3, matrix products: 6.71 us -> 8.39 us  [the longest x1 3.79 us: body(): lax.dot_general(jnp.concatenate([token_pick, grad_pick], axis=0), jnp.con...]
  transfers between devices with their start and end apart: 11 -> 10, of which waited for: 7 -> 5; matrix products, arithmetic and copies ran while one was open for 22% -> 22% of each run, Pallas kernels for 0% -> 0%
where the time goes in v2:
time: 346 us; the launch traced here: 345 us
  waiting for transfers between devices  209 us (60%)
  matrix products  47.7 us (14%)
  starting transfers between devices  26.4 us (8%)
  local copies, waits for them, and re-layouts  24.6 us (7%)
  other arithmetic  23.1 us (7%)
  between operations  14.7 us (4%)
    ppermute x4, waiting for transfers between devices, partner(): return lax.ppermute(value, axis, pairs)  137 us
    all_to_all x1, waiting for transfers between devices, body(): lax.all_to_all(send_both.reshape(experts, 2 * capacity, model_width), 'ex...  71.8 us
    dot_general x2, matrix products, contract_cols(): lax.dot_general(left, right, (((1,), (1,)), ((), ())), preferred_element_...  14.9 us
    all_to_all x1, starting transfers between devices, body(): lax.all_to_all(send_both.reshape(experts, 2 * capacity, model_width), 'ex...  11.3 us
    dot_general x2, matrix products, contract_rows(): lax.dot_general(left, right, (((0,), (0,)), ((), ())), preferred_element_...  10.3 us
    all_to_all x1, starting transfers between devices, body(): lax.all_to_all(jnp.concatenate([expert_out.reshape(experts, capacity, mod...  8.7 us
    dot_general x1, matrix products, body(): up_act = jnp.dot(expert_rows, up_full, preferred_element_type=jnp.float32)  7.25 us
  transfers between devices with their start and end apart: 10, of which 5 were waited for; matrix products, arithmetic and copies ran while one was open for 22% of the time, Pallas kernels for 0%

profile of v2, /device:TPU:6, one launch (start us, length us, event | category | flops | bytes accessed | tf_op | source)
XLA Modules:
  0.0 345.3 jit_solution(13211149728115280449)
XLA Ops:
  12.3 3.8 %multiply_convert_fusion = bf16[768,2048]{1,0:T(8,128)(2,1)} fusion(f32[768]{0:T(1024)S(1)} %add.107, bf16[48,2048]{1,0:T(8,128)(2,1)} %param.14, bf16[48,2048]{1,0:T(8,128)(2,1)} %param.11, bf16[48,768]{1,0:T(8,128)(2,1)S(1)} %get-tuple-element.47, bf16[48,768]{1,0:T(8,128)(2,1)S(1)} %get-tuple-element.46), kind=kOutput, calls=%fused_computation.2 | convolution fusion | flops 306216960 | bytes 3689472 | tf_op jit(solution)/shard_map/dot_general | solution.py:99
  16.1 1.9 collective-permute-start
  21.9 13.5 %collective-permute-done = bf16[1,256,1408]{2,1,0:T(8,128)(2,1)} collective-permute-done((bf16[1,256,1408]{2,1,0:T(8,128)(2,1)}, bf16[1,256,1408]{2,1,0:T(8,128)(2,1)}, u32[]{:S(2)}, u32[]{:S(2)}) %collective-permute-start) | collective-permute-done | bytes 720928 | tf_op jit(solution)/shard_map/ppermute | solution.py:18
  35.4 14.5 %collective-permute-done.1 = bf16[1,176,2048]{2,1,0:T(8,128)(2,1)} collective-permute-done((bf16[1,176,2048]{2,1,0:T(8,128)(2,1)}, bf16[1,176,2048]{2,1,0:T(8,128)(2,1)}, u32[]{:S(2)}, u32[]{:S(2)}) %collective-permute-start.1) | collective-permute-done | bytes 720928 | tf_op jit(solution)/shard_map/ppermute | solution.py:18
  49.9 2.1 broadcast_select_fusion
  52.0 2.1 broadcast_select_fusion.1
  54.1 11.3 %all-to-all-start = ((bf16[32,24,2048]{2,1,0:T(8,128)(2,1)}), bf16[32,24,2048]{2,1,0:T(8,128)(2,1)S(1)}, u32[]{:S(2)}, u32[]{:S(2)}) async-start(bf16[32,24,2048]{2,1,0:T(8,128)(2,1)} %bitcast.107), calls=%async_computation | async-start | bytes 6291456 | tf_op jit(solution)/shard_map/all_to_all | solution.py:109
  65.5 1.9 collective-permute-start.2
  67.4 71.8 %all-to-all-done = bf16[32,24,2048]{2,1,0:T(8,128)(2,1)S(1)} async-done(((bf16[32,24,2048]{2,1,0:T(8,128)(2,1)}), bf16[32,24,2048]{2,1,0:T(8,128)(2,1)S(1)}, u32[]{:S(2)}, u32[]{:S(2)}) %all-to-all-start) | async-done | bytes 3145760 | tf_op jit(solution)/shard_map/all_to_all | solution.py:109
  139.1 2.8 fusion.44
  142.0 3.8 %reshape.190 = bf16[384,2048]{1,0:T(8,128)(2,1)} reshape(bf16[32,12,2048]{2,1,0:T(8,128)(2,1)} %get-tuple-element.34) | data formatting | bytes 3145728 | tf_op jit(solution)/shard_map/reshape | solution.py:130
  145.8 1.3 reshape.192
  147.1 7.2 %multiply_convert_fusion.1 = (bf16[384,1408]{1,0:T(8,128)(2,1)S(1)}, f32[384,1408]{1,0:T(8,128)}) fusion(bf16[384,2048]{1,0:T(8,128)(2,1)} %reshape.190, bf16[1,2048,1408]{2,1,0:T(8,128)(2,1)} %all-gather.5.cloned.1.call-done), kind=kOutput, calls=%fused_computation.13 | convolution fusion | flops 2217295872 | bytes 10584064 | tf_op jit(solution)/shard_map/dot_general | solution.py:132
  154.4 10.7 %collective-permute-done.2 = bf16[2,256,1408]{2,1,0:T(8,128)(2,1)} collective-permute-done((bf16[2,256,1408]{2,1,0:T(8,128)(2,1)}, bf16[2,256,1408]{2,1,0:T(8,128)(2,1)}, u32[]{:S(2)}, u32[]{:S(2)}) %collective-permute-start.2) | collective-permute-done | bytes 1441824 | tf_op jit(solution)/shard_map/ppermute | solution.py:18
  165.1 5.0 %convolution_convert_fusion = bf16[1408,2048]{1,0:T(8,128)(2,1)} fusion(bf16[384,1408]{1,0:T(8,128)(2,1)S(1)} %get-tuple-element.26, bf16[384,2048]{1,0:T(8,128)(2,1)S(1)} %copy-done.11), kind=kOutput, calls=%fused_computation | convolution fusion | flops 2217476096 | bytes 8421376 | tf_op jit(solution)/shard_map/dot_general | solution.py:44
  170.3 7.2 %fusion.4 = bf16[384,1408]{1,0:T(8,128)(2,1)S(1)} fusion(bf16[384,2048]{1,0:T(8,128)(2,1)S(1)} %copy-done.11, bf16[1408,2048]{1,0:T(8,128)(2,1)} %bitcast.109, f32[384,1408]{1,0:T(8,128)} %get-tuple-element.45), kind=kOutput, calls=%fused_computation.9 | convolution fusion | flops 2219458560 | bytes 10584064 | tf_op jit(solution)/shard_map/dot_general | solution.py:50
  177.6 5.3 %convolution_convert_fusion.1 = bf16[2048,1408]{1,0:T(8,128)(2,1)} fusion(bf16[384,2048]{1,0:T(8,128)(2,1)S(1)} %copy-done.10, bf16[384,1408]{1,0:T(8,128)(2,1)S(1)} %fusion.4), kind=kOutput, calls=%fused_computation.1 | convolution fusion | flops 2217476096 | bytes 8421376 | tf_op jit(solution)/shard_map/dot_general | solution.py:44
  182.9 7.7 %fusion.5 = bf16[384,2048]{1,0:T(8,128)(2,1)} fusion(bf16[384,1408]{1,0:T(8,128)(2,1)S(1)} %fusion.4, bf16[1,2048,1408]{2,1,0:T(8,128)(2,1)} %all-gather.5.cloned.1.call-done), kind=kOutput, calls=%fused_computation.10 | convolution fusion | flops 2215378944 | bytes 8421376 | tf_op jit(solution)/shard_map/dot_general | solution.py:50
  190.5 2.4 reshape.193
  192.9 6.9 %convolution_convert_fusion.2 = bf16[384,2048]{1,0:T(8,128)(2,1)} fusion(bf16[384,1408]{1,0:T(8,128)(2,1)} %copy-done.15, bf16[1408,2048]{1,0:T(8,128)(2,1)} %bitcast.110), kind=kOutput, calls=%fused_computation.11 | convolution fusion | flops 2215378944 | bytes 8421376 | tf_op jit(solution)/shard_map/dot_general | solution.py:135
  199.8 3.6 %reshape.191 = bf16[32,12,2048]{2,1,0:T(8,128)(2,1)} reshape(bf16[384,2048]{1,0:T(8,128)(2,1)} %convolution_convert_fusion.2) | data formatting | bytes 3145728 | tf_op jit(solution)/shard_map/reshape | solution.py:142
  203.5 4.3 %pad_maximum_fusion = bf16[32,24,2048]{2,1,0:T(8,128)(2,1)} fusion(bf16[32,12,2048]{2,1,0:T(8,128)(2,1)S(1)} %reshape.193, bf16[32,12,2048]{2,1,0:T(8,128)(2,1)} %reshape.191), kind=kLoop, calls=%fused_computation.7 | loop fusion | flops 6291456 | bytes 6291456 | tf_op jit(solution)/shard_map/concatenate | solution.py:140
  207.8 8.7 %all-to-all-start.1 = ((bf16[32,24,2048]{2,1,0:T(8,128)(2,1)}), bf16[32,24,2048]{2,1,0:T(8,128)(2,1)S(1)}, u32[]{:S(2)}, u32[]{:S(2)}) async-start(bf16[32,24,2048]{2,1,0:T(8,128)(2,1)} %pad_maximum_fusion), calls=%async_computation.1 | async-start | bytes 6291456 | tf_op jit(solution)/shard_map/all_to_all | solution.py:139
  216.5 2.1 collective-permute-start.3
  218.7 98.4 %collective-permute-done.3 = bf16[2,176,2048]{2,1,0:T(8,128)(2,1)} collective-permute-done((bf16[2,176,2048]{2,1,0:T(8,128)(2,1)}, bf16[2,176,2048]{2,1,0:T(8,128)(2,1)}, u32[]{:S(2)}, u32[]{:S(2)}) %collective-permute-start.3) | collective-permute-done | bytes 1441824 | tf_op jit(solution)/shard_map/ppermute | solution.py:18
  317.1 2.9 fusion.43
  320.1 3.8 %reshape.199 = bf16[384,2048,1]{1,0,2:T(8,128)(2,1)} reshape(bf16[32,12,2048]{2,1,0:T(8,128)(2,1)} %get-tuple-element.32) | data formatting | bytes 3145728 | tf_op jit(solution)/shard_map/reshape | solution.py:161
  323.8 1.4 reshape.198
  325.2 3.1 convolution_reduce_fusion
  328.3 1.5 fusion.8
  329.8 4.5 %fusion.22 = (bf16[1,176,2048]{2,1,0:T(8,128)(2,1)}, bf16[1,176,2048]{2,1,0:T(8,128)(2,1)}, bf16[1,176,2048]{2,1,0:T(8,128)(2,1)}) fusion(bf16[176,2048]{1,0:T(8,128)(2,1)} %reduce-scatter.5.cloned.1.call-done, bf16[1,176,2048]{2,1,0:T(8,128)(2,1)S(1)} %copy-done.5, bf16[2,176,2048]{2,1,0:T(8,128)(2,1)} %collective-permute-done.3, pred[]{:T(512)} %bitcast.3, ...), kind=kLoop, calls=%fused_computation.41 | loop fusion | flops 7569408 | bytes 6488065 | tf_op jit(solution)/shard_map/broadcast_in_dim | solution.py:191
  334.3 4.5 %fusion.21 = (bf16[1,256,1408]{2,1,0:T(8,128)(2,1)}, bf16[1,256,1408]{2,1,0:T(8,128)(2,1)}, bf16[1,256,1408]{2,1,0:T(8,128)(2,1)}) fusion(bf16[256,1408]{1,0:T(8,128)(2,1)} %reduce-scatter.3.cloned.1.call-done, bf16[1,256,1408]{2,1,0:T(8,128)(2,1)} %param.19, bf16[2,256,1408]{2,1,0:T(8,128)(2,1)} %collective-permute-done.2, pred[]{:T(512)} %bitcast.3, ...), kind=kLoop, calls=%fused_computation.40 | loop fusion | flops 7569408 | bytes 6488065 | tf_op jit(solution)/shard_map/broadcast_in_dim | solution.py:189
  (76 shorter events, 8.8 us)
Async XLA Ops:
  7.2 140.0 %all-gather.5.cloned.1.call-start = ((), (), s32[]{:S(2)}) async-start(), calls=%async_computation.5 | async-start | bytes 6488064 | tf_op jit(solution)/shard_map/all_gather | solution.py:128
  12.3 5.9 %copy-start.14 = (s32[32]{0:T(128)S(1)}, s32[32]{0:T(128)}, u32[]{:S(2)}) copy-start(s32[32]{0:T(128)} %param.15) | copy-start | bytes 388
  12.3 7.1 %copy-start.4 = (bf16[1,176,2048]{2,1,0:T(8,128)(2,1)S(1)}, bf16[1,176,2048]{2,1,0:T(8,128)(2,1)}, u32[]{:S(2)}) copy-start(bf16[1,176,2048]{2,1,0:T(8,128)(2,1)} %param.21) | copy-start | bytes 2162692
  12.3 7.1 %copy-start.6 = (bf16[1,176,2048]{2,1,0:T(8,128)(2,1)S(1)}, bf16[1,176,2048]{2,1,0:T(8,128)(2,1)}, u32[]{:S(2)}) copy-start(bf16[1,176,2048]{2,1,0:T(8,128)(2,1)} %param.20) | copy-start | bytes 2162692
  16.1 4.5 %copy-start.8 = (bf16[1,256,1408]{2,1,0:T(8,128)(2,1)S(1)}, bf16[1,256,1408]{2,1,0:T(8,128)(2,1)}, u32[]{:S(2)}) copy-start(bf16[1,256,1408]{2,1,0:T(8,128)(2,1)} %param.19) | copy-start | bytes 2162692
  16.1 4.5 %copy-start.9 = (bf16[1,256,1408]{2,1,0:T(8,128)(2,1)S(1)}, bf16[1,256,1408]{2,1,0:T(8,128)(2,1)}, u32[]{:S(2)}) copy-start(bf16[1,256,1408]{2,1,0:T(8,128)(2,1)} %param.18) | copy-start | bytes 2162692
  16.1 19.3 %collective-permute-start = (bf16[1,256,1408]{2,1,0:T(8,128)(2,1)}, bf16[1,256,1408]{2,1,0:T(8,128)(2,1)}, u32[]{:S(2)}, u32[]{:S(2)}) collective-permute-start(bf16[1,256,1408]{2,1,0:T(8,128)(2,1)} %param.16), channel_id=1, source_target_pairs={{0,1},{1,0},{2,3},{3,2},{4,5},{5,4},{6,7},{7,6},{8,9},{9,8},{10,11... | collective-permute-start | bytes 2162696 | tf_op jit(solution)/shard_map/ppermute | solution.py:18
  18.0 31.9 %collective-permute-start.1 = (bf16[1,176,2048]{2,1,0:T(8,128)(2,1)}, bf16[1,176,2048]{2,1,0:T(8,128)(2,1)}, u32[]{:S(2)}, u32[]{:S(2)}) collective-permute-start(bf16[1,176,2048]{2,1,0:T(8,128)(2,1)} %param.17), channel_id=1, source_target_pairs={{0,1},{1,0},{2,3},{3,2},{4,5},{5,4},{6,7},{7,6},{8,9},{9,8},{10,11... | collective-permute-start | bytes 2162696 | tf_op jit(solution)/shard_map/ppermute | solution.py:18
  52.0 113.1 %all-gather.3.cloned.1.call-start = ((), (), s32[]{:S(2)}) async-start(), calls=%async_computation.4 | async-start | bytes 6488064 | tf_op jit(solution)/shard_map/all_gather | solution.py:129
  54.1 85.0 %all-to-all-start = ((bf16[32,24,2048]{2,1,0:T(8,128)(2,1)}), bf16[32,24,2048]{2,1,0:T(8,128)(2,1)S(1)}, u32[]{:S(2)}, u32[]{:S(2)}) async-start(bf16[32,24,2048]{2,1,0:T(8,128)(2,1)} %bitcast.107), calls=%async_computation | async-start | bytes 6291456 | tf_op jit(solution)/shard_map/all_to_all | solution.py:109
  65.4 264.4 %reduce-scatter.5.cloned.1.call-start = ((), (), s32[]{:S(2)}) async-start(), calls=%async_computation.7 | async-start | bytes 6488064 | tf_op jit(solution)/shard_map/reduce_scatter | solution.py:171
  65.5 99.5 %collective-permute-start.2 = (bf16[2,256,1408]{2,1,0:T(8,128)(2,1)}, bf16[2,256,1408]{2,1,0:T(8,128)(2,1)}, u32[]{:S(2)}, u32[]{:S(2)}) collective-permute-start(bf16[2,256,1408]{2,1,0:T(8,128)(2,1)} %pad_maximum_fusion.1), channel_id=1, source_target_pairs={{0,1},{1,0},{2,3},{3,2},{4,5},{5,4},{6,7},{7,6},{8,9},{9,8},{10,11... | collective-permute-start | bytes 4325384 | tf_op jit(solution)/shard_map/ppermute | solution.py:18
  142.0 3.8 %copy-start = (bf16[32,12,2048]{2,1,0:T(8,128)(2,1)S(1)}, bf16[32,12,2048]{2,1,0:T(8,128)(2,1)}, u32[]{:S(2)}) copy-start(bf16[32,12,2048]{2,1,0:T(8,128)(2,1)} %get-tuple-element.35) | copy-start | bytes 4718596
  147.1 17.9 %copy-start.11 = (bf16[384,2048]{1,0:T(8,128)(2,1)S(1)}, bf16[384,2048]{1,0:T(8,128)(2,1)}, u32[]{:S(2)}) copy-start(bf16[384,2048]{1,0:T(8,128)(2,1)} %reshape.192) | copy-start | bytes 4718596
  154.4 15.7 %copy-start.15 = (bf16[384,1408]{1,0:T(8,128)(2,1)}, bf16[384,1408]{1,0:T(8,128)(2,1)S(1)}, u32[]{:S(2)}) copy-start(bf16[384,1408]{1,0:T(8,128)(2,1)S(1)} %get-tuple-element.26) | copy-start | bytes 3244036
  170.1 164.2 %reduce-scatter.3.cloned.1.call-start = ((), (), s32[]{:S(2)}) async-start(), calls=%async_computation.6 | async-start | bytes 6488064 | tf_op jit(solution)/shard_map/reduce_scatter | solution.py:165
  170.3 7.3 %copy-start.10 = (bf16[384,2048]{1,0:T(8,128)(2,1)S(1)}, bf16[384,2048]{1,0:T(8,128)(2,1)}, u32[]{:S(2)}) copy-start(bf16[384,2048]{1,0:T(8,128)(2,1)} %reshape.190) | copy-start | bytes 4718596
  207.8 109.4 %all-to-all-start.1 = ((bf16[32,24,2048]{2,1,0:T(8,128)(2,1)}), bf16[32,24,2048]{2,1,0:T(8,128)(2,1)S(1)}, u32[]{:S(2)}, u32[]{:S(2)}) async-start(bf16[32,24,2048]{2,1,0:T(8,128)(2,1)} %pad_maximum_fusion), calls=%async_computation.1 | async-start | bytes 6291456 | tf_op jit(solution)/shard_map/all_to_all | solution.py:139
  216.5 100.7 %collective-permute-start.3 = (bf16[2,176,2048]{2,1,0:T(8,128)(2,1)}, bf16[2,176,2048]{2,1,0:T(8,128)(2,1)}, u32[]{:S(2)}, u32[]{:S(2)}) collective-permute-start(bf16[2,176,2048]{2,1,0:T(8,128)(2,1)} %pad_maximum_fusion.2), channel_id=1, source_target_pairs={{0,1},{1,0},{2,3},{3,2},{4,5},{5,4},{6,7},{7,6},{8,9},{9,8},{10,11... | collective-permute-start | bytes 4325384 | tf_op jit(solution)/shard_map/ppermute | solution.py:18
  320.1 3.8 %copy-start.1 = (bf16[32,12,2048]{2,1,0:T(8,128)(2,1)S(1)}, bf16[32,12,2048]{2,1,0:T(8,128)(2,1)}, u32[]{:S(2)}) copy-start(bf16[32,12,2048]{2,1,0:T(8,128)(2,1)} %get-tuple-element.33) | copy-start | bytes 4718596
  325.2 3.1 copy-start.12
  325.2 3.1 copy-start.13
  328.3 1.6 copy-start.3
  328.3 1.6 copy-start.5
  328.3 1.6 copy-start.7
  329.8 4.5 %copy-start.2 = (bf16[1,256,1408]{2,1,0:T(8,128)(2,1)S(1)}, bf16[1,256,1408]{2,1,0:T(8,128)(2,1)}, u32[]{:S(2)}) copy-start(bf16[1,256,1408]{2,1,0:T(8,128)(2,1)} %broadcast_select_fusion) | copy-start | bytes 2162692
Sparse Core Ops, SparseCore 0:
  52.1 42.1 all-gather.4
  96.7 41.3 all-gather.2
  170.2 40.9 reduce-scatter.4
  213.6 43.2 reduce-scatter.2

commit v3 on v2

--- a/solution.py
+++ b/solution.py
@@ -79,9 +79,6 @@
     dest_hot = jnp.where(swap_flag[None, :] == 1, paired_hot, route_hot)
     position = jnp.sum(jnp.cumsum(dest_hot, axis=0) * dest_hot, axis=1) - 1
     dest = jnp.sum(dest_hot * expert_ids[None, :], axis=1)
-    slot_index = dest * capacity + position
-    pick = slot_index[:, None] == jnp.arange(row_total, dtype=jnp.int32)[None, :]
-    pick_bf = pick.astype(jnp.bfloat16)
     send_row = (dest * (2 * capacity) + position).reshape(tok_count, chosen)
     row_ids = jnp.arange(2 * row_total, dtype=jnp.int32)
     token_pick = jnp.sum(
@@ -122,7 +119,6 @@
         )
     )
     up_moments = partner(up_local, "expert", 0)
-    down_moments = partner(down_local, "expert", 0)
     w_up_use = jnp.where(swapped, w_up_in, w_up)
     w_down_use = jnp.where(swapped, w_down_in, w_down)
     up_full = lax.all_gather(w_up_use, "dp", axis=1, tiled=True)[0]
@@ -131,11 +127,15 @@
     grad_rows = got_both[:, capacity:].reshape(row_total, model_width)
     up_act = jnp.dot(expert_rows, up_full, preferred_element_type=jnp.float32)
     hidden = jax.nn.silu(up_act).astype(jnp.bfloat16)
-    down_full, hidden, up_moments = lax.optimization_barrier((down_full, hidden, up_moments))
+    down_full, hidden, up_moments, down_local = lax.optimization_barrier(
+        (down_full, hidden, up_moments, down_local)
+    )
+    down_moments = partner(down_local, "expert", 0)
     expert_out = jnp.dot(hidden, down_full, preferred_element_type=jnp.float32).astype(jnp.bfloat16)
     hidden_grad = contract_cols(grad_rows, down_full)
     up_grad = (hidden_grad * silu_slope(up_act)).astype(jnp.bfloat16)
     input_part = contract_cols(up_grad, up_full).astype(jnp.bfloat16)
+    input_part, down_moments = lax.optimization_barrier((input_part, down_moments))
     both_back = lax.all_to_all(
         jnp.concatenate(
             [
@@ -149,16 +149,18 @@
         concat_axis=0,
         tiled=True,
     )
-    both_back, down_moments = lax.optimization_barrier((both_back, down_moments))
+    back_rows = both_back.reshape(2 * row_total, model_width)
     picked = jnp.dot(
-        pick_bf,
-        both_back[:, :capacity].reshape(row_total, model_width),
+        (send_row.reshape(pair_count)[:, None] == row_ids[None, :]).astype(jnp.bfloat16),
+        back_rows,
         preferred_element_type=jnp.float32,
     ).reshape(tok_count, chosen, model_width)
     mixed = jnp.sum(gates[:, :, None] * picked, axis=1).astype(jnp.bfloat16)
     picked_grad = jnp.dot(
-        pick_bf,
-        both_back[:, capacity:].reshape(row_total, model_width),
+        (send_row.reshape(pair_count)[:, None] + capacity == row_ids[None, :]).astype(
+            jnp.bfloat16
+        ),
+        back_rows,
         preferred_element_type=jnp.float32,
     ).reshape(tok_count, chosen, model_width)
     input_grad = jnp.sum(picked_grad, axis=1).astype(jnp.bfloat16)

time: 346 us -> 325 us (0.939)
  waiting for transfers between devices: 209 us -> 126 us
  blocking collectives: 0 us -> 82.6 us
  starting transfers between devices: 26.4 us -> 16 us
  local copies, waits for them, and re-layouts: 24.6 us -> 17.5 us
    ppermute x4, waiting for transfers between devices: 137 us -> 54.4 us  [partner(): return lax.ppermute(value, axis, pairs)]
    all_to_all x0 -> x1, blocking collectives: none -> 82.6 us  [body(): lax.all_to_all(jnp.concatenate([expert_out.reshape(experts, capacity, mod...]
    all_to_all x1 -> x0, starting transfers between devices: 8.7 us -> none  [body(): lax.all_to_all(jnp.concatenate([expert_out.reshape(experts, capacity, mod...]
    reshape x3 -> x1, local copies, waits for them, and re-layouts: 5.14 us -> 0.01 us  [the longest x1 3.75 us: body(): both_back[:, capacity:].reshape(row_total, model_width)]
  transfers between devices with their start and end apart: 10 -> 9, of which waited for: 5 -> 5; matrix products, arithmetic and copies ran while one was open for 22% -> 20% of each run, Pallas kernels for 0% -> 0%
where the time goes in v3:
time: 325 us; the launch traced here: 324 us
  waiting for transfers between devices  126 us (39%)
  blocking collectives  82.6 us (25%)
  matrix products  45.7 us (14%)
  other arithmetic  21.2 us (7%)
  local copies, waits for them, and re-layouts  17.5 us (5%)
  starting transfers between devices  16 us (5%)
  between operations  14.6 us (4%)
    all_to_all x1, blocking collectives, body(): lax.all_to_all(jnp.concatenate([expert_out.reshape(experts, capacity, mod...  82.6 us
    all_to_all x1, waiting for transfers between devices, body(): lax.all_to_all(send_both.reshape(experts, 2 * capacity, model_width), 'ex...  71.8 us
    ppermute x4, waiting for transfers between devices, partner(): return lax.ppermute(value, axis, pairs)  54.4 us
    dot_general x2, matrix products, contract_cols(): lax.dot_general(left, right, (((1,), (1,)), ((), ())), preferred_element_...  14.2 us
    all_to_all x1, starting transfers between devices, body(): lax.all_to_all(send_both.reshape(experts, 2 * capacity, model_width), 'ex...  11.3 us
    dot_general x2, matrix products, contract_rows(): lax.dot_general(left, right, (((0,), (0,)), ((), ())), preferred_element_...  10.2 us
    dot_general x1, matrix products, body(): up_act = jnp.dot(expert_rows, up_full, preferred_element_type=jnp.float32)  7.29 us
  transfers between devices with their start and end apart: 9, of which 5 were waited for; matrix products, arithmetic and copies ran while one was open for 20% of the time, Pallas kernels for 0%

profile of v3, /device:TPU:6, one launch (start us, length us, event | category | flops | bytes accessed | tf_op | source)
XLA Modules:
  0.0 323.9 jit_solution(8174421439520088173)
XLA Ops:
  9.5 0.9 reduce-window.6
  11.3 0.8 select_reduce_fusion
  12.2 3.9 %multiply_convert_fusion = bf16[768,2048]{1,0:T(8,128)(2,1)} fusion(f32[768]{0:T(1024)S(1)} %add.112, bf16[48,2048]{1,0:T(8,128)(2,1)} %param.14, bf16[48,2048]{1,0:T(8,128)(2,1)} %param.11, bf16[48,768]{1,0:T(8,128)(2,1)S(1)} %get-tuple-element.45, bf16[48,768]{1,0:T(8,128)(2,1)S(1)} %get-tuple-element.44), kind=kOutput, calls=%fused_computation.2 | convolution fusion | flops 306216960 | bytes 3689472 | tf_op jit(solution)/shard_map/dot_general | solution.py:96
  16.1 1.9 collective-permute-start
  19.4 1.2 pad_maximum_fusion.2
  20.6 1.2 pad_maximum_fusion.1
  21.9 13.6 %collective-permute-done = bf16[1,256,1408]{2,1,0:T(8,128)(2,1)} collective-permute-done((bf16[1,256,1408]{2,1,0:T(8,128)(2,1)}, bf16[1,256,1408]{2,1,0:T(8,128)(2,1)}, u32[]{:S(2)}, u32[]{:S(2)}) %collective-permute-start) | collective-permute-done | bytes 720928 | tf_op jit(solution)/shard_map/ppermute | solution.py:18
  35.4 14.5 %collective-permute-done.1 = bf16[1,176,2048]{2,1,0:T(8,128)(2,1)} collective-permute-done((bf16[1,176,2048]{2,1,0:T(8,128)(2,1)}, bf16[1,176,2048]{2,1,0:T(8,128)(2,1)}, u32[]{:S(2)}, u32[]{:S(2)}) %collective-permute-start.1) | collective-permute-done | bytes 720928 | tf_op jit(solution)/shard_map/ppermute | solution.py:18
  49.9 2.1 broadcast_select_fusion
  52.0 2.1 broadcast_select_fusion.1
  54.1 11.3 %all-to-all-start = ((bf16[32,24,2048]{2,1,0:T(8,128)(2,1)}), bf16[32,24,2048]{2,1,0:T(8,128)(2,1)S(1)}, u32[]{:S(2)}, u32[]{:S(2)}) async-start(bf16[32,24,2048]{2,1,0:T(8,128)(2,1)} %bitcast.112), calls=%async_computation | async-start | bytes 6291456 | tf_op jit(solution)/shard_map/all_to_all | solution.py:106
  65.5 1.9 collective-permute-start.2
  67.4 71.8 %all-to-all-done = bf16[32,24,2048]{2,1,0:T(8,128)(2,1)S(1)} async-done(((bf16[32,24,2048]{2,1,0:T(8,128)(2,1)}), bf16[32,24,2048]{2,1,0:T(8,128)(2,1)S(1)}, u32[]{:S(2)}, u32[]{:S(2)}) %all-to-all-start) | async-done | bytes 3145760 | tf_op jit(solution)/shard_map/all_to_all | solution.py:106
  139.1 3.0 fusion.44
  142.1 3.8 %reshape.201 = bf16[384,2048]{1,0:T(8,128)(2,1)} reshape(bf16[32,12,2048]{2,1,0:T(8,128)(2,1)} %get-tuple-element.34) | data formatting | bytes 3145728 | tf_op jit(solution)/shard_map/reshape | solution.py:126
  145.9 1.4 reshape.203
  147.3 7.3 %multiply_convert_fusion.1 = (bf16[384,1408]{1,0:T(8,128)(2,1)S(1)}, f32[384,1408]{1,0:T(8,128)}) fusion(bf16[384,2048]{1,0:T(8,128)(2,1)} %reshape.201, bf16[1,2048,1408]{2,1,0:T(8,128)(2,1)} %all-gather.5.cloned.1.call-done), kind=kOutput, calls=%fused_computation.13 | convolution fusion | flops 2217295872 | bytes 10584064 | tf_op jit(solution)/shard_map/dot_general | solution.py:128
  154.5 10.5 %collective-permute-done.2 = bf16[2,256,1408]{2,1,0:T(8,128)(2,1)} collective-permute-done((bf16[2,256,1408]{2,1,0:T(8,128)(2,1)}, bf16[2,256,1408]{2,1,0:T(8,128)(2,1)}, u32[]{:S(2)}, u32[]{:S(2)}) %collective-permute-start.2) | collective-permute-done | bytes 1441824 | tf_op jit(solution)/shard_map/ppermute | solution.py:18
  165.1 5.0 %convolution_convert_fusion = bf16[1408,2048]{1,0:T(8,128)(2,1)} fusion(bf16[384,1408]{1,0:T(8,128)(2,1)S(1)} %get-tuple-element.28, bf16[384,2048]{1,0:T(8,128)(2,1)S(1)} %copy-done.10), kind=kOutput, calls=%fused_computation | convolution fusion | flops 2217476096 | bytes 8421376 | tf_op jit(solution)/shard_map/dot_general | solution.py:44
  170.3 7.2 %fusion.4 = bf16[384,1408]{1,0:T(8,128)(2,1)S(1)} fusion(bf16[384,2048]{1,0:T(8,128)(2,1)S(1)} %copy-done.10, bf16[1408,2048]{1,0:T(8,128)(2,1)} %bitcast.116, f32[384,1408]{1,0:T(8,128)} %get-tuple-element.43), kind=kOutput, calls=%fused_computation.9 | convolution fusion | flops 2219458560 | bytes 10584064 | tf_op jit(solution)/shard_map/dot_general | solution.py:50
  177.6 5.2 %convolution_convert_fusion.1 = bf16[2048,1408]{1,0:T(8,128)(2,1)} fusion(bf16[384,2048]{1,0:T(8,128)(2,1)S(1)} %copy-done.9, bf16[384,1408]{1,0:T(8,128)(2,1)S(1)} %fusion.4), kind=kOutput, calls=%fused_computation.1 | convolution fusion | flops 2217476096 | bytes 8421376 | tf_op jit(solution)/shard_map/dot_general | solution.py:44
  184.0 6.4 %convolution_convert_fusion.2 = bf16[384,2048]{1,0:T(8,128)(2,1)} fusion(bf16[384,1408]{1,0:T(8,128)(2,1)S(1)} %copy-done.15, bf16[1408,2048]{1,0:T(8,128)(2,1)} %bitcast.117), kind=kOutput, calls=%fused_computation.11 | convolution fusion | flops 2215378944 | bytes 8421376 | tf_op jit(solution)/shard_map/dot_general | solution.py:134
  190.4 2.4 reshape.202
  192.8 6.9 %fusion.5 = bf16[384,2048]{1,0:T(8,128)(2,1)} fusion(bf16[384,1408]{1,0:T(8,128)(2,1)} %copy-done.16, bf16[1,2048,1408]{2,1,0:T(8,128)(2,1)} %all-gather.5.cloned.1.call-done), kind=kOutput, calls=%fused_computation.10 | convolution fusion | flops 2215378944 | bytes 8421376 | tf_op jit(solution)/shard_map/dot_general | solution.py:50
  199.8 15.8 %collective-permute-done.3 = bf16[2,176,2048]{2,1,0:T(8,128)(2,1)S(1)} collective-permute-done((bf16[2,176,2048]{2,1,0:T(8,128)(2,1)}, bf16[2,176,2048]{2,1,0:T(8,128)(2,1)S(1)}, u32[]{:S(2)}, u32[]{:S(2)}) %collective-permute-start.3) | collective-permute-done | bytes 1441824 | tf_op jit(solution)/shard_map/ppermute | solution.py:18
  215.6 4.0 %reshape.204 = bf16[32,12,2048]{2,1,0:T(8,128)(2,1)} reshape(bf16[384,2048]{1,0:T(8,128)(2,1)} %fusion.5) | data formatting | bytes 3145728 | tf_op jit(solution)/shard_map/reshape | solution.py:143
  219.6 2.5 pad_maximum_fusion
  222.1 82.6 %all_to_all.10 = bf16[32,24,2048]{2,1,0:T(8,128)(2,1)S(1)} all-to-all(bf16[32,24,2048]{2,1,0:T(8,128)(2,1)S(1)} %pad_maximum_fusion), channel_id=1, replica_groups=mesh['dp'=8,'expert'=32] {'expert'}, dimensions={0} | all-to-all | bytes 6291456 | tf_op jit(solution)/shard_map/all_to_all | solution.py:139
  304.7 1.8 convolution_reduce_fusion
  306.5 1.9 fusion.8
  308.4 4.5 %fusion.26 = (bf16[1,176,2048]{2,1,0:T(8,128)(2,1)}, bf16[1,176,2048]{2,1,0:T(8,128)(2,1)}, bf16[1,176,2048]{2,1,0:T(8,128)(2,1)}) fusion(bf16[176,2048]{1,0:T(8,128)(2,1)} %reduce-scatter.5.cloned.1.call-done, bf16[1,176,2048]{2,1,0:T(8,128)(2,1)S(1)} %copy-done.4, bf16[2,176,2048]{2,1,0:T(8,128)(2,1)} %copy-done.11, pred[]{:T(512)} %bitcast.3, ...), kind=kLoop, calls=%fused_computation.45 | loop fusion | flops 7569408 | bytes 6488065 | tf_op jit(solution)/shard_map/broadcast_in_dim | solution.py:193
  312.9 4.5 %fusion.25 = (bf16[1,256,1408]{2,1,0:T(8,128)(2,1)}, bf16[1,256,1408]{2,1,0:T(8,128)(2,1)}, bf16[1,256,1408]{2,1,0:T(8,128)(2,1)}) fusion(bf16[256,1408]{1,0:T(8,128)(2,1)} %reduce-scatter.3.cloned.1.call-done, bf16[1,256,1408]{2,1,0:T(8,128)(2,1)} %param.19, bf16[2,256,1408]{2,1,0:T(8,128)(2,1)} %collective-permute-done.2, pred[]{:T(512)} %bitcast.3, ...), kind=kLoop, calls=%fused_computation.44 | loop fusion | flops 7569408 | bytes 6488065 | tf_op jit(solution)/shard_map/broadcast_in_dim | solution.py:191
  (71 shorter events, 5.5 us)
Async XLA Ops:
  7.2 140.1 %all-gather.5.cloned.1.call-start = ((), (), s32[]{:S(2)}) async-start(), calls=%async_computation.5 | async-start | bytes 6488064 | tf_op jit(solution)/shard_map/all_gather | solution.py:124
  12.2 6.0 %copy-start.13 = (s32[32]{0:T(128)S(1)}, s32[32]{0:T(128)}, u32[]{:S(2)}) copy-start(s32[32]{0:T(128)} %param.15) | copy-start | bytes 388
  12.2 7.2 %copy-start.3 = (bf16[1,176,2048]{2,1,0:T(8,128)(2,1)S(1)}, bf16[1,176,2048]{2,1,0:T(8,128)(2,1)}, u32[]{:S(2)}) copy-start(bf16[1,176,2048]{2,1,0:T(8,128)(2,1)} %param.21) | copy-start | bytes 2162692
  12.2 7.2 %copy-start.5 = (bf16[1,176,2048]{2,1,0:T(8,128)(2,1)S(1)}, bf16[1,176,2048]{2,1,0:T(8,128)(2,1)}, u32[]{:S(2)}) copy-start(bf16[1,176,2048]{2,1,0:T(8,128)(2,1)} %param.20) | copy-start | bytes 2162692
  16.1 4.5 %copy-start.7 = (bf16[1,256,1408]{2,1,0:T(8,128)(2,1)S(1)}, bf16[1,256,1408]{2,1,0:T(8,128)(2,1)}, u32[]{:S(2)}) copy-start(bf16[1,256,1408]{2,1,0:T(8,128)(2,1)} %param.19) | copy-start | bytes 2162692
  16.1 4.5 %copy-start.8 = (bf16[1,256,1408]{2,1,0:T(8,128)(2,1)S(1)}, bf16[1,256,1408]{2,1,0:T(8,128)(2,1)}, u32[]{:S(2)}) copy-start(bf16[1,256,1408]{2,1,0:T(8,128)(2,1)} %param.18) | copy-start | bytes 2162692
  16.1 19.3 %collective-permute-start = (bf16[1,256,1408]{2,1,0:T(8,128)(2,1)}, bf16[1,256,1408]{2,1,0:T(8,128)(2,1)}, u32[]{:S(2)}, u32[]{:S(2)}) collective-permute-start(bf16[1,256,1408]{2,1,0:T(8,128)(2,1)} %param.16), channel_id=1, source_target_pairs={{0,1},{1,0},{2,3},{3,2},{4,5},{5,4},{6,7},{7,6},{8,9},{9,8},{10,11... | collective-permute-start | bytes 2162696 | tf_op jit(solution)/shard_map/ppermute | solution.py:18
  18.0 31.9 %collective-permute-start.1 = (bf16[1,176,2048]{2,1,0:T(8,128)(2,1)}, bf16[1,176,2048]{2,1,0:T(8,128)(2,1)}, u32[]{:S(2)}, u32[]{:S(2)}) collective-permute-start(bf16[1,176,2048]{2,1,0:T(8,128)(2,1)} %param.17), channel_id=1, source_target_pairs={{0,1},{1,0},{2,3},{3,2},{4,5},{5,4},{6,7},{7,6},{8,9},{9,8},{10,11... | collective-permute-start | bytes 2162696 | tf_op jit(solution)/shard_map/ppermute | solution.py:18
  52.0 113.1 %all-gather.3.cloned.1.call-start = ((), (), s32[]{:S(2)}) async-start(), calls=%async_computation.4 | async-start | bytes 6488064 | tf_op jit(solution)/shard_map/all_gather | solution.py:125
  54.1 85.0 %all-to-all-start = ((bf16[32,24,2048]{2,1,0:T(8,128)(2,1)}), bf16[32,24,2048]{2,1,0:T(8,128)(2,1)S(1)}, u32[]{:S(2)}, u32[]{:S(2)}) async-start(bf16[32,24,2048]{2,1,0:T(8,128)(2,1)} %bitcast.112), calls=%async_computation | async-start | bytes 6291456 | tf_op jit(solution)/shard_map/all_to_all | solution.py:106
  65.5 243.0 %reduce-scatter.5.cloned.1.call-start = ((), (), s32[]{:S(2)}) async-start(), calls=%async_computation.7 | async-start | bytes 6488064 | tf_op jit(solution)/shard_map/reduce_scatter | solution.py:173
  65.5 99.5 %collective-permute-start.2 = (bf16[2,256,1408]{2,1,0:T(8,128)(2,1)}, bf16[2,256,1408]{2,1,0:T(8,128)(2,1)}, u32[]{:S(2)}, u32[]{:S(2)}) collective-permute-start(bf16[2,256,1408]{2,1,0:T(8,128)(2,1)} %pad_maximum_fusion.1), channel_id=1, source_target_pairs={{0,1},{1,0},{2,3},{3,2},{4,5},{5,4},{6,7},{7,6},{8,9},{9,8},{10,11... | collective-permute-start | bytes 4325384 | tf_op jit(solution)/shard_map/ppermute | solution.py:18
  142.1 3.8 %copy-start = (bf16[32,12,2048]{2,1,0:T(8,128)(2,1)S(1)}, bf16[32,12,2048]{2,1,0:T(8,128)(2,1)}, u32[]{:S(2)}) copy-start(bf16[32,12,2048]{2,1,0:T(8,128)(2,1)} %get-tuple-element.35) | copy-start | bytes 4718596
  147.2 17.8 %copy-start.10 = (bf16[384,2048]{1,0:T(8,128)(2,1)S(1)}, bf16[384,2048]{1,0:T(8,128)(2,1)}, u32[]{:S(2)}) copy-start(bf16[384,2048]{1,0:T(8,128)(2,1)} %reshape.203) | copy-start | bytes 4718596
  154.5 15.5 %copy-start.14 = (bf16[384,1408]{1,0:T(8,128)(2,1)}, bf16[384,1408]{1,0:T(8,128)(2,1)S(1)}, u32[]{:S(2)}) copy-start(bf16[384,1408]{1,0:T(8,128)(2,1)S(1)} %get-tuple-element.28) | copy-start | bytes 3244036
  170.1 142.9 %reduce-scatter.3.cloned.1.call-start = ((), (), s32[]{:S(2)}) async-start(), calls=%async_computation.6 | async-start | bytes 6488064 | tf_op jit(solution)/shard_map/reduce_scatter | solution.py:167
  170.3 7.3 %copy-start.9 = (bf16[384,2048]{1,0:T(8,128)(2,1)S(1)}, bf16[384,2048]{1,0:T(8,128)(2,1)}, u32[]{:S(2)}) copy-start(bf16[384,2048]{1,0:T(8,128)(2,1)} %reshape.201) | copy-start | bytes 4718596
  177.6 5.2 %copy-start.16 = (bf16[384,1408]{1,0:T(8,128)(2,1)}, bf16[384,1408]{1,0:T(8,128)(2,1)S(1)}, u32[]{:S(2)}) copy-start(bf16[384,1408]{1,0:T(8,128)(2,1)S(1)} %fusion.4) | copy-start | bytes 3244036
  182.8 1.2 copy-start.15
  182.8 32.8 %collective-permute-start.3 = (bf16[2,176,2048]{2,1,0:T(8,128)(2,1)}, bf16[2,176,2048]{2,1,0:T(8,128)(2,1)S(1)}, u32[]{:S(2)}, u32[]{:S(2)}) collective-permute-start(bf16[2,176,2048]{2,1,0:T(8,128)(2,1)} %pad_maximum_fusion.2), channel_id=1, source_target_pairs={{0,1},{1,0},{2,3},{3,2},{4,5},{5,4},{6,7},{7,6},{8,9},{9,8},{10,11... | collective-permute-start | bytes 4325384 | tf_op jit(solution)/shard_map/ppermute | solution.py:18
  215.6 4.0 %copy-start.11 = (bf16[2,176,2048]{2,1,0:T(8,128)(2,1)}, bf16[2,176,2048]{2,1,0:T(8,128)(2,1)S(1)}, u32[]{:S(2)}) copy-start(bf16[2,176,2048]{2,1,0:T(8,128)(2,1)S(1)} %collective-permute-done.3) | copy-start | bytes 4325380
  304.7 1.9 copy-start.12
  306.5 1.9 copy-start.2
  306.5 1.9 copy-start.4
  306.5 1.9 copy-start.6
  308.4 4.5 %copy-start.1 = (bf16[1,256,1408]{2,1,0:T(8,128)(2,1)S(1)}, bf16[1,256,1408]{2,1,0:T(8,128)(2,1)}, u32[]{:S(2)}) copy-start(bf16[1,256,1408]{2,1,0:T(8,128)(2,1)} %broadcast_select_fusion) | copy-start | bytes 2162692
Sparse Core Ops, SparseCore 0:
  52.1 42.1 all-gather.4
  96.7 41.3 all-gather.2
  170.2 40.9 reduce-scatter.4
  213.6 43.2 reduce-scatter.2

commit v4 on v2

--- a/solution.py
+++ b/solution.py
@@ -79,40 +79,41 @@
     dest_hot = jnp.where(swap_flag[None, :] == 1, paired_hot, route_hot)
     position = jnp.sum(jnp.cumsum(dest_hot, axis=0) * dest_hot, axis=1) - 1
     dest = jnp.sum(dest_hot * expert_ids[None, :], axis=1)
-    slot_index = dest * capacity + position
-    pick = slot_index[:, None] == jnp.arange(row_total, dtype=jnp.int32)[None, :]
-    pick_bf = pick.astype(jnp.bfloat16)
-    send_row = (dest * (2 * capacity) + position).reshape(tok_count, chosen)
-    row_ids = jnp.arange(2 * row_total, dtype=jnp.int32)
-    token_pick = jnp.sum(
-        (send_row[:, :, None] == row_ids[None, None, :]).astype(jnp.bfloat16), axis=1
-    )
-    grad_pick = jnp.sum(
-        (send_row[:, :, None] + capacity == row_ids[None, None, :]).astype(jnp.bfloat16), axis=1
-    )
-    row_scale = jnp.sum(
-        jnp.where(
-            send_row[:, :, None] + capacity == row_ids[None, None, :], gates[:, :, None], 0.0
-        ),
-        axis=(0, 1),
-    ) + jnp.sum(token_pick.astype(jnp.float32), axis=0)
+    half = capacity // 2
+    chunk_rows = experts * 2 * half
+    send_row = (
+        (position // half) * chunk_rows + dest * (2 * half) + position % half
+    ).reshape(tok_count, chosen)
+    row_ids = jnp.arange(2 * chunk_rows, dtype=jnp.int32)
+    token_hit = send_row[:, :, None] == row_ids[None, None, :]
+    grad_hit = send_row[:, :, None] + half == row_ids[None, None, :]
+    token_pick = jnp.sum(token_hit.astype(jnp.bfloat16), axis=1)
+    grad_pick = jnp.sum(grad_hit.astype(jnp.bfloat16), axis=1)
+    row_scale = jnp.sum(jnp.where(grad_hit, gates[:, :, None], 0.0), axis=(0, 1)) + jnp.sum(
+        token_pick.astype(jnp.float32), axis=0
+    )
     picked_rows = lax.dot_general(
         jnp.concatenate([token_pick, grad_pick], axis=0),
         jnp.concatenate([tokens, cotangent], axis=0),
         (((0,), (0,)), ((), ())),
         preferred_element_type=jnp.float32,
     )
-    send_both = (row_scale[:, None] * picked_rows).astype(jnp.bfloat16)
-    w_up, w_down, send_both = lax.optimization_barrier((w_up, w_down, send_both))
+    send_all = (row_scale[:, None] * picked_rows).astype(jnp.bfloat16)
+    w_up, w_down, send_all = lax.optimization_barrier((w_up, w_down, send_all))
     w_up_in = partner(w_up, "expert", 0)
     w_down_in = partner(w_down, "expert", 0)
-    got_both = lax.all_to_all(
-        send_both.reshape(experts, 2 * capacity, model_width),
-        "expert",
-        split_axis=0,
-        concat_axis=0,
-        tiled=True,
-    )
+    got = [
+        lax.all_to_all(
+            send_all[number * chunk_rows : (number + 1) * chunk_rows].reshape(
+                experts, 2 * half, model_width
+            ),
+            "expert",
+            split_axis=0,
+            concat_axis=0,
+            tiled=True,
+        )
+        for number in range(2)
+    ]
     w_up_in, w_down_in, up_local, down_local = lax.optimization_barrier(
         (
             w_up_in,
@@ -122,57 +123,79 @@
         )
     )
     up_moments = partner(up_local, "expert", 0)
-    down_moments = partner(down_local, "expert", 0)
     w_up_use = jnp.where(swapped, w_up_in, w_up)
     w_down_use = jnp.where(swapped, w_down_in, w_down)
     up_full = lax.all_gather(w_up_use, "dp", axis=1, tiled=True)[0]
     down_full = lax.all_gather(w_down_use, "dp", axis=1, tiled=True)[0]
-    expert_rows = got_both[:, :capacity].reshape(row_total, model_width)
-    grad_rows = got_both[:, capacity:].reshape(row_total, model_width)
-    up_act = jnp.dot(expert_rows, up_full, preferred_element_type=jnp.float32)
-    hidden = jax.nn.silu(up_act).astype(jnp.bfloat16)
-    down_full, hidden, up_moments = lax.optimization_barrier((down_full, hidden, up_moments))
-    expert_out = jnp.dot(hidden, down_full, preferred_element_type=jnp.float32).astype(jnp.bfloat16)
-    hidden_grad = contract_cols(grad_rows, down_full)
-    up_grad = (hidden_grad * silu_slope(up_act)).astype(jnp.bfloat16)
-    input_part = contract_cols(up_grad, up_full).astype(jnp.bfloat16)
-    both_back = lax.all_to_all(
-        jnp.concatenate(
-            [
-                expert_out.reshape(experts, capacity, model_width),
-                input_part.reshape(experts, capacity, model_width),
-            ],
-            axis=1,
-        ),
-        "expert",
-        split_axis=0,
-        concat_axis=0,
-        tiled=True,
-    )
-    both_back, down_moments = lax.optimization_barrier((both_back, down_moments))
-    picked = jnp.dot(
-        pick_bf,
-        both_back[:, :capacity].reshape(row_total, model_width),
-        preferred_element_type=jnp.float32,
+    part_rows = experts * half
+    back = []
+    up_part = None
+    down_part = None
+    for number in range(2):
+        expert_rows = got[number][:, :half].reshape(part_rows, model_width)
+        grad_rows = got[number][:, half:].reshape(part_rows, model_width)
+        up_act = jnp.dot(expert_rows, up_full, preferred_element_type=jnp.float32)
+        hidden = jax.nn.silu(up_act).astype(jnp.bfloat16)
+        if number == 0:
+            down_full, hidden, up_moments, down_local = lax.optimization_barrier(
+                (down_full, hidden, up_moments, down_local)
+            )
+            down_moments = partner(down_local, "expert", 0)
+        expert_out = jnp.dot(hidden, down_full, preferred_element_type=jnp.float32).astype(
+            jnp.bfloat16
+        )
+        hidden_grad = contract_cols(grad_rows, down_full)
+        up_grad = (hidden_grad * silu_slope(up_act)).astype(jnp.bfloat16)
+        input_part = contract_cols(up_grad, up_full).astype(jnp.bfloat16)
+        if number == 1:
+            input_part, down_moments = lax.optimization_barrier((input_part, down_moments))
+        back.append(
+            lax.all_to_all(
+                jnp.concatenate(
+                    [
+                        expert_out.reshape(experts, half, model_width),
+                        input_part.reshape(experts, half, model_width),
+                    ],
+                    axis=1,
+                ),
+                "expert",
+                split_axis=0,
+                concat_axis=0,
+                tiled=True,
+            ).reshape(chunk_rows, model_width)
+        )
+        up_term = contract_rows(expert_rows, up_grad)
+        down_term = contract_rows(hidden, grad_rows)
+        up_part = up_term if up_part is None else up_part + up_term
+        down_part = down_term if down_part is None else down_part + down_term
+    flat_row = send_row.reshape(pair_count)[:, None]
+    picked = sum(
+        jnp.dot(
+            (flat_row == row_ids[None, number * chunk_rows : (number + 1) * chunk_rows]).astype(
+                jnp.bfloat16
+            ),
+            back[number],
+            preferred_element_type=jnp.float32,
+        )
+        for number in range(2)
     ).reshape(tok_count, chosen, model_width)
     mixed = jnp.sum(gates[:, :, None] * picked, axis=1).astype(jnp.bfloat16)
-    picked_grad = jnp.dot(
-        pick_bf,
-        both_back[:, capacity:].reshape(row_total, model_width),
-        preferred_element_type=jnp.float32,
+    picked_grad = sum(
+        jnp.dot(
+            (
+                flat_row + half == row_ids[None, number * chunk_rows : (number + 1) * chunk_rows]
+            ).astype(jnp.bfloat16),
+            back[number],
+            preferred_element_type=jnp.float32,
+        )
+        for number in range(2)
     ).reshape(tok_count, chosen, model_width)
     input_grad = jnp.sum(picked_grad, axis=1).astype(jnp.bfloat16)
     up_gradient = lax.psum_scatter(
-        contract_rows(expert_rows, up_grad).astype(jnp.bfloat16),
-        "dp",
-        scatter_dimension=0,
-        tiled=True,
+        up_part.astype(jnp.bfloat16), "dp", scatter_dimension=0, tiled=True
     ).astype(jnp.float32)
     down_gradient = lax.psum_scatter(
-        contract_rows(hidden, grad_rows).astype(jnp.bfloat16),
-        "dp",
-        scatter_dimension=0,
-        tiled=True,
+        down_part.astype(jnp.bfloat16), "dp", scatter_dimension=0, tiled=True
     ).astype(jnp.float32)
     m_up_use = jnp.where(swapped, up_moments[0:1], m_up)
     v_up_use = jnp.where(swapped, up_moments[1:2], v_up)

time: 346 us -> 440 us (1.27); the launches traced: 345 us -> 434 us
  waiting for transfers between devices: 209 us -> 239 us
  local copies, waits for them, and re-layouts: 24.6 us -> 43.4 us
  matrix products: 47.7 us -> 63.5 us
  starting transfers between devices: 26.4 us -> 41.1 us
  other arithmetic: 23.1 us -> 31.5 us
    all_to_all x2 -> x4, waiting for transfers between devices: 71.8 us -> 132 us  [the longest x2 87.8 us: body(): lax.all_to_all(send_all[number * chunk_rows:(number + 1) * chunk_rows].re...]
    ppermute x4, waiting for transfers between devices: 137 us -> 107 us  [partner(): return lax.ppermute(value, axis, pairs)]
    all_to_all x2 -> x4, starting transfers between devices: 20 us -> 34.4 us  [the longest x2 17.3 us: body(): lax.all_to_all(jnp.concatenate([expert_out.reshape(experts, half, model_w...]
    reshape x7 -> x15, local copies, waits for them, and re-layouts: 16.3 us -> 30.3 us  [the longest x2 7.27 us: body(): send_all[number * chunk_rows:(number + 1) * chunk_rows]]
    dot_general x2 -> x4, matrix products: 4.6 us -> 12.8 us  [the longest x2 6.74 us: body(): jnp.dot((flat_row == row_ids[None, number * chunk_rows:(number + 1) * chu...]
    reduce_sum x2 -> x4, other arithmetic: 1.12 us -> 6.64 us  [the longest x1 3.72 us: body(): input_grad = jnp.sum(picked_grad, axis=1).astype(jnp.bfloat16)]
    dot_general x1 -> x2, matrix products: 6.91 us -> 10.3 us  [body(): jnp.dot(hidden, down_full, preferred_element_type=jnp.float32)]
    dot_general x2 -> x4, matrix products: 14.9 us -> 17.8 us  [contract_cols(): lax.dot_general(left, right, (((1,), (1,)), ((), ())), preferred_element_...]
  transfers between devices with their start and end apart: 10 -> 12, of which waited for: 5 -> 7; matrix products, arithmetic and copies ran while one was open for 22% -> 26% of each run, Pallas kernels for 0% -> 0%
where the time goes in v4:
time: 440 us; the launch traced here: 434 us
  waiting for transfers between devices  239 us (54%)
  matrix products  63.5 us (14%)
  local copies, waits for them, and re-layouts  43.4 us (10%)
  starting transfers between devices  41.1 us (9%)
  other arithmetic  31.5 us (7%)
  between operations  15.3 us (3%)
    ppermute x4, waiting for transfers between devices, partner(): return lax.ppermute(value, axis, pairs)  107 us
    all_to_all x2, waiting for transfers between devices, body(): lax.all_to_all(send_all[number * chunk_rows:(number + 1) * chunk_rows].re...  87.8 us
    all_to_all x2, waiting for transfers between devices, body(): lax.all_to_all(jnp.concatenate([expert_out.reshape(experts, half, model_w...  44 us
    dot_general x4, matrix products, contract_cols(): lax.dot_general(left, right, (((1,), (1,)), ((), ())), preferred_element_...  17.8 us
    all_to_all x2, starting transfers between devices, body(): lax.all_to_all(jnp.concatenate([expert_out.reshape(experts, half, model_w...  17.3 us
    all_to_all x2, starting transfers between devices, body(): lax.all_to_all(send_all[number * chunk_rows:(number + 1) * chunk_rows].re...  17.1 us
    dot_general x4, matrix products, contract_rows(): lax.dot_general(left, right, (((0,), (0,)), ((), ())), preferred_element_...  12.1 us
    dot_general x2, matrix products, body(): jnp.dot(hidden, down_full, preferred_element_type=jnp.float32)  10.3 us
  transfers between devices with their start and end apart: 12, of which 7 were waited for; matrix products, arithmetic and copies ran while one was open for 26% of the time, Pallas kernels for 0%

profile of v4, /device:TPU:6, one launch (start us, length us, event | category | flops | bytes accessed | tf_op | source)
XLA Modules:
  0.0 434.2 jit_solution(9814252083954812429)
XLA Ops:
  21.3 12.1 %collective-permute-done = bf16[1,256,1408]{2,1,0:T(8,128)(2,1)} collective-permute-done((bf16[1,256,1408]{2,1,0:T(8,128)(2,1)}, bf16[1,256,1408]{2,1,0:T(8,128)(2,1)}, u32[]{:S(2)}, u32[]{:S(2)}) %collective-permute-start) | collective-permute-done | bytes 720928 | tf_op jit(solution)/shard_map/ppermute | solution.py:18
  33.4 14.5 %collective-permute-done.1 = bf16[1,176,2048]{2,1,0:T(8,128)(2,1)} collective-permute-done((bf16[1,176,2048]{2,1,0:T(8,128)(2,1)}, bf16[1,176,2048]{2,1,0:T(8,128)(2,1)}, u32[]{:S(2)}, u32[]{:S(2)}) %collective-permute-start.1) | collective-permute-done | bytes 720928 | tf_op jit(solution)/shard_map/ppermute | solution.py:18
  54.1 3.7 reshape.213
  57.7 11.3 %all-to-all-start.2 = ((bf16[32,12,2048]{2,1,0:T(8,128)(2,1)}), bf16[32,12,2048]{2,1,0:T(8,128)(2,1)S(1)}, u32[]{:S(2)}, u32[]{:S(2)}) async-start(bf16[32,12,2048]{2,1,0:T(8,128)(2,1)} %reshape.213), calls=%async_computation.2 | async-start | bytes 4194304 | tf_op jit(solution)/shard_map/all_to_all | solution.py:106
  69.1 3.6 reshape.207
  72.7 45.9 %all-to-all-done.2 = bf16[32,12,2048]{2,1,0:T(8,128)(2,1)S(1)} async-done(((bf16[32,12,2048]{2,1,0:T(8,128)(2,1)}), bf16[32,12,2048]{2,1,0:T(8,128)(2,1)S(1)}, u32[]{:S(2)}, u32[]{:S(2)}) %all-to-all-start.2) | async-done | bytes 1572896 | tf_op jit(solution)/shard_map/all_to_all | solution.py:106
  119.9 5.8 %all-to-all-start = ((bf16[32,12,2048]{2,1,0:T(8,128)(2,1)}), bf16[32,12,2048]{2,1,0:T(8,128)(2,1)S(1)}, u32[]{:S(2)}, u32[]{:S(2)}) async-start(bf16[32,12,2048]{2,1,0:T(8,128)(2,1)} %reshape.207), calls=%async_computation | async-start | bytes 4194304 | tf_op jit(solution)/shard_map/all_to_all | solution.py:106
  127.9 3.3 fusion.69
  134.6 42.0 %all-to-all-done = bf16[32,12,2048]{2,1,0:T(8,128)(2,1)S(1)} async-done(((bf16[32,12,2048]{2,1,0:T(8,128)(2,1)}), bf16[32,12,2048]{2,1,0:T(8,128)(2,1)S(1)}, u32[]{:S(2)}, u32[]{:S(2)}) %all-to-all-start) | async-done | bytes 1572896 | tf_op jit(solution)/shard_map/all_to_all | solution.py:106
  180.6 5.3 %multiply_convert_fusion.2 = (bf16[192,1408]{1,0:T(8,128)(2,1)}, f32[192,1408]{1,0:T(8,128)}) fusion(bf16[192,2048]{1,0:T(8,128)(2,1)S(1)} %reshape.208, bf16[1,2048,1408]{2,1,0:T(8,128)(2,1)} %all-gather.5.cloned.1.call-done), kind=kOutput, calls=%fused_computation.44 | convolution fusion | flops 1108647936 | bytes 8175616 | tf_op jit(solution)/shard_map/dot_general | solution.py:137
  185.9 17.4 %collective-permute-done.2 = bf16[2,256,1408]{2,1,0:T(8,128)(2,1)} collective-permute-done((bf16[2,256,1408]{2,1,0:T(8,128)(2,1)}, bf16[2,256,1408]{2,1,0:T(8,128)(2,1)}, u32[]{:S(2)}, u32[]{:S(2)}) %collective-permute-start.2) | collective-permute-done | bytes 1441824 | tf_op jit(solution)/shard_map/ppermute | solution.py:18
  203.3 4.1 fusion.2
  209.2 4.2 add_convert_fusion
  213.7 5.1 %fusion.8 = bf16[192,1408]{1,0:T(8,128)(2,1)S(1)} fusion(bf16[192,2048]{1,0:T(8,128)(2,1)S(1)} %copy-done.6, bf16[1408,2048]{1,0:T(8,128)(2,1)} %bitcast.119, f32[192,1408]{1,0:T(8,128)} %get-tuple-element.55), kind=kOutput, calls=%fused_computation.16 | convolution fusion | flops 1109729280 | bytes 8175616 | tf_op jit(solution)/shard_map/dot_general | solution.py:50
  223.7 4.3 add_convert_fusion.1
  229.1 4.8 %fusion.10 = bf16[192,2048]{1,0:T(8,128)(2,1)S(1)} fusion(bf16[192,1408]{1,0:T(8,128)(2,1)S(1)} %copy-done.14, bf16[1,2048,1408]{2,1,0:T(8,128)(2,1)} %all-gather.5.cloned.1.call-done), kind=kOutput, calls=%fused_computation.18 | convolution fusion | flops 1107689472 | bytes 7094272 | tf_op jit(solution)/shard_map/dot_general | solution.py:50
  234.2 5.3 %convolution_convert_fusion.1 = bf16[192,2048]{1,0:T(8,128)(2,1)} fusion(bf16[192,1408]{1,0:T(8,128)(2,1)} %get-tuple-element.28, bf16[1408,2048]{1,0:T(8,128)(2,1)} %bitcast.120), kind=kOutput, calls=%fused_computation.21 | convolution fusion | flops 1107689472 | bytes 7094272 | tf_op jit(solution)/shard_map/dot_general | solution.py:144
  242.9 8.5 %all-to-all-start.1 = ((bf16[32,12,2048]{2,1,0:T(8,128)(2,1)}), bf16[32,12,2048]{2,1,0:T(8,128)(2,1)S(1)}, u32[]{:S(2)}, u32[]{:S(2)}) async-start(bf16[32,12,2048]{2,1,0:T(8,128)(2,1)} %pad_maximum_fusion), calls=%async_computation.1 | async-start | bytes 4194304 | tf_op jit(solution)/shard_map/all_to_all | solution.py:153
  253.6 5.1 %convolution_convert_fusion = bf16[192,2048]{1,0:T(8,128)(2,1)} fusion(bf16[1408,2048]{1,0:T(8,128)(2,1)} %bitcast.121, f32[192,1408]{1,0:T(8,128)S(1)} %copy-done.12), kind=kOutput, calls=%fused_computation.20 | convolution fusion | flops 1109041152 | bytes 7634944 | tf_op jit(solution)/shard_map/dot_general | solution.py:144
  260.0 5.8 %fusion.13 = bf16[192,2048]{1,0:T(8,128)(2,1)} fusion(bf16[192,1408]{1,0:T(8,128)(2,1)} %copy-done.16, bf16[1,2048,1408]{2,1,0:T(8,128)(2,1)} %all-gather.5.cloned.1.call-done), kind=kOutput, calls=%fused_computation.19 | convolution fusion | flops 1107689472 | bytes 7094272 | tf_op jit(solution)/shard_map/dot_general | solution.py:50
  265.7 63.5 %collective-permute-done.3 = bf16[2,176,2048]{2,1,0:T(8,128)(2,1)} collective-permute-done((bf16[2,176,2048]{2,1,0:T(8,128)(2,1)}, bf16[2,176,2048]{2,1,0:T(8,128)(2,1)}, u32[]{:S(2)}, u32[]{:S(2)}) %collective-permute-start.3) | collective-permute-done | bytes 1441824 | tf_op jit(solution)/shard_map/ppermute | solution.py:18
  331.4 3.3 pad_maximum_fusion.1
  334.7 8.8 %all-to-all-start.3 = ((bf16[32,12,2048]{2,1,0:T(8,128)(2,1)}), bf16[32,12,2048]{2,1,0:T(8,128)(2,1)}, u32[]{:S(2)}, u32[]{:S(2)}) async-start(bf16[32,12,2048]{2,1,0:T(8,128)(2,1)} %pad_maximum_fusion.1), calls=%async_computation.3 | async-start | bytes 4194304 | tf_op jit(solution)/shard_map/all_to_all | solution.py:153
  349.6 44.0 %all-to-all-done.3 = bf16[32,12,2048]{2,1,0:T(8,128)(2,1)} async-done(((bf16[32,12,2048]{2,1,0:T(8,128)(2,1)}), bf16[32,12,2048]{2,1,0:T(8,128)(2,1)}, u32[]{:S(2)}, u32[]{:S(2)}) %all-to-all-start.3) | async-done | bytes 1572896 | tf_op jit(solution)/shard_map/all_to_all | solution.py:153
  393.6 3.6 reshape.218
  397.3 4.4 %convolution_add_fusion.1 = f32[288,2048]{1,0:T(8,128)} fusion(f32[288,2048]{1,0:T(8,128)} %fusion.40, bf16[384,2048]{1,0:T(8,128)(2,1)} %reshape.218, s32[384]{0:T(512)S(1)} %slice.58, s32[288]{0:T(512)S(1)} %get-tuple-element.35), kind=kOutput, calls=%fused_computation.13 | convolution fusion | flops 453685248 | bytes 6294144 | tf_op jit(solution)/shard_map/dot_general | solution.py:173
  401.7 3.5 reshape.219
  405.2 3.7 convolution_add_fusion
  408.9 3.5 reshape.220
  412.4 3.7 reduce_sum.85
  418.0 4.8 %fusion.29 = (bf16[1,176,2048]{2,1,0:T(8,128)(2,1)}, bf16[1,176,2048]{2,1,0:T(8,128)(2,1)}, bf16[1,176,2048]{2,1,0:T(8,128)(2,1)}) fusion(bf16[176,2048]{1,0:T(8,128)(2,1)} %reduce-scatter.5.cloned.1.call-done, bf16[1,176,2048]{2,1,0:T(8,128)(2,1)} %param.21, bf16[2,176,2048]{2,1,0:T(8,128)(2,1)} %collective-permute-done.3, pred[]{:T(512)} %bitcast.2, ...), kind=kLoop, calls=%fused_computation.52 | loop fusion | flops 7569408 | bytes 6488065 | tf_op jit(solution)/shard_map/broadcast_in_dim | solution.py:214
  422.8 4.5 %fusion.28 = (bf16[1,256,1408]{2,1,0:T(8,128)(2,1)}, bf16[1,256,1408]{2,1,0:T(8,128)(2,1)}, bf16[1,256,1408]{2,1,0:T(8,128)(2,1)}) fusion(bf16[256,1408]{1,0:T(8,128)(2,1)} %reduce-scatter.3.cloned.1.call-done, bf16[1,256,1408]{2,1,0:T(8,128)(2,1)S(1)} %copy-done.8, bf16[2,256,1408]{2,1,0:T(8,128)(2,1)} %collective-permute-done.2, pred[]{:T(512)} %bitcast.2, ...), kind=kLoop, calls=%fused_computation.51 | loop fusion | flops 7569408 | bytes 6488065 | tf_op jit(solution)/shard_map/broadcast_in_dim | solution.py:212
  (123 shorter events, 55.6 us)
Async XLA Ops:
  7.2 5.8 %copy-start.17 = (bf16[48,2048]{1,0:T(8,128)(2,1)S(1)}, bf16[48,2048]{1,0:T(8,128)(2,1)}, u32[]{:S(2)}) copy-start(bf16[48,2048]{1,0:T(8,128)(2,1)} %param.14) | copy-start | bytes 589828
  7.2 5.8 %copy-start.18 = (bf16[48,2048]{1,0:T(8,128)(2,1)S(1)}, bf16[48,2048]{1,0:T(8,128)(2,1)}, u32[]{:S(2)}) copy-start(bf16[48,2048]{1,0:T(8,128)(2,1)} %param.11) | copy-start | bytes 589828
  7.2 173.5 %all-gather.5.cloned.1.call-start = ((), (), s32[]{:S(2)}) async-start(), calls=%async_computation.7 | async-start | bytes 6488064 | tf_op jit(solution)/shard_map/all_gather | solution.py:128
  13.0 3.1 copy-start.20
  14.0 19.4 %collective-permute-start = (bf16[1,256,1408]{2,1,0:T(8,128)(2,1)}, bf16[1,256,1408]{2,1,0:T(8,128)(2,1)}, u32[]{:S(2)}, u32[]{:S(2)}) collective-permute-start(bf16[1,256,1408]{2,1,0:T(8,128)(2,1)} %param.16), channel_id=1, source_target_pairs={{0,1},{1,0},{2,3},{3,2},{4,5},{5,4},{6,7},{7,6},{8,9},{9,8},{10,11... | collective-permute-start | bytes 2162696 | tf_op jit(solution)/shard_map/ppermute | solution.py:18
  16.0 31.9 %collective-permute-start.1 = (bf16[1,176,2048]{2,1,0:T(8,128)(2,1)}, bf16[1,176,2048]{2,1,0:T(8,128)(2,1)}, u32[]{:S(2)}, u32[]{:S(2)}) collective-permute-start(bf16[1,176,2048]{2,1,0:T(8,128)(2,1)} %param.17), channel_id=1, source_target_pairs={{0,1},{1,0},{2,3},{3,2},{4,5},{5,4},{6,7},{7,6},{8,9},{9,8},{10,11... | collective-permute-start | bytes 2162696 | tf_op jit(solution)/shard_map/ppermute | solution.py:18
  17.4 2.7 copy-start.7
  17.4 2.7 copy-start.9
  50.0 153.3 %all-gather.3.cloned.1.call-start = ((), (), s32[]{:S(2)}) async-start(), calls=%async_computation.6 | async-start | bytes 6488064 | tf_op jit(solution)/shard_map/all_gather | solution.py:129
  57.7 60.8 %all-to-all-start.2 = ((bf16[32,12,2048]{2,1,0:T(8,128)(2,1)}), bf16[32,12,2048]{2,1,0:T(8,128)(2,1)S(1)}, u32[]{:S(2)}, u32[]{:S(2)}) async-start(bf16[32,12,2048]{2,1,0:T(8,128)(2,1)} %reshape.213), calls=%async_computation.2 | async-start | bytes 4194304 | tf_op jit(solution)/shard_map/all_to_all | solution.py:106
  119.9 56.6 %all-to-all-start = ((bf16[32,12,2048]{2,1,0:T(8,128)(2,1)}), bf16[32,12,2048]{2,1,0:T(8,128)(2,1)S(1)}, u32[]{:S(2)}, u32[]{:S(2)}) async-start(bf16[32,12,2048]{2,1,0:T(8,128)(2,1)} %reshape.207), calls=%async_computation | async-start | bytes 4194304 | tf_op jit(solution)/shard_map/all_to_all | solution.py:106
  125.8 292.2 %reduce-scatter.5.cloned.1.call-start = ((), (), s32[]{:S(2)}) async-start(), calls=%async_computation.9 | async-start | bytes 6488064 | tf_op jit(solution)/shard_map/reduce_scatter | solution.py:197
  125.8 77.5 %collective-permute-start.2 = (bf16[2,256,1408]{2,1,0:T(8,128)(2,1)}, bf16[2,256,1408]{2,1,0:T(8,128)(2,1)}, u32[]{:S(2)}, u32[]{:S(2)}) collective-permute-start(bf16[2,256,1408]{2,1,0:T(8,128)(2,1)} %pad_maximum_fusion.2), channel_id=1, source_target_pairs={{0,1},{1,0},{2,3},{3,2},{4,5},{5,4},{6,7},{7,6},{8,9},{9,8},{10,11... | collective-permute-start | bytes 4325384 | tf_op jit(solution)/shard_map/ppermute | solution.py:18
  180.6 22.6 %copy-start.5 = (bf16[192,2048]{1,0:T(8,128)(2,1)S(1)}, bf16[192,2048]{1,0:T(8,128)(2,1)}, u32[]{:S(2)}) copy-start(bf16[192,2048]{1,0:T(8,128)(2,1)} %reshape.214) | copy-start | bytes 2359300
  203.3 4.1 copy-start.4
  207.4 1.8 copy-start.11
  207.4 1.8 copy-start.6
  207.4 1.8 copy-start.15
  213.5 209.3 %reduce-scatter.3.cloned.1.call-start = ((), (), s32[]{:S(2)}) async-start(), calls=%async_computation.8 | async-start | bytes 6488064 | tf_op jit(solution)/shard_map/reduce_scatter | solution.py:194
  213.7 7.0 %slice-start = ((s8[5767168]{0:T(1024)(128)(4,1)}), s8[4194304]{0:T(1024)(128)(4,1)S(1)}, s32[]{:S(2)}) async-start(s8[5767168]{0:T(1024)(128)(4,1)} %bitcast.122), calls=%async_computation.10 | async-start | bytes 8388608
  218.9 1.9 copy-start.13
  218.9 1.9 copy-start.12
  218.9 1.9 slice-start.1
  242.9 91.8 %all-to-all-start.1 = ((bf16[32,12,2048]{2,1,0:T(8,128)(2,1)}), bf16[32,12,2048]{2,1,0:T(8,128)(2,1)S(1)}, u32[]{:S(2)}, u32[]{:S(2)}) async-start(bf16[32,12,2048]{2,1,0:T(8,128)(2,1)} %pad_maximum_fusion), calls=%async_computation.1 | async-start | bytes 4194304 | tf_op jit(solution)/shard_map/all_to_all | solution.py:153
  251.4 77.8 %collective-permute-start.3 = (bf16[2,176,2048]{2,1,0:T(8,128)(2,1)}, bf16[2,176,2048]{2,1,0:T(8,128)(2,1)}, u32[]{:S(2)}, u32[]{:S(2)}) collective-permute-start(bf16[2,176,2048]{2,1,0:T(8,128)(2,1)} %pad_maximum_fusion.3), channel_id=1, source_target_pairs={{0,1},{1,0},{2,3},{3,2},{4,5},{5,4},{6,7},{7,6},{8,9},{9,8},{10,11... | collective-permute-start | bytes 4325384 | tf_op jit(solution)/shard_map/ppermute | solution.py:18
  334.7 8.8 %copy-start.19 = (f32[48,6]{0,1:T(8,128)S(1)}, f32[48,6]{0,1:T(8,128)}, u32[]{:S(2)}) copy-start(f32[48,6]{0,1:T(8,128)} %param.13) | copy-start | bytes 3460
  334.7 58.9 %all-to-all-start.3 = ((bf16[32,12,2048]{2,1,0:T(8,128)(2,1)}), bf16[32,12,2048]{2,1,0:T(8,128)(2,1)}, u32[]{:S(2)}, u32[]{:S(2)}) async-start(bf16[32,12,2048]{2,1,0:T(8,128)(2,1)} %pad_maximum_fusion.1), calls=%async_computation.3 | async-start | bytes 4194304 | tf_op jit(solution)/shard_map/all_to_all | solution.py:153
  345.0 2.4 copy-start
  412.4 3.7 copy-start.1
  418.0 4.8 %copy-start.3 = (bf16[1,256,1408]{2,1,0:T(8,128)(2,1)S(1)}, bf16[1,256,1408]{2,1,0:T(8,128)(2,1)}, u32[]{:S(2)}) copy-start(bf16[1,256,1408]{2,1,0:T(8,128)(2,1)} %broadcast_select_fusion) | copy-start | bytes 2162692
  418.0 4.8 %copy-start.8 = (bf16[1,256,1408]{2,1,0:T(8,128)(2,1)S(1)}, bf16[1,256,1408]{2,1,0:T(8,128)(2,1)}, u32[]{:S(2)}) copy-start(bf16[1,256,1408]{2,1,0:T(8,128)(2,1)} %param.19) | copy-start | bytes 2162692
  418.0 4.8 %copy-start.10 = (bf16[1,256,1408]{2,1,0:T(8,128)(2,1)S(1)}, bf16[1,256,1408]{2,1,0:T(8,128)(2,1)}, u32[]{:S(2)}) copy-start(bf16[1,256,1408]{2,1,0:T(8,128)(2,1)} %param.18) | copy-start | bytes 2162692
  (3 other events, 3.3 us)
Sparse Core Ops, SparseCore 0:
  50.1 42.1 all-gather.4
  94.7 41.3 all-gather.2
  213.6 40.7 reduce-scatter.4
  256.8 43.4 reduce-scatter.2

commit v5 on v3

--- a/solution.py
+++ b/solution.py
@@ -100,23 +100,23 @@
         preferred_element_type=jnp.float32,
     )
     send_both = (row_scale[:, None] * picked_rows).astype(jnp.bfloat16)
-    w_up, w_down, send_both = lax.optimization_barrier((w_up, w_down, send_both))
     w_up_in = partner(w_up, "expert", 0)
     w_down_in = partner(w_down, "expert", 0)
+    w_up_in, w_down_in, send_both, up_local, down_local = lax.optimization_barrier(
+        (
+            w_up_in,
+            w_down_in,
+            send_both,
+            jnp.concatenate([m_up, v_up], axis=0),
+            jnp.concatenate([m_down, v_down], axis=0),
+        )
+    )
     got_both = lax.all_to_all(
         send_both.reshape(experts, 2 * capacity, model_width),
         "expert",
         split_axis=0,
         concat_axis=0,
         tiled=True,
-    )
-    w_up_in, w_down_in, up_local, down_local = lax.optimization_barrier(
-        (
-            w_up_in,
-            w_down_in,
-            jnp.concatenate([m_up, v_up], axis=0),
-            jnp.concatenate([m_down, v_down], axis=0),
-        )
     )
     up_moments = partner(up_local, "expert", 0)
     w_up_use = jnp.where(swapped, w_up_in, w_up)

time: 325 us -> 314 us (0.966)
  waiting for transfers between devices: 126 us -> 117 us
    ppermute x4, waiting for transfers between devices: 54.4 us -> 44.7 us  [partner(): return lax.ppermute(value, axis, pairs)]
  transfers between devices with their start and end apart: 9 -> 9, of which waited for: 5 -> 5; matrix products, arithmetic and copies ran while one was open for 20% -> 23% of each run, Pallas kernels for 0% -> 0%
where the time goes in v5:
time: 314 us; the launch traced here: 313 us
  waiting for transfers between devices  117 us (37%)
  blocking collectives  82.6 us (26%)
  matrix products  44.6 us (14%)
  other arithmetic  20.3 us (6%)
  local copies, waits for them, and re-layouts  18.1 us (6%)
  starting transfers between devices  16.1 us (5%)
  between operations  14.6 us (5%)
    all_to_all x1, blocking collectives, body(): lax.all_to_all(jnp.concatenate([expert_out.reshape(experts, capacity, mod...  82.6 us
    all_to_all x1, waiting for transfers between devices, body(): lax.all_to_all(send_both.reshape(experts, 2 * capacity, model_width), 'ex...  71.8 us
    ppermute x4, waiting for transfers between devices, partner(): return lax.ppermute(value, axis, pairs)  44.7 us
    dot_general x2, matrix products, contract_cols(): lax.dot_general(left, right, (((1,), (1,)), ((), ())), preferred_element_...  14.2 us
    all_to_all x1, starting transfers between devices, body(): lax.all_to_all(send_both.reshape(experts, 2 * capacity, model_width), 'ex...  11.3 us
    dot_general x2, matrix products, contract_rows(): lax.dot_general(left, right, (((0,), (0,)), ((), ())), preferred_element_...  10.2 us
    dot_general x1, matrix products, body(): up_act = jnp.dot(expert_rows, up_full, preferred_element_type=jnp.float32)  7.3 us
    dot_general x1, matrix products, body(): jnp.dot(hidden, down_full, preferred_element_type=jnp.float32)  6.44 us
  transfers between devices with their start and end apart: 9, of which 5 were waited for; matrix products, arithmetic and copies ran while one was open for 23% of the time, Pallas kernels for 0%

profile of v5, /device:TPU:6, one launch (start us, length us, event | category | flops | bytes accessed | tf_op | source)
XLA Modules:
  0.0 312.8 jit_solution(13721611434572264463)
XLA Ops:
  7.2 2.0 collective-permute-start
  10.0 1.2 dynamic_slice.3
  14.6 1.0 select_reduce_fusion
  16.3 2.3 pad_maximum_fusion.2
  18.7 1.3 pad_maximum_fusion.1
  20.0 2.7 multiply_convert_fusion
  22.7 3.8 %collective-permute-done = bf16[1,256,1408]{2,1,0:T(8,128)(2,1)S(1)} collective-permute-done((bf16[1,256,1408]{2,1,0:T(8,128)(2,1)}, bf16[1,256,1408]{2,1,0:T(8,128)(2,1)S(1)}, u32[]{:S(2)}, u32[]{:S(2)}) %collective-permute-start) | collective-permute-done | bytes 720928 | tf_op jit(solution)/shard_map/ppermute | solution.py:18
  26.5 14.5 %collective-permute-done.1 = bf16[1,176,2048]{2,1,0:T(8,128)(2,1)S(1)} collective-permute-done((bf16[1,176,2048]{2,1,0:T(8,128)(2,1)}, bf16[1,176,2048]{2,1,0:T(8,128)(2,1)S(1)}, u32[]{:S(2)}, u32[]{:S(2)}) %collective-permute-start.1) | collective-permute-done | bytes 720928 | tf_op jit(solution)/shard_map/ppermute | solution.py:18
  41.0 1.0 broadcast_select_fusion
  42.1 0.9 broadcast_select_fusion.1
  43.0 11.3 %all-to-all-start = ((bf16[32,24,2048]{2,1,0:T(8,128)(2,1)}), bf16[32,24,2048]{2,1,0:T(8,128)(2,1)S(1)}, u32[]{:S(2)}, u32[]{:S(2)}) async-start(bf16[32,24,2048]{2,1,0:T(8,128)(2,1)} %bitcast.112), calls=%async_computation | async-start | bytes 6291456 | tf_op jit(solution)/shard_map/all_to_all | solution.py:114
  54.4 1.9 collective-permute-start.2
  56.3 71.8 %all-to-all-done = bf16[32,24,2048]{2,1,0:T(8,128)(2,1)S(1)} async-done(((bf16[32,24,2048]{2,1,0:T(8,128)(2,1)}), bf16[32,24,2048]{2,1,0:T(8,128)(2,1)S(1)}, u32[]{:S(2)}, u32[]{:S(2)}) %all-to-all-start) | async-done | bytes 3145760 | tf_op jit(solution)/shard_map/all_to_all | solution.py:114
  128.1 2.9 fusion.44
  131.0 3.7 %reshape.201 = bf16[384,2048]{1,0:T(8,128)(2,1)} reshape(bf16[32,12,2048]{2,1,0:T(8,128)(2,1)} %get-tuple-element.30) | data formatting | bytes 3145728 | tf_op jit(solution)/shard_map/reshape | solution.py:126
  134.8 1.4 reshape.203
  136.1 7.3 %multiply_convert_fusion.1 = (bf16[384,1408]{1,0:T(8,128)(2,1)S(1)}, f32[384,1408]{1,0:T(8,128)}) fusion(bf16[384,2048]{1,0:T(8,128)(2,1)} %reshape.201, bf16[1,2048,1408]{2,1,0:T(8,128)(2,1)} %all-gather.5.cloned.1.call-done), kind=kOutput, calls=%fused_computation.13 | convolution fusion | flops 2217295872 | bytes 10584064 | tf_op jit(solution)/shard_map/dot_general | solution.py:128
  143.4 10.5 %collective-permute-done.2 = bf16[2,256,1408]{2,1,0:T(8,128)(2,1)} collective-permute-done((bf16[2,256,1408]{2,1,0:T(8,128)(2,1)}, bf16[2,256,1408]{2,1,0:T(8,128)(2,1)}, u32[]{:S(2)}, u32[]{:S(2)}) %collective-permute-start.2) | collective-permute-done | bytes 1441824 | tf_op jit(solution)/shard_map/ppermute | solution.py:18
  154.0 5.0 %convolution_convert_fusion = bf16[1408,2048]{1,0:T(8,128)(2,1)} fusion(bf16[384,1408]{1,0:T(8,128)(2,1)S(1)} %get-tuple-element.24, bf16[384,2048]{1,0:T(8,128)(2,1)S(1)} %copy-done.9), kind=kOutput, calls=%fused_computation | convolution fusion | flops 2217476096 | bytes 8421376 | tf_op jit(solution)/shard_map/dot_general | solution.py:44
  159.2 7.2 %fusion.4 = bf16[384,1408]{1,0:T(8,128)(2,1)S(1)} fusion(bf16[384,2048]{1,0:T(8,128)(2,1)S(1)} %copy-done.9, bf16[1408,2048]{1,0:T(8,128)(2,1)} %bitcast.116, f32[384,1408]{1,0:T(8,128)} %get-tuple-element.39), kind=kOutput, calls=%fused_computation.9 | convolution fusion | flops 2219458560 | bytes 10584064 | tf_op jit(solution)/shard_map/dot_general | solution.py:50
  166.5 5.2 %convolution_convert_fusion.1 = bf16[2048,1408]{1,0:T(8,128)(2,1)} fusion(bf16[384,2048]{1,0:T(8,128)(2,1)S(1)} %copy-done.8, bf16[384,1408]{1,0:T(8,128)(2,1)S(1)} %fusion.4), kind=kOutput, calls=%fused_computation.1 | convolution fusion | flops 2217476096 | bytes 8421376 | tf_op jit(solution)/shard_map/dot_general | solution.py:44
  172.9 6.4 %convolution_convert_fusion.2 = bf16[384,2048]{1,0:T(8,128)(2,1)} fusion(bf16[384,1408]{1,0:T(8,128)(2,1)S(1)} %copy-done.17, bf16[1408,2048]{1,0:T(8,128)(2,1)} %bitcast.117), kind=kOutput, calls=%fused_computation.11 | convolution fusion | flops 2215378944 | bytes 8421376 | tf_op jit(solution)/shard_map/dot_general | solution.py:134
  179.3 2.4 reshape.202
  181.8 6.9 %fusion.5 = bf16[384,2048]{1,0:T(8,128)(2,1)} fusion(bf16[384,1408]{1,0:T(8,128)(2,1)} %copy-done.18, bf16[1,2048,1408]{2,1,0:T(8,128)(2,1)} %all-gather.5.cloned.1.call-done), kind=kOutput, calls=%fused_computation.10 | convolution fusion | flops 2215378944 | bytes 8421376 | tf_op jit(solution)/shard_map/dot_general | solution.py:50
  188.7 15.8 %collective-permute-done.3 = bf16[2,176,2048]{2,1,0:T(8,128)(2,1)S(1)} collective-permute-done((bf16[2,176,2048]{2,1,0:T(8,128)(2,1)}, bf16[2,176,2048]{2,1,0:T(8,128)(2,1)S(1)}, u32[]{:S(2)}, u32[]{:S(2)}) %collective-permute-start.3) | collective-permute-done | bytes 1441824 | tf_op jit(solution)/shard_map/ppermute | solution.py:18
  204.5 3.9 %reshape.204 = bf16[32,12,2048]{2,1,0:T(8,128)(2,1)} reshape(bf16[384,2048]{1,0:T(8,128)(2,1)} %fusion.5) | data formatting | bytes 3145728 | tf_op jit(solution)/shard_map/reshape | solution.py:143
  208.5 2.5 pad_maximum_fusion
  211.0 82.6 %all_to_all.10 = bf16[32,24,2048]{2,1,0:T(8,128)(2,1)S(1)} all-to-all(bf16[32,24,2048]{2,1,0:T(8,128)(2,1)S(1)} %pad_maximum_fusion), channel_id=1, replica_groups=mesh['dp'=8,'expert'=32] {'expert'}, dimensions={0} | all-to-all | bytes 6291456 | tf_op jit(solution)/shard_map/all_to_all | solution.py:139
  293.6 1.8 convolution_reduce_fusion
  295.4 1.9 fusion.8
  297.3 4.5 %fusion.26 = (bf16[1,176,2048]{2,1,0:T(8,128)(2,1)}, bf16[1,176,2048]{2,1,0:T(8,128)(2,1)}, bf16[1,176,2048]{2,1,0:T(8,128)(2,1)}) fusion(bf16[176,2048]{1,0:T(8,128)(2,1)} %reduce-scatter.5.cloned.1.call-done, bf16[1,176,2048]{2,1,0:T(8,128)(2,1)S(1)} %copy-done.4, bf16[2,176,2048]{2,1,0:T(8,128)(2,1)} %copy-done.10, pred[]{:T(512)} %bitcast.3, ...), kind=kLoop, calls=%fused_computation.45 | loop fusion | flops 7569408 | bytes 6488065 | tf_op jit(solution)/shard_map/broadcast_in_dim | solution.py:193
  301.8 4.5 %fusion.25 = (bf16[1,256,1408]{2,1,0:T(8,128)(2,1)}, bf16[1,256,1408]{2,1,0:T(8,128)(2,1)}, bf16[1,256,1408]{2,1,0:T(8,128)(2,1)}) fusion(bf16[256,1408]{1,0:T(8,128)(2,1)} %reduce-scatter.3.cloned.1.call-done, bf16[1,256,1408]{2,1,0:T(8,128)(2,1)} %param.19, bf16[2,256,1408]{2,1,0:T(8,128)(2,1)} %collective-permute-done.2, pred[]{:T(512)} %bitcast.3, ...), kind=kLoop, calls=%fused_computation.44 | loop fusion | flops 7569408 | bytes 6488065 | tf_op jit(solution)/shard_map/broadcast_in_dim | solution.py:191
  (75 shorter events, 5.8 us)
Async XLA Ops:
  7.2 9.2 %copy-start.3 = (bf16[1,176,2048]{2,1,0:T(8,128)(2,1)S(1)}, bf16[1,176,2048]{2,1,0:T(8,128)(2,1)}, u32[]{:S(2)}) copy-start(bf16[1,176,2048]{2,1,0:T(8,128)(2,1)} %param.21) | copy-start | bytes 2162692
  7.2 129.0 %all-gather.5.cloned.1.call-start = ((), (), s32[]{:S(2)}) async-start(), calls=%async_computation.5 | async-start | bytes 6488064 | tf_op jit(solution)/shard_map/all_gather | solution.py:124
  7.2 19.3 %collective-permute-start = (bf16[1,256,1408]{2,1,0:T(8,128)(2,1)}, bf16[1,256,1408]{2,1,0:T(8,128)(2,1)S(1)}, u32[]{:S(2)}, u32[]{:S(2)}) collective-permute-start(bf16[1,256,1408]{2,1,0:T(8,128)(2,1)} %param.16), channel_id=1, source_target_pairs={{0,1},{1,0},{2,3},{3,2},{4,5},{5,4},{6,7},{7,6},{8,9},{9,8},{10,11... | collective-permute-start | bytes 2162696 | tf_op jit(solution)/shard_map/ppermute | solution.py:18
  9.2 31.8 %collective-permute-start.1 = (bf16[1,176,2048]{2,1,0:T(8,128)(2,1)}, bf16[1,176,2048]{2,1,0:T(8,128)(2,1)S(1)}, u32[]{:S(2)}, u32[]{:S(2)}) collective-permute-start(bf16[1,176,2048]{2,1,0:T(8,128)(2,1)} %param.17), channel_id=1, source_target_pairs={{0,1},{1,0},{2,3},{3,2},{4,5},{5,4},{6,7},{7,6},{8,9},{9,8},{10,11... | collective-permute-start | bytes 2162696 | tf_op jit(solution)/shard_map/ppermute | solution.py:18
  14.3 4.3 %copy-start.6 = (bf16[1,256,1408]{2,1,0:T(8,128)(2,1)S(1)}, bf16[1,256,1408]{2,1,0:T(8,128)(2,1)}, u32[]{:S(2)}) copy-start(bf16[1,256,1408]{2,1,0:T(8,128)(2,1)} %param.19) | copy-start | bytes 2162692
  14.3 4.3 %copy-start.7 = (bf16[1,256,1408]{2,1,0:T(8,128)(2,1)S(1)}, bf16[1,256,1408]{2,1,0:T(8,128)(2,1)}, u32[]{:S(2)}) copy-start(bf16[1,256,1408]{2,1,0:T(8,128)(2,1)} %param.18) | copy-start | bytes 2162692
  18.7 1.3 copy-start.13
  18.7 1.3 copy-start.14
  20.0 21.1 %copy-start.11 = (bf16[1,256,1408]{2,1,0:T(8,128)(2,1)S(1)}, bf16[1,256,1408]{2,1,0:T(8,128)(2,1)}, u32[]{:S(2)}) copy-start(bf16[1,256,1408]{2,1,0:T(8,128)(2,1)} %param.16) | copy-start | bytes 2162692
  22.7 19.4 %copy-start.12 = (bf16[1,176,2048]{2,1,0:T(8,128)(2,1)S(1)}, bf16[1,176,2048]{2,1,0:T(8,128)(2,1)}, u32[]{:S(2)}) copy-start(bf16[1,176,2048]{2,1,0:T(8,128)(2,1)} %param.17) | copy-start | bytes 2162692
  42.0 111.9 %all-gather.3.cloned.1.call-start = ((), (), s32[]{:S(2)}) async-start(), calls=%async_computation.4 | async-start | bytes 6488064 | tf_op jit(solution)/shard_map/all_gather | solution.py:125
  43.0 85.0 %all-to-all-start = ((bf16[32,24,2048]{2,1,0:T(8,128)(2,1)}), bf16[32,24,2048]{2,1,0:T(8,128)(2,1)S(1)}, u32[]{:S(2)}, u32[]{:S(2)}) async-start(bf16[32,24,2048]{2,1,0:T(8,128)(2,1)} %bitcast.112), calls=%async_computation | async-start | bytes 6291456 | tf_op jit(solution)/shard_map/all_to_all | solution.py:114
  54.4 242.9 %reduce-scatter.5.cloned.1.call-start = ((), (), s32[]{:S(2)}) async-start(), calls=%async_computation.7 | async-start | bytes 6488064 | tf_op jit(solution)/shard_map/reduce_scatter | solution.py:173
  54.4 99.5 %collective-permute-start.2 = (bf16[2,256,1408]{2,1,0:T(8,128)(2,1)}, bf16[2,256,1408]{2,1,0:T(8,128)(2,1)}, u32[]{:S(2)}, u32[]{:S(2)}) collective-permute-start(bf16[2,256,1408]{2,1,0:T(8,128)(2,1)} %pad_maximum_fusion.1), channel_id=1, source_target_pairs={{0,1},{1,0},{2,3},{3,2},{4,5},{5,4},{6,7},{7,6},{8,9},{9,8},{10,11... | collective-permute-start | bytes 4325384 | tf_op jit(solution)/shard_map/ppermute | solution.py:18
  131.0 3.8 %copy-start = (bf16[32,12,2048]{2,1,0:T(8,128)(2,1)S(1)}, bf16[32,12,2048]{2,1,0:T(8,128)(2,1)}, u32[]{:S(2)}) copy-start(bf16[32,12,2048]{2,1,0:T(8,128)(2,1)} %get-tuple-element.31) | copy-start | bytes 4718596
  136.1 17.8 %copy-start.9 = (bf16[384,2048]{1,0:T(8,128)(2,1)S(1)}, bf16[384,2048]{1,0:T(8,128)(2,1)}, u32[]{:S(2)}) copy-start(bf16[384,2048]{1,0:T(8,128)(2,1)} %reshape.203) | copy-start | bytes 4718596
  143.4 15.5 %copy-start.16 = (bf16[384,1408]{1,0:T(8,128)(2,1)}, bf16[384,1408]{1,0:T(8,128)(2,1)S(1)}, u32[]{:S(2)}) copy-start(bf16[384,1408]{1,0:T(8,128)(2,1)S(1)} %get-tuple-element.24) | copy-start | bytes 3244036
  159.0 142.8 %reduce-scatter.3.cloned.1.call-start = ((), (), s32[]{:S(2)}) async-start(), calls=%async_computation.6 | async-start | bytes 6488064 | tf_op jit(solution)/shard_map/reduce_scatter | solution.py:167
  159.2 7.3 %copy-start.8 = (bf16[384,2048]{1,0:T(8,128)(2,1)S(1)}, bf16[384,2048]{1,0:T(8,128)(2,1)}, u32[]{:S(2)}) copy-start(bf16[384,2048]{1,0:T(8,128)(2,1)} %reshape.201) | copy-start | bytes 4718596
  166.5 5.2 %copy-start.18 = (bf16[384,1408]{1,0:T(8,128)(2,1)}, bf16[384,1408]{1,0:T(8,128)(2,1)S(1)}, u32[]{:S(2)}) copy-start(bf16[384,1408]{1,0:T(8,128)(2,1)S(1)} %fusion.4) | copy-start | bytes 3244036
  171.7 1.2 copy-start.17
  171.7 32.8 %collective-permute-start.3 = (bf16[2,176,2048]{2,1,0:T(8,128)(2,1)}, bf16[2,176,2048]{2,1,0:T(8,128)(2,1)S(1)}, u32[]{:S(2)}, u32[]{:S(2)}) collective-permute-start(bf16[2,176,2048]{2,1,0:T(8,128)(2,1)} %pad_maximum_fusion.2), channel_id=1, source_target_pairs={{0,1},{1,0},{2,3},{3,2},{4,5},{5,4},{6,7},{7,6},{8,9},{9,8},{10,11... | collective-permute-start | bytes 4325384 | tf_op jit(solution)/shard_map/ppermute | solution.py:18
  204.5 3.9 %copy-start.10 = (bf16[2,176,2048]{2,1,0:T(8,128)(2,1)}, bf16[2,176,2048]{2,1,0:T(8,128)(2,1)S(1)}, u32[]{:S(2)}) copy-start(bf16[2,176,2048]{2,1,0:T(8,128)(2,1)S(1)} %collective-permute-done.3) | copy-start | bytes 4325380
  293.6 1.9 copy-start.15
  295.4 1.9 copy-start.2
  295.4 1.9 copy-start.4
  295.4 1.9 copy-start.5
  297.3 4.5 %copy-start.1 = (bf16[1,256,1408]{2,1,0:T(8,128)(2,1)S(1)}, bf16[1,256,1408]{2,1,0:T(8,128)(2,1)}, u32[]{:S(2)}) copy-start(bf16[1,256,1408]{2,1,0:T(8,128)(2,1)} %broadcast_select_fusion) | copy-start | bytes 2162692
Sparse Core Ops, SparseCore 0:
  42.1 42.1 all-gather.4
  86.7 41.3 all-gather.2
  159.1 40.9 reduce-scatter.4
  202.5 43.2 reduce-scatter.2

commit v6 on v5

--- a/solution.py
+++ b/solution.py
@@ -123,8 +123,22 @@
     w_down_use = jnp.where(swapped, w_down_in, w_down)
     up_full = lax.all_gather(w_up_use, "dp", axis=1, tiled=True)[0]
     down_full = lax.all_gather(w_down_use, "dp", axis=1, tiled=True)[0]
-    expert_rows = got_both[:, :capacity].reshape(row_total, model_width)
-    grad_rows = got_both[:, capacity:].reshape(row_total, model_width)
+    slot_ids, buffer_ids = lax.optimization_barrier(
+        (
+            jnp.arange(row_total, dtype=jnp.int32),
+            jnp.arange(2 * row_total, dtype=jnp.int32),
+        )
+    )
+    token_at = (slot_ids // capacity) * (2 * capacity) + slot_ids % capacity
+    take_token = (token_at[:, None] == buffer_ids[None, :]).astype(jnp.bfloat16)
+    take_grad = (token_at[:, None] + capacity == buffer_ids[None, :]).astype(jnp.bfloat16)
+    got_rows = got_both.reshape(2 * row_total, model_width)
+    expert_rows = jnp.dot(take_token, got_rows, preferred_element_type=jnp.float32).astype(
+        jnp.bfloat16
+    )
+    grad_rows = jnp.dot(take_grad, got_rows, preferred_element_type=jnp.float32).astype(
+        jnp.bfloat16
+    )
     up_act = jnp.dot(expert_rows, up_full, preferred_element_type=jnp.float32)
     hidden = jax.nn.silu(up_act).astype(jnp.bfloat16)
     down_full, hidden, up_moments, down_local = lax.optimization_barrier(
@@ -137,13 +151,9 @@
     input_part = contract_cols(up_grad, up_full).astype(jnp.bfloat16)
     input_part, down_moments = lax.optimization_barrier((input_part, down_moments))
     both_back = lax.all_to_all(
-        jnp.concatenate(
-            [
-                expert_out.reshape(experts, capacity, model_width),
-                input_part.reshape(experts, capacity, model_width),
-            ],
-            axis=1,
-        ),
+        (contract_rows(take_token, expert_out) + contract_rows(take_grad, input_part))
+        .astype(jnp.bfloat16)
+        .reshape(experts, 2 * capacity, model_width),
         "expert",
         split_axis=0,
         concat_axis=0,

time: 314 us -> 315 us (level)
  local copies, waits for them, and re-layouts: 18.1 us -> 5.1 us
  matrix products: 44.6 us -> 57.4 us
    dot_general x2 -> x4, matrix products: 10.2 us -> 25.4 us  [contract_rows(): lax.dot_general(left, right, (((0,), (0,)), ((), ())), preferred_element_...]
    reshape x5 -> x1, local copies, waits for them, and re-layouts: 11.5 us -> 0.01 us  [the longest x1 3.94 us: body(): input_part.reshape(experts, capacity, model_width)]
    ppermute x4, waiting for transfers between devices: 44.7 us -> 48.3 us  [partner(): return lax.ppermute(value, axis, pairs)]
    dot_general x1 -> x2, matrix products: 6.44 us -> 5.16 us  [the longest x1 2.59 us: body(): jnp.dot(take_token, got_rows, preferred_element_type=jnp.float32)]
  transfers between devices with their start and end apart: 9 -> 9, of which waited for: 5 -> 5; matrix products, arithmetic and copies ran while one was open for 23% -> 19% of each run, Pallas kernels for 0% -> 0%
where the time goes in v6:
time: 315 us; the launch traced here: 314 us
  waiting for transfers between devices  120 us (38%)
  blocking collectives  82.7 us (26%)
  matrix products  57.4 us (18%)
  other arithmetic  17.9 us (6%)
  starting transfers between devices  16.3 us (5%)
  between operations  14.6 us (5%)
  local copies, waits for them, and re-layouts  5.1 us (2%)
    all_to_all x1, blocking collectives, body(): lax.all_to_all((contract_rows(take_token, expert_out) + contract_rows(tak...  82.7 us
    all_to_all x1, waiting for transfers between devices, body(): lax.all_to_all(send_both.reshape(experts, 2 * capacity, model_width), 'ex...  71.5 us
    ppermute x4, waiting for transfers between devices, partner(): return lax.ppermute(value, axis, pairs)  48.3 us
    dot_general x4, matrix products, contract_rows(): lax.dot_general(left, right, (((0,), (0,)), ((), ())), preferred_element_...  25.4 us
    dot_general x2, matrix products, contract_cols(): lax.dot_general(left, right, (((1,), (1,)), ((), ())), preferred_element_...  12.8 us
    all_to_all x1, starting transfers between devices, body(): lax.all_to_all(send_both.reshape(experts, 2 * capacity, model_width), 'ex...  11.3 us
    dot_general x1, matrix products, body(): up_act = jnp.dot(expert_rows, up_full, preferred_element_type=jnp.float32)  7.63 us
  transfers between devices with their start and end apart: 9, of which 5 were waited for; matrix products, arithmetic and copies ran while one was open for 19% of the time, Pallas kernels for 0%

profile of v6, /device:TPU:6, one launch (start us, length us, event | category | flops | bytes accessed | tf_op | source)
XLA Modules:
  0.0 314.1 jit_solution(4850015056384521962)
XLA Ops:
  7.2 2.0 collective-permute-start
  10.0 1.2 dynamic_slice.3
  12.8 0.9 reduce-window.6
  14.6 1.0 select_reduce_fusion
  16.3 2.3 pad_maximum_fusion.1
  18.7 1.3 pad_maximum_fusion
  20.0 2.7 multiply_convert_fusion
  22.7 3.8 %collective-permute-done = bf16[1,256,1408]{2,1,0:T(8,128)(2,1)S(1)} collective-permute-done((bf16[1,256,1408]{2,1,0:T(8,128)(2,1)}, bf16[1,256,1408]{2,1,0:T(8,128)(2,1)S(1)}, u32[]{:S(2)}, u32[]{:S(2)}) %collective-permute-start) | collective-permute-done | bytes 720928 | tf_op jit(solution)/shard_map/ppermute | solution.py:18
  26.5 14.5 %collective-permute-done.1 = bf16[1,176,2048]{2,1,0:T(8,128)(2,1)S(1)} collective-permute-done((bf16[1,176,2048]{2,1,0:T(8,128)(2,1)}, bf16[1,176,2048]{2,1,0:T(8,128)(2,1)S(1)}, u32[]{:S(2)}, u32[]{:S(2)}) %collective-permute-start.1) | collective-permute-done | bytes 720928 | tf_op jit(solution)/shard_map/ppermute | solution.py:18
  41.0 1.0 broadcast_select_fusion
  42.1 0.9 broadcast_select_fusion.1
  43.0 11.3 %all-to-all-start = ((bf16[32,24,2048]{2,1,0:T(8,128)(2,1)}), bf16[32,24,2048]{2,1,0:T(8,128)(2,1)S(1)}, u32[]{:S(2)}, u32[]{:S(2)}) async-start(bf16[32,24,2048]{2,1,0:T(8,128)(2,1)} %bitcast.5), calls=%async_computation | async-start | bytes 6291456 | tf_op jit(solution)/shard_map/all_to_all | solution.py:114
  54.5 2.1 collective-permute-start.2
  56.5 71.5 %all-to-all-done = bf16[32,24,2048]{2,1,0:T(8,128)(2,1)S(1)} async-done(((bf16[32,24,2048]{2,1,0:T(8,128)(2,1)}), bf16[32,24,2048]{2,1,0:T(8,128)(2,1)S(1)}, u32[]{:S(2)}, u32[]{:S(2)}) %all-to-all-start) | async-done | bytes 3145760 | tf_op jit(solution)/shard_map/all_to_all | solution.py:114
  128.1 2.6 convolution_convert_fusion.2
  130.6 2.6 convolution_convert_fusion.3
  133.2 7.6 %multiply_convert_fusion.1 = (bf16[384,1408]{1,0:T(8,128)(2,1)}, f32[384,1408]{1,0:T(8,128)}) fusion(bf16[384,2048]{1,0:T(8,128)(2,1)} %convolution_convert_fusion.3, bf16[1,2048,1408]{2,1,0:T(8,128)(2,1)} %all-gather.5.cloned.1.call-done), kind=kOutput, calls=%fused_computation.15 | convolution fusion | flops 2217295872 | bytes 10584064 | tf_op jit(solution)/shard_map/dot_general | solution.py:142
  140.8 13.1 %collective-permute-done.2 = bf16[2,256,1408]{2,1,0:T(8,128)(2,1)} collective-permute-done((bf16[2,256,1408]{2,1,0:T(8,128)(2,1)}, bf16[2,256,1408]{2,1,0:T(8,128)(2,1)}, u32[]{:S(2)}, u32[]{:S(2)}) %collective-permute-start.2) | collective-permute-done | bytes 1441824 | tf_op jit(solution)/shard_map/ppermute | solution.py:18
  154.0 7.2 %fusion.4 = bf16[384,1408]{1,0:T(8,128)(2,1)S(1)} fusion(bf16[384,2048]{1,0:T(8,128)(2,1)S(1)} %copy-done.13, bf16[1408,2048]{1,0:T(8,128)(2,1)} %bitcast.123, f32[384,1408]{1,0:T(8,128)} %get-tuple-element.43), kind=kOutput, calls=%fused_computation.9 | convolution fusion | flops 2219458560 | bytes 10584064 | tf_op jit(solution)/shard_map/dot_general | solution.py:50
  161.2 1.0 copy-done.16
  162.2 5.2 %convolution_convert_fusion.1 = bf16[2048,1408]{1,0:T(8,128)(2,1)} fusion(bf16[384,2048]{1,0:T(8,128)(2,1)S(1)} %copy-done.14, bf16[384,1408]{1,0:T(8,128)(2,1)S(1)} %fusion.4), kind=kOutput, calls=%fused_computation.1 | convolution fusion | flops 2217476096 | bytes 8421376 | tf_op jit(solution)/shard_map/dot_general | solution.py:44
  167.5 1.2 copy-done.15
  168.7 5.0 %convolution_convert_fusion = bf16[1408,2048]{1,0:T(8,128)(2,1)} fusion(bf16[384,1408]{1,0:T(8,128)(2,1)S(1)} %copy-done.15, bf16[384,2048]{1,0:T(8,128)(2,1)S(1)} %copy-done.13), kind=kOutput, calls=%fused_computation | convolution fusion | flops 2217476096 | bytes 8421376 | tf_op jit(solution)/shard_map/dot_general | solution.py:44
  174.3 5.6 %fusion.5 = bf16[384,2048]{1,0:T(8,128)(2,1)S(1)} fusion(bf16[384,1408]{1,0:T(8,128)(2,1)} %copy-done.16, bf16[1,2048,1408]{2,1,0:T(8,128)(2,1)} %all-gather.5.cloned.1.call-done), kind=kOutput, calls=%fused_computation.12 | convolution fusion | flops 2215378944 | bytes 8421376 | tf_op jit(solution)/shard_map/dot_general | solution.py:50
  179.9 9.9 %fusion.10 = f32[768,2048]{1,0:T(8,128)} fusion(bf16[384,1408]{1,0:T(8,128)(2,1)} %get-tuple-element.28, bf16[1408,2048]{1,0:T(8,128)(2,1)} %bitcast.124, s32[768]{0:T(1024)S(1)} %iota.43, s32[384]{0:T(512)S(1)} %get-tuple-element.35), kind=kOutput, calls=%fused_computation.23 | convolution fusion | flops 3423633408 | bytes 13144576 | tf_op jit(solution)/shard_map/dot_general | solution.py:44
  189.8 16.9 %collective-permute-done.3 = bf16[2,176,2048]{2,1,0:T(8,128)(2,1)S(1)} collective-permute-done((bf16[2,176,2048]{2,1,0:T(8,128)(2,1)}, bf16[2,176,2048]{2,1,0:T(8,128)(2,1)S(1)}, u32[]{:S(2)}, u32[]{:S(2)}) %collective-permute-start.3) | collective-permute-done | bytes 1441824 | tf_op jit(solution)/shard_map/ppermute | solution.py:18
  206.7 5.3 %add_convert_fusion = bf16[768,2048]{1,0:T(8,128)(2,1)S(1)} fusion(f32[768,2048]{1,0:T(8,128)} %fusion.10, bf16[384,2048]{1,0:T(8,128)(2,1)S(1)} %fusion.5, s32[768]{0:T(1024)S(1)} %iota.43, s32[384]{0:T(512)S(1)} %get-tuple-element.34), kind=kOutput, calls=%fused_computation.2 | convolution fusion | flops 1211400192 | bytes 11014656 | tf_op jit(solution)/shard_map/dot_general | solution.py:44
  212.0 82.7 %all_to_all.10 = bf16[32,24,2048]{2,1,0:T(8,128)(2,1)S(1)} all-to-all(bf16[32,24,2048]{2,1,0:T(8,128)(2,1)S(1)} %bitcast.117), channel_id=1, replica_groups=mesh['dp'=8,'expert'=32] {'expert'}, dimensions={0} | all-to-all | bytes 6291456 | tf_op jit(solution)/shard_map/all_to_all | solution.py:153
  294.8 1.8 convolution_reduce_fusion
  296.6 1.9 fusion.13
  298.5 4.6 %fusion.30 = (bf16[1,256,1408]{2,1,0:T(8,128)(2,1)}, bf16[1,256,1408]{2,1,0:T(8,128)(2,1)}, bf16[1,256,1408]{2,1,0:T(8,128)(2,1)}) fusion(bf16[256,1408]{1,0:T(8,128)(2,1)} %reduce-scatter.3.cloned.1.call-done, bf16[1,256,1408]{2,1,0:T(8,128)(2,1)S(1)} %copy-done.3, bf16[2,256,1408]{2,1,0:T(8,128)(2,1)} %collective-permute-done.2, pred[]{:T(512)} %bitcast.3, ...), kind=kLoop, calls=%fused_computation.51 | loop fusion | flops 7569408 | bytes 6488065 | tf_op jit(solution)/shard_map/broadcast_in_dim | solution.py:201
  303.1 4.4 %fusion.31 = (bf16[1,176,2048]{2,1,0:T(8,128)(2,1)}, bf16[1,176,2048]{2,1,0:T(8,128)(2,1)}, bf16[1,176,2048]{2,1,0:T(8,128)(2,1)}) fusion(bf16[176,2048]{1,0:T(8,128)(2,1)} %reduce-scatter.5.cloned.1.call-done, bf16[1,176,2048]{2,1,0:T(8,128)(2,1)} %param.21, bf16[2,176,2048]{2,1,0:T(8,128)(2,1)} %copy-done.7, pred[]{:T(512)} %bitcast.3, ...), kind=kLoop, calls=%fused_computation.52 | loop fusion | flops 7569408 | bytes 6488065 | tf_op jit(solution)/shard_map/broadcast_in_dim | solution.py:203
  (71 shorter events, 4.3 us)
Async XLA Ops:
  7.2 9.2 %copy-start.6 = (bf16[1,176,2048]{2,1,0:T(8,128)(2,1)S(1)}, bf16[1,176,2048]{2,1,0:T(8,128)(2,1)}, u32[]{:S(2)}) copy-start(bf16[1,176,2048]{2,1,0:T(8,128)(2,1)} %param.21) | copy-start | bytes 2162692
  7.2 126.0 %all-gather.5.cloned.1.call-start = ((), (), s32[]{:S(2)}) async-start(), calls=%async_computation.5 | async-start | bytes 6488064 | tf_op jit(solution)/shard_map/all_gather | solution.py:124
  7.2 19.3 %collective-permute-start = (bf16[1,256,1408]{2,1,0:T(8,128)(2,1)}, bf16[1,256,1408]{2,1,0:T(8,128)(2,1)S(1)}, u32[]{:S(2)}, u32[]{:S(2)}) collective-permute-start(bf16[1,256,1408]{2,1,0:T(8,128)(2,1)} %param.16), channel_id=1, source_target_pairs={{0,1},{1,0},{2,3},{3,2},{4,5},{5,4},{6,7},{7,6},{8,9},{9,8},{10,11... | collective-permute-start | bytes 2162696 | tf_op jit(solution)/shard_map/ppermute | solution.py:18
  9.2 31.8 %collective-permute-start.1 = (bf16[1,176,2048]{2,1,0:T(8,128)(2,1)}, bf16[1,176,2048]{2,1,0:T(8,128)(2,1)S(1)}, u32[]{:S(2)}, u32[]{:S(2)}) collective-permute-start(bf16[1,176,2048]{2,1,0:T(8,128)(2,1)} %param.17), channel_id=1, source_target_pairs={{0,1},{1,0},{2,3},{3,2},{4,5},{5,4},{6,7},{7,6},{8,9},{9,8},{10,11... | collective-permute-start | bytes 2162696 | tf_op jit(solution)/shard_map/ppermute | solution.py:18
  14.3 4.3 %copy-start.2 = (bf16[1,256,1408]{2,1,0:T(8,128)(2,1)S(1)}, bf16[1,256,1408]{2,1,0:T(8,128)(2,1)}, u32[]{:S(2)}) copy-start(bf16[1,256,1408]{2,1,0:T(8,128)(2,1)} %param.19) | copy-start | bytes 2162692
  14.3 4.3 %copy-start.4 = (bf16[1,256,1408]{2,1,0:T(8,128)(2,1)S(1)}, bf16[1,256,1408]{2,1,0:T(8,128)(2,1)}, u32[]{:S(2)}) copy-start(bf16[1,256,1408]{2,1,0:T(8,128)(2,1)} %param.18) | copy-start | bytes 2162692
  18.7 1.3 copy-start.10
  18.7 1.3 copy-start.11
  20.0 21.0 %copy-start.8 = (bf16[1,256,1408]{2,1,0:T(8,128)(2,1)S(1)}, bf16[1,256,1408]{2,1,0:T(8,128)(2,1)}, u32[]{:S(2)}) copy-start(bf16[1,256,1408]{2,1,0:T(8,128)(2,1)} %param.16) | copy-start | bytes 2162692
  22.7 19.4 %copy-start.9 = (bf16[1,176,2048]{2,1,0:T(8,128)(2,1)S(1)}, bf16[1,176,2048]{2,1,0:T(8,128)(2,1)}, u32[]{:S(2)}) copy-start(bf16[1,176,2048]{2,1,0:T(8,128)(2,1)} %param.17) | copy-start | bytes 2162692
  42.0 111.9 %all-gather.3.cloned.1.call-start = ((), (), s32[]{:S(2)}) async-start(), calls=%async_computation.4 | async-start | bytes 6488064 | tf_op jit(solution)/shard_map/all_gather | solution.py:125
  43.0 85.0 %all-to-all-start = ((bf16[32,24,2048]{2,1,0:T(8,128)(2,1)}), bf16[32,24,2048]{2,1,0:T(8,128)(2,1)S(1)}, u32[]{:S(2)}, u32[]{:S(2)}) async-start(bf16[32,24,2048]{2,1,0:T(8,128)(2,1)} %bitcast.5), calls=%async_computation | async-start | bytes 6291456 | tf_op jit(solution)/shard_map/all_to_all | solution.py:114
  54.4 244.2 %reduce-scatter.3.cloned.1.call-start = ((), (), s32[]{:S(2)}) async-start(), calls=%async_computation.6 | async-start | bytes 6488064 | tf_op jit(solution)/shard_map/reduce_scatter | solution.py:177
  54.5 99.5 %collective-permute-start.2 = (bf16[2,256,1408]{2,1,0:T(8,128)(2,1)}, bf16[2,256,1408]{2,1,0:T(8,128)(2,1)}, u32[]{:S(2)}, u32[]{:S(2)}) collective-permute-start(bf16[2,256,1408]{2,1,0:T(8,128)(2,1)} %pad_maximum_fusion), channel_id=1, source_target_pairs={{0,1},{1,0},{2,3},{3,2},{4,5},{5,4},{6,7},{7,6},{8,9},{9,8},{10,11... | collective-permute-start | bytes 4325384 | tf_op jit(solution)/shard_map/ppermute | solution.py:18
  133.2 20.8 %copy-start.13 = (bf16[384,2048]{1,0:T(8,128)(2,1)S(1)}, bf16[384,2048]{1,0:T(8,128)(2,1)}, u32[]{:S(2)}) copy-start(bf16[384,2048]{1,0:T(8,128)(2,1)} %convolution_convert_fusion.2) | copy-start | bytes 4718596
  154.0 8.2 %copy-start.14 = (bf16[384,2048]{1,0:T(8,128)(2,1)S(1)}, bf16[384,2048]{1,0:T(8,128)(2,1)}, u32[]{:S(2)}) copy-start(bf16[384,2048]{1,0:T(8,128)(2,1)} %convolution_convert_fusion.3) | copy-start | bytes 4718596
  161.2 1.0 copy-start.16
  167.4 1.2 copy-start.15
  167.4 135.7 %reduce-scatter.5.cloned.1.call-start = ((), (), s32[]{:S(2)}) async-start(), calls=%async_computation.7 | async-start | bytes 6488064 | tf_op jit(solution)/shard_map/reduce_scatter | solution.py:183
  173.6 33.1 %collective-permute-start.3 = (bf16[2,176,2048]{2,1,0:T(8,128)(2,1)}, bf16[2,176,2048]{2,1,0:T(8,128)(2,1)S(1)}, u32[]{:S(2)}, u32[]{:S(2)}) collective-permute-start(bf16[2,176,2048]{2,1,0:T(8,128)(2,1)} %pad_maximum_fusion.1), channel_id=1, source_target_pairs={{0,1},{1,0},{2,3},{3,2},{4,5},{5,4},{6,7},{7,6},{8,9},{9,8},{10,11... | collective-permute-start | bytes 4325384 | tf_op jit(solution)/shard_map/ppermute | solution.py:18
  206.7 5.3 %copy-start.7 = (bf16[2,176,2048]{2,1,0:T(8,128)(2,1)}, bf16[2,176,2048]{2,1,0:T(8,128)(2,1)S(1)}, u32[]{:S(2)}) copy-start(bf16[2,176,2048]{2,1,0:T(8,128)(2,1)S(1)} %collective-permute-done.3) | copy-start | bytes 4325380
  294.8 1.9 copy-start.12
  296.6 1.9 copy-start
  296.6 1.9 copy-start.3
  296.6 1.9 copy-start.5
  298.5 4.6 %copy-start.1 = (bf16[1,176,2048]{2,1,0:T(8,128)(2,1)S(1)}, bf16[1,176,2048]{2,1,0:T(8,128)(2,1)}, u32[]{:S(2)}) copy-start(bf16[1,176,2048]{2,1,0:T(8,128)(2,1)} %broadcast_select_fusion.1) | copy-start | bytes 2162692
Sparse Core Ops, SparseCore 0:
  42.1 42.1 all-gather.4
  86.7 41.3 all-gather.2
  167.6 40.9 reduce-scatter.2
  211.0 43.2 reduce-scatter.4

commit v7 on v6

--- a/solution.py
+++ b/solution.py
@@ -159,6 +159,25 @@
         concat_axis=0,
         tiled=True,
     )
+    up_gradient = lax.psum_scatter(
+        contract_rows(expert_rows, up_grad).astype(jnp.bfloat16),
+        "dp",
+        scatter_dimension=0,
+        tiled=True,
+    ).astype(jnp.float32)
+    down_gradient = lax.psum_scatter(
+        contract_rows(hidden, grad_rows).astype(jnp.bfloat16),
+        "dp",
+        scatter_dimension=0,
+        tiled=True,
+    ).astype(jnp.float32)
+    m_up_use = jnp.where(swapped, up_moments[0:1], m_up)
+    v_up_use = jnp.where(swapped, up_moments[1:2], v_up)
+    m_down_use = jnp.where(swapped, down_moments[0:1], m_down)
+    v_down_use = jnp.where(swapped, down_moments[1:2], v_down)
+    up_new = adam_update(w_up_use[0], m_up_use[0], v_up_use[0], up_gradient)
+    down_new = adam_update(w_down_use[0], m_down_use[0], v_down_use[0], down_gradient)
+    both_back, up_new, down_new = lax.optimization_barrier((both_back, up_new, down_new))
     back_rows = both_back.reshape(2 * row_total, model_width)
     picked = jnp.dot(
         (send_row.reshape(pair_count)[:, None] == row_ids[None, :]).astype(jnp.bfloat16),
@@ -174,24 +193,6 @@
         preferred_element_type=jnp.float32,
     ).reshape(tok_count, chosen, model_width)
     input_grad = jnp.sum(picked_grad, axis=1).astype(jnp.bfloat16)
-    up_gradient = lax.psum_scatter(
-        contract_rows(expert_rows, up_grad).astype(jnp.bfloat16),
-        "dp",
-        scatter_dimension=0,
-        tiled=True,
-    ).astype(jnp.float32)
-    down_gradient = lax.psum_scatter(
-        contract_rows(hidden, grad_rows).astype(jnp.bfloat16),
-        "dp",
-        scatter_dimension=0,
-        tiled=True,
-    ).astype(jnp.float32)
-    m_up_use = jnp.where(swapped, up_moments[0:1], m_up)
-    v_up_use = jnp.where(swapped, up_moments[1:2], v_up)
-    m_down_use = jnp.where(swapped, down_moments[0:1], m_down)
-    v_down_use = jnp.where(swapped, down_moments[1:2], v_down)
-    up_new = adam_update(w_up_use[0], m_up_use[0], v_up_use[0], up_gradient)
-    down_new = adam_update(w_down_use[0], m_down_use[0], v_down_use[0], down_gradient)
     return (
         mixed,
         input_grad,

time: 315 us -> 310 us (0.984)
  blocking collectives: 82.7 us -> 0 us
  waiting for transfers between devices: 120 us -> 185 us
  starting transfers between devices: 16.3 us -> 26.3 us
  matrix products: 57.4 us -> 62.7 us
    all_to_all x1 -> x0, blocking collectives: 82.7 us -> none  [body(): lax.all_to_all((contract_rows(take_token, expert_out) + contract_rows(tak...]
    all_to_all x0 -> x1, waiting for transfers between devices: none -> 45 us  [body(): lax.all_to_all((contract_rows(take_token, expert_out) + contract_rows(tak...]
    reduce_scatter x1, waiting for transfers between devices: 0.01 us -> 19.6 us  [body(): lax.psum_scatter(contract_rows(expert_rows, up_grad).astype(jnp.bfloat16)...]
    all_to_all x0 -> x1, starting transfers between devices: none -> 10.2 us  [body(): lax.all_to_all((contract_rows(take_token, expert_out) + contract_rows(tak...]
    convert_element_type x0 -> x2, other arithmetic: none -> 9.01 us  [adam_update(): second_new.astype(jnp.bfloat16)]
    broadcast_in_dim x2 -> x0, other arithmetic: 8.96 us -> none  [the longest x1 4.57 us: body(): up_new[2][None]]
  transfers between devices with their start and end apart: 9 -> 10, of which waited for: 5 -> 7; matrix products, arithmetic and copies ran while one was open for 19% -> 23% of each run, Pallas kernels for 0% -> 0%
where the time goes in v7:
time: 310 us; the launch traced here: 309 us
  waiting for transfers between devices  185 us (60%)
  matrix products  62.7 us (20%)
  starting transfers between devices  26.3 us (8%)
  other arithmetic  18 us (6%)
  between operations  14.7 us (5%)
    all_to_all x1, waiting for transfers between devices, body(): lax.all_to_all(send_both.reshape(experts, 2 * capacity, model_width), 'ex...  71.7 us
    ppermute x4, waiting for transfers between devices, partner(): return lax.ppermute(value, axis, pairs)  48.3 us
    all_to_all x1, waiting for transfers between devices, body(): lax.all_to_all((contract_rows(take_token, expert_out) + contract_rows(tak...  45 us
    dot_general x4, matrix products, contract_rows(): lax.dot_general(left, right, (((0,), (0,)), ((), ())), preferred_element_...  27.1 us
    reduce_scatter x1, waiting for transfers between devices, body(): lax.psum_scatter(contract_rows(expert_rows, up_grad).astype(jnp.bfloat16)...  19.6 us
    dot_general x2, matrix products, contract_cols(): lax.dot_general(left, right, (((1,), (1,)), ((), ())), preferred_element_...  12.9 us
    all_to_all x1, starting transfers between devices, body(): lax.all_to_all(send_both.reshape(experts, 2 * capacity, model_width), 'ex...  11.3 us
    all_to_all x1, starting transfers between devices, body(): lax.all_to_all((contract_rows(take_token, expert_out) + contract_rows(tak...  10.2 us
  transfers between devices with their start and end apart: 10, of which 7 were waited for; matrix products, arithmetic and copies ran while one was open for 23% of the time, Pallas kernels for 0%

profile of v7, /device:TPU:6, one launch (start us, length us, event | category | flops | bytes accessed | tf_op | source)
XLA Modules:
  0.0 309.4 jit_solution(3745145657182362838)
XLA Ops:
  7.2 2.0 collective-permute-start
  10.0 1.2 dynamic_slice.3
  12.8 0.9 reduce-window.6
  14.6 1.0 select_reduce_fusion
  16.3 2.5 pad_maximum_fusion.1
  18.8 1.3 pad_maximum_fusion
  20.1 2.7 multiply_convert_fusion
  22.8 3.7 %collective-permute-done = bf16[1,256,1408]{2,1,0:T(8,128)(2,1)S(1)} collective-permute-done((bf16[1,256,1408]{2,1,0:T(8,128)(2,1)}, bf16[1,256,1408]{2,1,0:T(8,128)(2,1)S(1)}, u32[]{:S(2)}, u32[]{:S(2)}) %collective-permute-start) | collective-permute-done | bytes 720928 | tf_op jit(solution)/shard_map/ppermute | solution.py:18
  26.5 14.5 %collective-permute-done.1 = bf16[1,176,2048]{2,1,0:T(8,128)(2,1)S(1)} collective-permute-done((bf16[1,176,2048]{2,1,0:T(8,128)(2,1)}, bf16[1,176,2048]{2,1,0:T(8,128)(2,1)S(1)}, u32[]{:S(2)}, u32[]{:S(2)}) %collective-permute-start.1) | collective-permute-done | bytes 720928 | tf_op jit(solution)/shard_map/ppermute | solution.py:18
  41.0 1.0 broadcast_select_fusion
  42.1 0.9 broadcast_select_fusion.1
  43.0 11.3 %all-to-all-start = ((bf16[32,24,2048]{2,1,0:T(8,128)(2,1)}), bf16[32,24,2048]{2,1,0:T(8,128)(2,1)S(1)}, u32[]{:S(2)}, u32[]{:S(2)}) async-start(bf16[32,24,2048]{2,1,0:T(8,128)(2,1)} %bitcast.5), calls=%async_computation | async-start | bytes 6291456 | tf_op jit(solution)/shard_map/all_to_all | solution.py:114
  54.5 1.9 collective-permute-start.2
  56.3 71.7 %all-to-all-done = bf16[32,24,2048]{2,1,0:T(8,128)(2,1)S(1)} async-done(((bf16[32,24,2048]{2,1,0:T(8,128)(2,1)}), bf16[32,24,2048]{2,1,0:T(8,128)(2,1)S(1)}, u32[]{:S(2)}, u32[]{:S(2)}) %all-to-all-start) | async-done | bytes 3145760 | tf_op jit(solution)/shard_map/all_to_all | solution.py:114
  128.1 2.7 convolution_convert_fusion.2
  130.7 2.6 convolution_convert_fusion.3
  133.3 7.3 %multiply_convert_fusion.1 = (bf16[384,1408]{1,0:T(8,128)(2,1)S(1)}, f32[384,1408]{1,0:T(8,128)}) fusion(bf16[384,2048]{1,0:T(8,128)(2,1)} %convolution_convert_fusion.3, bf16[1,2048,1408]{2,1,0:T(8,128)(2,1)} %all-gather.5.cloned.1.call-done), kind=kOutput, calls=%fused_computation.15 | convolution fusion | flops 2217295872 | bytes 10584064 | tf_op jit(solution)/shard_map/dot_general | solution.py:142
  140.6 13.4 %collective-permute-done.2 = bf16[2,256,1408]{2,1,0:T(8,128)(2,1)} collective-permute-done((bf16[2,256,1408]{2,1,0:T(8,128)(2,1)}, bf16[2,256,1408]{2,1,0:T(8,128)(2,1)}, u32[]{:S(2)}, u32[]{:S(2)}) %collective-permute-start.2) | collective-permute-done | bytes 1441824 | tf_op jit(solution)/shard_map/ppermute | solution.py:18
  154.0 4.9 %convolution_convert_fusion = bf16[1408,2048]{1,0:T(8,128)(2,1)} fusion(bf16[384,1408]{1,0:T(8,128)(2,1)S(1)} %get-tuple-element.35, bf16[384,2048]{1,0:T(8,128)(2,1)S(1)} %copy-done.14), kind=kOutput, calls=%fused_computation | convolution fusion | flops 2217476096 | bytes 8421376 | tf_op jit(solution)/shard_map/dot_general | solution.py:44
  159.2 7.2 %fusion.4 = bf16[384,1408]{1,0:T(8,128)(2,1)S(1)} fusion(bf16[384,2048]{1,0:T(8,128)(2,1)S(1)} %copy-done.14, bf16[1408,2048]{1,0:T(8,128)(2,1)} %bitcast.100, f32[384,1408]{1,0:T(8,128)} %get-tuple-element.57), kind=kOutput, calls=%fused_computation.9 | convolution fusion | flops 2219458560 | bytes 10584064 | tf_op jit(solution)/shard_map/dot_general | solution.py:50
  166.5 5.2 %convolution_convert_fusion.1 = bf16[2048,1408]{1,0:T(8,128)(2,1)} fusion(bf16[384,2048]{1,0:T(8,128)(2,1)S(1)} %copy-done.13, bf16[384,1408]{1,0:T(8,128)(2,1)S(1)} %fusion.4), kind=kOutput, calls=%fused_computation.1 | convolution fusion | flops 2217476096 | bytes 8421376 | tf_op jit(solution)/shard_map/dot_general | solution.py:44
  172.2 5.7 %fusion.5 = bf16[384,2048]{1,0:T(8,128)(2,1)S(1)} fusion(bf16[384,1408]{1,0:T(8,128)(2,1)} %copy-done.16, bf16[1,2048,1408]{2,1,0:T(8,128)(2,1)} %all-gather.5.cloned.1.call-done), kind=kOutput, calls=%fused_computation.12 | convolution fusion | flops 2215378944 | bytes 8421376 | tf_op jit(solution)/shard_map/dot_general | solution.py:50
  177.9 10.0 %fusion.10 = f32[768,2048]{1,0:T(8,128)} fusion(bf16[384,1408]{1,0:T(8,128)(2,1)} %copy-done.15, bf16[1408,2048]{1,0:T(8,128)(2,1)} %bitcast.101, s32[768]{0:T(1024)S(1)} %iota.43, s32[384]{0:T(512)S(1)} %get-tuple-element.49), kind=kOutput, calls=%fused_computation.23 | convolution fusion | flops 3423633408 | bytes 13144576 | tf_op jit(solution)/shard_map/dot_general | solution.py:44
  187.9 16.7 %collective-permute-done.3 = bf16[2,176,2048]{2,1,0:T(8,128)(2,1)S(1)} collective-permute-done((bf16[2,176,2048]{2,1,0:T(8,128)(2,1)}, bf16[2,176,2048]{2,1,0:T(8,128)(2,1)S(1)}, u32[]{:S(2)}, u32[]{:S(2)}) %collective-permute-start.3) | collective-permute-done | bytes 1441824 | tf_op jit(solution)/shard_map/ppermute | solution.py:18
  204.5 6.9 %add_convert_fusion = bf16[768,2048]{1,0:T(8,128)(2,1)} fusion(f32[768,2048]{1,0:T(8,128)} %fusion.10, bf16[384,2048]{1,0:T(8,128)(2,1)S(1)} %fusion.5, s32[768]{0:T(1024)S(1)} %iota.43, s32[384]{0:T(512)S(1)} %get-tuple-element.48), kind=kOutput, calls=%fused_computation.2 | convolution fusion | flops 1211400192 | bytes 11014656 | tf_op jit(solution)/shard_map/dot_general | solution.py:44
  211.5 10.2 %all-to-all-start.1 = ((bf16[32,24,2048]{2,1,0:T(8,128)(2,1)}), bf16[32,24,2048]{2,1,0:T(8,128)(2,1)}, u32[]{:S(2)}, u32[]{:S(2)}) async-start(bf16[32,24,2048]{2,1,0:T(8,128)(2,1)} %bitcast.8), calls=%async_computation.1 | async-start | bytes 6291456 | tf_op jit(solution)/shard_map/all_to_all | solution.py:153
  221.7 4.5 %fusion.22 = (bf16[176,2048]{1,0:T(8,128)(2,1)}, bf16[176,2048]{1,0:T(8,128)(2,1)}, bf16[176,2048]{1,0:T(8,128)(2,1)}) fusion(bf16[176,2048]{1,0:T(8,128)(2,1)} %reduce-scatter.5.cloned.1.call-done, bf16[1,176,2048]{2,1,0:T(8,128)(2,1)S(1)} %copy-done.3, bf16[2,176,2048]{2,1,0:T(8,128)(2,1)} %copy-done.7, pred[]{:T(512)} %bitcast.3, ...), kind=kLoop, calls=%fused_computation.40 | loop fusion | flops 7569408 | bytes 6488065 | tf_op jit(solution)/shard_map/convert_element_type | solution.py:39
  226.2 19.6 %reduce-scatter.3.cloned.1.call-done = bf16[256,1408]{1,0:T(8,128)(2,1)} async-done(((bf16[2048,1408]{1,0:T(8,128)(2,1)}), bf16[256,1408]{1,0:T(8,128)(2,1)}) %reduce-scatter.3.cloned.1.call-update) | async-done | bytes 720912 | tf_op jit(solution)/shard_map/reduce_scatter | solution.py:162
  245.8 4.5 %fusion.23 = (bf16[256,1408]{1,0:T(8,128)(2,1)}, bf16[256,1408]{1,0:T(8,128)(2,1)}, bf16[256,1408]{1,0:T(8,128)(2,1)}) fusion(bf16[256,1408]{1,0:T(8,128)(2,1)} %reduce-scatter.3.cloned.1.call-done, bf16[1,256,1408]{2,1,0:T(8,128)(2,1)} %param.19, bf16[2,256,1408]{2,1,0:T(8,128)(2,1)} %collective-permute-done.2, pred[]{:T(512)} %bitcast.3, ...), kind=kLoop, calls=%fused_computation.41 | loop fusion | flops 7569408 | bytes 6488065 | tf_op jit(solution)/shard_map/convert_element_type | solution.py:39
  250.3 45.0 %all-to-all-done.1 = bf16[32,24,2048]{2,1,0:T(8,128)(2,1)} async-done(((bf16[32,24,2048]{2,1,0:T(8,128)(2,1)}), bf16[32,24,2048]{2,1,0:T(8,128)(2,1)}, u32[]{:S(2)}, u32[]{:S(2)}) %all-to-all-start.1) | async-done | bytes 3145760 | tf_op jit(solution)/shard_map/all_to_all | solution.py:153
  295.3 3.7 %convolution_reduce_fusion = bf16[48,2048]{1,0:T(8,128)(2,1)} fusion(bf16[768,2048,1]{1,0,2:T(8,128)(2,1)} %bitcast.16, s32[48,6]{0,1:T(8,128)S(1)} %broadcast_add_fusion), kind=kOutput, calls=%fused_computation.27 | convolution fusion | flops 906682368 | bytes 3343488 | tf_op jit(solution)/shard_map/dot_general | solution.py:188
  299.1 3.8 %fusion.13 = bf16[48,2048]{1,0:T(8,128)(2,1)} fusion(bf16[768,2048,1]{1,0,2:T(8,128)(2,1)} %bitcast.16, f32[48,6]{0,1:T(8,128)S(1)} %copy-done.12, s32[48,6]{0,1:T(8,128)S(1)} %copy.38), kind=kOutput, calls=%fused_computation.26 | convolution fusion | flops 907272192 | bytes 3344640 | tf_op jit(solution)/shard_map/dot_general | solution.py:182
  (72 shorter events, 4.2 us)
Async XLA Ops:
  7.2 9.2 %copy-start.2 = (bf16[1,176,2048]{2,1,0:T(8,128)(2,1)S(1)}, bf16[1,176,2048]{2,1,0:T(8,128)(2,1)}, u32[]{:S(2)}) copy-start(bf16[1,176,2048]{2,1,0:T(8,128)(2,1)} %param.21) | copy-start | bytes 2162692
  7.2 126.1 %all-gather.5.cloned.1.call-start = ((), (), s32[]{:S(2)}) async-start(), calls=%async_computation.5 | async-start | bytes 6488064 | tf_op jit(solution)/shard_map/all_gather | solution.py:124
  7.2 19.3 %collective-permute-start = (bf16[1,256,1408]{2,1,0:T(8,128)(2,1)}, bf16[1,256,1408]{2,1,0:T(8,128)(2,1)S(1)}, u32[]{:S(2)}, u32[]{:S(2)}) collective-permute-start(bf16[1,256,1408]{2,1,0:T(8,128)(2,1)} %param.16), channel_id=1, source_target_pairs={{0,1},{1,0},{2,3},{3,2},{4,5},{5,4},{6,7},{7,6},{8,9},{9,8},{10,11... | collective-permute-start | bytes 2162696 | tf_op jit(solution)/shard_map/ppermute | solution.py:18
  9.2 31.8 %collective-permute-start.1 = (bf16[1,176,2048]{2,1,0:T(8,128)(2,1)}, bf16[1,176,2048]{2,1,0:T(8,128)(2,1)S(1)}, u32[]{:S(2)}, u32[]{:S(2)}) collective-permute-start(bf16[1,176,2048]{2,1,0:T(8,128)(2,1)} %param.17), channel_id=1, source_target_pairs={{0,1},{1,0},{2,3},{3,2},{4,5},{5,4},{6,7},{7,6},{8,9},{9,8},{10,11... | collective-permute-start | bytes 2162696 | tf_op jit(solution)/shard_map/ppermute | solution.py:18
  14.3 4.4 %copy-start.5 = (bf16[1,256,1408]{2,1,0:T(8,128)(2,1)S(1)}, bf16[1,256,1408]{2,1,0:T(8,128)(2,1)}, u32[]{:S(2)}) copy-start(bf16[1,256,1408]{2,1,0:T(8,128)(2,1)} %param.19) | copy-start | bytes 2162692
  14.3 4.4 %copy-start.6 = (bf16[1,256,1408]{2,1,0:T(8,128)(2,1)S(1)}, bf16[1,256,1408]{2,1,0:T(8,128)(2,1)}, u32[]{:S(2)}) copy-start(bf16[1,256,1408]{2,1,0:T(8,128)(2,1)} %param.18) | copy-start | bytes 2162692
  18.8 1.3 copy-start.10
  18.8 1.3 copy-start.11
  20.1 20.9 %copy-start.8 = (bf16[1,256,1408]{2,1,0:T(8,128)(2,1)S(1)}, bf16[1,256,1408]{2,1,0:T(8,128)(2,1)}, u32[]{:S(2)}) copy-start(bf16[1,256,1408]{2,1,0:T(8,128)(2,1)} %param.16) | copy-start | bytes 2162692
  22.8 19.3 %copy-start.9 = (bf16[1,176,2048]{2,1,0:T(8,128)(2,1)S(1)}, bf16[1,176,2048]{2,1,0:T(8,128)(2,1)}, u32[]{:S(2)}) copy-start(bf16[1,176,2048]{2,1,0:T(8,128)(2,1)} %param.17) | copy-start | bytes 2162692
  42.0 111.9 %all-gather.3.cloned.1.call-start = ((), (), s32[]{:S(2)}) async-start(), calls=%async_computation.4 | async-start | bytes 6488064 | tf_op jit(solution)/shard_map/all_gather | solution.py:125
  43.0 85.0 %all-to-all-start = ((bf16[32,24,2048]{2,1,0:T(8,128)(2,1)}), bf16[32,24,2048]{2,1,0:T(8,128)(2,1)S(1)}, u32[]{:S(2)}, u32[]{:S(2)}) async-start(bf16[32,24,2048]{2,1,0:T(8,128)(2,1)} %bitcast.5), calls=%async_computation | async-start | bytes 6291456 | tf_op jit(solution)/shard_map/all_to_all | solution.py:114
  54.4 167.3 %reduce-scatter.5.cloned.1.call-start = ((), (), s32[]{:S(2)}) async-start(), calls=%async_computation.7 | async-start | bytes 6488064 | tf_op jit(solution)/shard_map/reduce_scatter | solution.py:168
  54.5 99.5 %collective-permute-start.2 = (bf16[2,256,1408]{2,1,0:T(8,128)(2,1)}, bf16[2,256,1408]{2,1,0:T(8,128)(2,1)}, u32[]{:S(2)}, u32[]{:S(2)}) collective-permute-start(bf16[2,256,1408]{2,1,0:T(8,128)(2,1)} %pad_maximum_fusion), channel_id=1, source_target_pairs={{0,1},{1,0},{2,3},{3,2},{4,5},{5,4},{6,7},{7,6},{8,9},{9,8},{10,11... | collective-permute-start | bytes 4325384 | tf_op jit(solution)/shard_map/ppermute | solution.py:18
  133.3 20.7 %copy-start.14 = (bf16[384,2048]{1,0:T(8,128)(2,1)S(1)}, bf16[384,2048]{1,0:T(8,128)(2,1)}, u32[]{:S(2)}) copy-start(bf16[384,2048]{1,0:T(8,128)(2,1)} %convolution_convert_fusion.2) | copy-start | bytes 4718596
  140.6 18.4 %copy-start.15 = (bf16[384,1408]{1,0:T(8,128)(2,1)}, bf16[384,1408]{1,0:T(8,128)(2,1)S(1)}, u32[]{:S(2)}) copy-start(bf16[384,1408]{1,0:T(8,128)(2,1)S(1)} %get-tuple-element.35) | copy-start | bytes 3244036
  159.0 86.9 %reduce-scatter.3.cloned.1.call-start = ((), (), s32[]{:S(2)}) async-start(), calls=%async_computation.6 | async-start | bytes 6488064 | tf_op jit(solution)/shard_map/reduce_scatter | solution.py:162
  159.2 7.3 %copy-start.13 = (bf16[384,2048]{1,0:T(8,128)(2,1)S(1)}, bf16[384,2048]{1,0:T(8,128)(2,1)}, u32[]{:S(2)}) copy-start(bf16[384,2048]{1,0:T(8,128)(2,1)} %convolution_convert_fusion.3) | copy-start | bytes 4718596
  166.5 5.2 %copy-start.16 = (bf16[384,1408]{1,0:T(8,128)(2,1)}, bf16[384,1408]{1,0:T(8,128)(2,1)S(1)}, u32[]{:S(2)}) copy-start(bf16[384,1408]{1,0:T(8,128)(2,1)S(1)} %fusion.4) | copy-start | bytes 3244036
  171.7 32.8 %collective-permute-start.3 = (bf16[2,176,2048]{2,1,0:T(8,128)(2,1)}, bf16[2,176,2048]{2,1,0:T(8,128)(2,1)S(1)}, u32[]{:S(2)}, u32[]{:S(2)}) collective-permute-start(bf16[2,176,2048]{2,1,0:T(8,128)(2,1)} %pad_maximum_fusion.1), channel_id=1, source_target_pairs={{0,1},{1,0},{2,3},{3,2},{4,5},{5,4},{6,7},{7,6},{8,9},{9,8},{10,11... | collective-permute-start | bytes 4325384 | tf_op jit(solution)/shard_map/ppermute | solution.py:18
  204.5 6.9 %copy-start.7 = (bf16[2,176,2048]{2,1,0:T(8,128)(2,1)}, bf16[2,176,2048]{2,1,0:T(8,128)(2,1)S(1)}, u32[]{:S(2)}) copy-start(bf16[2,176,2048]{2,1,0:T(8,128)(2,1)S(1)} %collective-permute-done.3) | copy-start | bytes 4325380
  211.5 10.2 %copy-start.1 = (bf16[1,176,2048]{2,1,0:T(8,128)(2,1)S(1)}, bf16[1,176,2048]{2,1,0:T(8,128)(2,1)}, u32[]{:S(2)}) copy-start(bf16[1,176,2048]{2,1,0:T(8,128)(2,1)} %broadcast_select_fusion.1) | copy-start | bytes 2162692
  211.5 10.2 %copy-start.3 = (bf16[1,176,2048]{2,1,0:T(8,128)(2,1)S(1)}, bf16[1,176,2048]{2,1,0:T(8,128)(2,1)}, u32[]{:S(2)}) copy-start(bf16[1,176,2048]{2,1,0:T(8,128)(2,1)} %param.21) | copy-start | bytes 2162692
  211.5 10.2 %copy-start.4 = (bf16[1,176,2048]{2,1,0:T(8,128)(2,1)S(1)}, bf16[1,176,2048]{2,1,0:T(8,128)(2,1)}, u32[]{:S(2)}) copy-start(bf16[1,176,2048]{2,1,0:T(8,128)(2,1)} %param.20) | copy-start | bytes 2162692
  211.5 83.9 %all-to-all-start.1 = ((bf16[32,24,2048]{2,1,0:T(8,128)(2,1)}), bf16[32,24,2048]{2,1,0:T(8,128)(2,1)}, u32[]{:S(2)}, u32[]{:S(2)}) async-start(bf16[32,24,2048]{2,1,0:T(8,128)(2,1)} %bitcast.8), calls=%async_computation.1 | async-start | bytes 6291456 | tf_op jit(solution)/shard_map/all_to_all | solution.py:153
  221.6 24.2 %copy-start = (bf16[1,256,1408]{2,1,0:T(8,128)(2,1)S(1)}, bf16[1,256,1408]{2,1,0:T(8,128)(2,1)}, u32[]{:S(2)}) copy-start(bf16[1,256,1408]{2,1,0:T(8,128)(2,1)} %broadcast_select_fusion) | copy-start | bytes 2162692
  295.3 3.8 %copy-start.12 = (f32[48,6]{0,1:T(8,128)S(1)}, f32[48,6]{0,1:T(8,128)}, u32[]{:S(2)}) copy-start(f32[48,6]{0,1:T(8,128)} %param.13) | copy-start | bytes 3460
Sparse Core Ops, SparseCore 0:
  42.1 42.1 all-gather.4
  86.7 41.3 all-gather.2
  159.1 40.9 reduce-scatter.4
  202.5 43.2 reduce-scatter.2

commit v8 on v7

--- a/solution.py
+++ b/solution.py
@@ -179,20 +179,20 @@
     down_new = adam_update(w_down_use[0], m_down_use[0], v_down_use[0], down_gradient)
     both_back, up_new, down_new = lax.optimization_barrier((both_back, up_new, down_new))
     back_rows = both_back.reshape(2 * row_total, model_width)
-    picked = jnp.dot(
-        (send_row.reshape(pair_count)[:, None] == row_ids[None, :]).astype(jnp.bfloat16),
+    out_hit = send_row[:, :, None] == row_ids[None, None, :]
+    mixed = jnp.dot(
+        jnp.sum(jnp.where(out_hit, gates[:, :, None], 0.0), axis=1),
+        back_rows.astype(jnp.float32),
+        precision=lax.Precision.HIGHEST,
+        preferred_element_type=jnp.float32,
+    ).astype(jnp.bfloat16)
+    input_grad = jnp.dot(
+        jnp.sum((send_row[:, :, None] + capacity == row_ids[None, None, :]).astype(
+            jnp.bfloat16
+        ), axis=1),
         back_rows,
         preferred_element_type=jnp.float32,
-    ).reshape(tok_count, chosen, model_width)
-    mixed = jnp.sum(gates[:, :, None] * picked, axis=1).astype(jnp.bfloat16)
-    picked_grad = jnp.dot(
-        (send_row.reshape(pair_count)[:, None] + capacity == row_ids[None, :]).astype(
-            jnp.bfloat16
-        ),
-        back_rows,
-        preferred_element_type=jnp.float32,
-    ).reshape(tok_count, chosen, model_width)
-    input_grad = jnp.sum(picked_grad, axis=1).astype(jnp.bfloat16)
+    ).astype(jnp.bfloat16)
     return (
         mixed,
         input_grad,

time: 310 us -> 306 us (0.987)
  matrix products: 62.7 us -> 59 us
    dot_general x2, matrix products: 7.5 us -> 3.74 us  [the longest x1 2.4 us: body(): jnp.dot(jnp.sum(jnp.where(out_hit, gates[:, :, None], 0.0), axis=1), back...]
where the time goes in v8:
time: 306 us; the launch traced here: 305 us
  waiting for transfers between devices  185 us (60%)
  matrix products  59 us (19%)
  starting transfers between devices  26 us (8%)
  other arithmetic  17.3 us (6%)
  between operations  14.7 us (5%)
    all_to_all x1, waiting for transfers between devices, body(): lax.all_to_all(send_both.reshape(experts, 2 * capacity, model_width), 'ex...  71.7 us
    ppermute x4, waiting for transfers between devices, partner(): return lax.ppermute(value, axis, pairs)  49.2 us
    all_to_all x1, waiting for transfers between devices, body(): lax.all_to_all((contract_rows(take_token, expert_out) + contract_rows(tak...  44.6 us
    dot_general x4, matrix products, contract_rows(): lax.dot_general(left, right, (((0,), (0,)), ((), ())), preferred_element_...  27.1 us
    reduce_scatter x1, waiting for transfers between devices, body(): lax.psum_scatter(contract_rows(expert_rows, up_grad).astype(jnp.bfloat16)...  19.7 us
    dot_general x2, matrix products, contract_cols(): lax.dot_general(left, right, (((1,), (1,)), ((), ())), preferred_element_...  12.9 us
    all_to_all x1, starting transfers between devices, body(): lax.all_to_all(send_both.reshape(experts, 2 * capacity, model_width), 'ex...  11.3 us
    all_to_all x1, starting transfers between devices, body(): lax.all_to_all((contract_rows(take_token, expert_out) + contract_rows(tak...  9.91 us
  transfers between devices with their start and end apart: 10, of which 7 were waited for; matrix products, arithmetic and copies ran while one was open for 23% of the time, Pallas kernels for 0%

profile of v8, /device:TPU:6, one launch (start us, length us, event | category | flops | bytes accessed | tf_op | source)
XLA Modules:
  0.0 305.4 jit_solution(8983814433233275418)
XLA Ops:
  7.2 2.0 collective-permute-start
  11.6 0.9 reduce-window.6
  13.1 1.3 dynamic_slice.3
  14.8 1.1 select_reduce_fusion
  16.5 1.3 pad_maximum_fusion.1
  17.9 1.3 pad_maximum_fusion
  19.2 2.7 multiply_convert_fusion
  21.9 4.7 %collective-permute-done = bf16[1,256,1408]{2,1,0:T(8,128)(2,1)S(1)} collective-permute-done((bf16[1,256,1408]{2,1,0:T(8,128)(2,1)}, bf16[1,256,1408]{2,1,0:T(8,128)(2,1)S(1)}, u32[]{:S(2)}, u32[]{:S(2)}) %collective-permute-start) | collective-permute-done | bytes 720928 | tf_op jit(solution)/shard_map/ppermute | solution.py:18
  26.5 14.5 %collective-permute-done.1 = bf16[1,176,2048]{2,1,0:T(8,128)(2,1)S(1)} collective-permute-done((bf16[1,176,2048]{2,1,0:T(8,128)(2,1)}, bf16[1,176,2048]{2,1,0:T(8,128)(2,1)S(1)}, u32[]{:S(2)}, u32[]{:S(2)}) %collective-permute-start.1) | collective-permute-done | bytes 720928 | tf_op jit(solution)/shard_map/ppermute | solution.py:18
  41.0 1.0 broadcast_select_fusion
  42.1 0.9 broadcast_select_fusion.1
  43.1 11.3 %all-to-all-start = ((bf16[32,24,2048]{2,1,0:T(8,128)(2,1)}), bf16[32,24,2048]{2,1,0:T(8,128)(2,1)S(1)}, u32[]{:S(2)}, u32[]{:S(2)}) async-start(bf16[32,24,2048]{2,1,0:T(8,128)(2,1)} %bitcast.4), calls=%async_computation | async-start | bytes 6291456 | tf_op jit(solution)/shard_map/all_to_all | solution.py:114
  54.5 1.9 collective-permute-start.2
  56.3 71.7 %all-to-all-done = bf16[32,24,2048]{2,1,0:T(8,128)(2,1)S(1)} async-done(((bf16[32,24,2048]{2,1,0:T(8,128)(2,1)}), bf16[32,24,2048]{2,1,0:T(8,128)(2,1)S(1)}, u32[]{:S(2)}, u32[]{:S(2)}) %all-to-all-start) | async-done | bytes 3145760 | tf_op jit(solution)/shard_map/all_to_all | solution.py:114
  128.1 2.7 convolution_convert_fusion.2
  130.7 2.6 convolution_convert_fusion.3
  133.3 7.3 %multiply_convert_fusion.1 = (bf16[384,1408]{1,0:T(8,128)(2,1)S(1)}, f32[384,1408]{1,0:T(8,128)}) fusion(bf16[384,2048]{1,0:T(8,128)(2,1)} %convolution_convert_fusion.3, bf16[1,2048,1408]{2,1,0:T(8,128)(2,1)} %all-gather.5.cloned.1.call-done), kind=kOutput, calls=%fused_computation.16 | convolution fusion | flops 2217295872 | bytes 10584064 | tf_op jit(solution)/shard_map/dot_general | solution.py:142
  140.6 13.4 %collective-permute-done.2 = bf16[2,256,1408]{2,1,0:T(8,128)(2,1)} collective-permute-done((bf16[2,256,1408]{2,1,0:T(8,128)(2,1)}, bf16[2,256,1408]{2,1,0:T(8,128)(2,1)}, u32[]{:S(2)}, u32[]{:S(2)}) %collective-permute-start.2) | collective-permute-done | bytes 1441824 | tf_op jit(solution)/shard_map/ppermute | solution.py:18
  154.0 5.0 %convolution_convert_fusion = bf16[1408,2048]{1,0:T(8,128)(2,1)} fusion(bf16[384,1408]{1,0:T(8,128)(2,1)S(1)} %get-tuple-element.35, bf16[384,2048]{1,0:T(8,128)(2,1)S(1)} %copy-done.10), kind=kOutput, calls=%fused_computation | convolution fusion | flops 2217476096 | bytes 8421376 | tf_op jit(solution)/shard_map/dot_general | solution.py:44
  159.2 7.2 %fusion.4 = bf16[384,1408]{1,0:T(8,128)(2,1)S(1)} fusion(bf16[384,2048]{1,0:T(8,128)(2,1)S(1)} %copy-done.10, bf16[1408,2048]{1,0:T(8,128)(2,1)} %bitcast.97, f32[384,1408]{1,0:T(8,128)} %get-tuple-element.59), kind=kOutput, calls=%fused_computation.9 | convolution fusion | flops 2219458560 | bytes 10584064 | tf_op jit(solution)/shard_map/dot_general | solution.py:50
  166.5 5.2 %convolution_convert_fusion.1 = bf16[2048,1408]{1,0:T(8,128)(2,1)} fusion(bf16[384,2048]{1,0:T(8,128)(2,1)S(1)} %copy-done.9, bf16[384,1408]{1,0:T(8,128)(2,1)S(1)} %fusion.4), kind=kOutput, calls=%fused_computation.1 | convolution fusion | flops 2217476096 | bytes 8421376 | tf_op jit(solution)/shard_map/dot_general | solution.py:44
  172.2 5.7 %fusion.5 = bf16[384,2048]{1,0:T(8,128)(2,1)S(1)} fusion(bf16[384,1408]{1,0:T(8,128)(2,1)} %copy-done.12, bf16[1,2048,1408]{2,1,0:T(8,128)(2,1)} %all-gather.5.cloned.1.call-done), kind=kOutput, calls=%fused_computation.12 | convolution fusion | flops 2215378944 | bytes 8421376 | tf_op jit(solution)/shard_map/dot_general | solution.py:50
  177.9 10.0 %fusion.10 = f32[768,2048]{1,0:T(8,128)} fusion(bf16[384,1408]{1,0:T(8,128)(2,1)} %copy-done.11, bf16[1408,2048]{1,0:T(8,128)(2,1)} %bitcast.98, s32[768]{0:T(1024)S(1)} %iota.33, s32[384]{0:T(512)S(1)} %get-tuple-element.51), kind=kOutput, calls=%fused_computation.24 | convolution fusion | flops 3423633408 | bytes 13144576 | tf_op jit(solution)/shard_map/dot_general | solution.py:44
  187.9 16.7 %collective-permute-done.3 = bf16[2,176,2048]{2,1,0:T(8,128)(2,1)S(1)} collective-permute-done((bf16[2,176,2048]{2,1,0:T(8,128)(2,1)}, bf16[2,176,2048]{2,1,0:T(8,128)(2,1)S(1)}, u32[]{:S(2)}, u32[]{:S(2)}) %collective-permute-start.3) | collective-permute-done | bytes 1441824 | tf_op jit(solution)/shard_map/ppermute | solution.py:18
  204.5 6.9 %add_convert_fusion = bf16[768,2048]{1,0:T(8,128)(2,1)} fusion(f32[768,2048]{1,0:T(8,128)} %fusion.10, bf16[384,2048]{1,0:T(8,128)(2,1)S(1)} %fusion.5, s32[768]{0:T(1024)S(1)} %iota.33, s32[384]{0:T(512)S(1)} %get-tuple-element.50), kind=kOutput, calls=%fused_computation.2 | convolution fusion | flops 1211400192 | bytes 11014656 | tf_op jit(solution)/shard_map/dot_general | solution.py:44
  211.5 9.9 %all-to-all-start.1 = ((bf16[32,24,2048]{2,1,0:T(8,128)(2,1)}), bf16[32,24,2048]{2,1,0:T(8,128)(2,1)S(1)}, u32[]{:S(2)}, u32[]{:S(2)}) async-start(bf16[32,24,2048]{2,1,0:T(8,128)(2,1)} %bitcast.87), calls=%async_computation.1 | async-start | bytes 6291456 | tf_op jit(solution)/shard_map/all_to_all | solution.py:153
  221.4 4.7 %fusion.21 = (bf16[176,2048]{1,0:T(8,128)(2,1)}, bf16[176,2048]{1,0:T(8,128)(2,1)}, bf16[176,2048]{1,0:T(8,128)(2,1)}) fusion(bf16[176,2048]{1,0:T(8,128)(2,1)} %reduce-scatter.5.cloned.1.call-done, bf16[1,176,2048]{2,1,0:T(8,128)(2,1)} %param.21, bf16[2,176,2048]{2,1,0:T(8,128)(2,1)} %copy-done.4, pred[]{:T(512)} %bitcast.2, ...), kind=kLoop, calls=%fused_computation.39 | loop fusion | flops 7569408 | bytes 6488065 | tf_op jit(solution)/shard_map/convert_element_type | solution.py:39
  226.1 19.7 %reduce-scatter.3.cloned.1.call-done = bf16[256,1408]{1,0:T(8,128)(2,1)} async-done(((bf16[2048,1408]{1,0:T(8,128)(2,1)}), bf16[256,1408]{1,0:T(8,128)(2,1)}) %reduce-scatter.3.cloned.1.call-update) | async-done | bytes 720912 | tf_op jit(solution)/shard_map/reduce_scatter | solution.py:162
  245.8 4.7 %fusion.22 = (bf16[256,1408]{1,0:T(8,128)(2,1)}, bf16[256,1408]{1,0:T(8,128)(2,1)}, bf16[256,1408]{1,0:T(8,128)(2,1)}) fusion(bf16[256,1408]{1,0:T(8,128)(2,1)} %reduce-scatter.3.cloned.1.call-done, bf16[1,256,1408]{2,1,0:T(8,128)(2,1)} %param.19, bf16[2,256,1408]{2,1,0:T(8,128)(2,1)} %collective-permute-done.2, pred[]{:T(512)} %bitcast.2, ...), kind=kLoop, calls=%fused_computation.40 | loop fusion | flops 7569408 | bytes 6488065 | tf_op jit(solution)/shard_map/convert_element_type | solution.py:39
  250.5 44.6 %all-to-all-done.1 = bf16[32,24,2048]{2,1,0:T(8,128)(2,1)S(1)} async-done(((bf16[32,24,2048]{2,1,0:T(8,128)(2,1)}), bf16[32,24,2048]{2,1,0:T(8,128)(2,1)S(1)}, u32[]{:S(2)}, u32[]{:S(2)}) %all-to-all-start.1) | async-done | bytes 3145760 | tf_op jit(solution)/shard_map/all_to_all | solution.py:153
  295.1 1.3 convolution_convert_fusion.5
  296.4 2.4 convolution_convert_fusion.6
  (65 shorter events, 4.3 us)
Async XLA Ops:
  7.2 9.3 %copy-start = (bf16[1,176,2048]{2,1,0:T(8,128)(2,1)S(1)}, bf16[1,176,2048]{2,1,0:T(8,128)(2,1)}, u32[]{:S(2)}) copy-start(bf16[1,176,2048]{2,1,0:T(8,128)(2,1)} %param.21) | copy-start | bytes 2162692
  7.2 9.3 %copy-start.1 = (bf16[1,176,2048]{2,1,0:T(8,128)(2,1)S(1)}, bf16[1,176,2048]{2,1,0:T(8,128)(2,1)}, u32[]{:S(2)}) copy-start(bf16[1,176,2048]{2,1,0:T(8,128)(2,1)} %param.20) | copy-start | bytes 2162692
  7.2 126.1 %all-gather.5.cloned.1.call-start = ((), (), s32[]{:S(2)}) async-start(), calls=%async_computation.5 | async-start | bytes 6488064 | tf_op jit(solution)/shard_map/all_gather | solution.py:124
  7.2 19.3 %collective-permute-start = (bf16[1,256,1408]{2,1,0:T(8,128)(2,1)}, bf16[1,256,1408]{2,1,0:T(8,128)(2,1)S(1)}, u32[]{:S(2)}, u32[]{:S(2)}) collective-permute-start(bf16[1,256,1408]{2,1,0:T(8,128)(2,1)} %param.16), channel_id=1, source_target_pairs={{0,1},{1,0},{2,3},{3,2},{4,5},{5,4},{6,7},{7,6},{8,9},{9,8},{10,11... | collective-permute-start | bytes 2162696 | tf_op jit(solution)/shard_map/ppermute | solution.py:18
  9.2 31.8 %collective-permute-start.1 = (bf16[1,176,2048]{2,1,0:T(8,128)(2,1)}, bf16[1,176,2048]{2,1,0:T(8,128)(2,1)S(1)}, u32[]{:S(2)}, u32[]{:S(2)}) collective-permute-start(bf16[1,176,2048]{2,1,0:T(8,128)(2,1)} %param.17), channel_id=1, source_target_pairs={{0,1},{1,0},{2,3},{3,2},{4,5},{5,4},{6,7},{7,6},{8,9},{9,8},{10,11... | collective-permute-start | bytes 2162696 | tf_op jit(solution)/shard_map/ppermute | solution.py:18
  14.7 3.1 %copy-start.2 = (bf16[1,256,1408]{2,1,0:T(8,128)(2,1)S(1)}, bf16[1,256,1408]{2,1,0:T(8,128)(2,1)}, u32[]{:S(2)}) copy-start(bf16[1,256,1408]{2,1,0:T(8,128)(2,1)} %param.19) | copy-start | bytes 2162692
  14.7 3.1 %copy-start.3 = (bf16[1,256,1408]{2,1,0:T(8,128)(2,1)S(1)}, bf16[1,256,1408]{2,1,0:T(8,128)(2,1)}, u32[]{:S(2)}) copy-start(bf16[1,256,1408]{2,1,0:T(8,128)(2,1)} %param.18) | copy-start | bytes 2162692
  17.9 1.3 copy-start.7
  17.9 1.3 copy-start.8
  19.2 21.9 %copy-start.5 = (bf16[1,256,1408]{2,1,0:T(8,128)(2,1)S(1)}, bf16[1,256,1408]{2,1,0:T(8,128)(2,1)}, u32[]{:S(2)}) copy-start(bf16[1,256,1408]{2,1,0:T(8,128)(2,1)} %param.16) | copy-start | bytes 2162692
  21.9 20.2 %copy-start.6 = (bf16[1,176,2048]{2,1,0:T(8,128)(2,1)S(1)}, bf16[1,176,2048]{2,1,0:T(8,128)(2,1)}, u32[]{:S(2)}) copy-start(bf16[1,176,2048]{2,1,0:T(8,128)(2,1)} %param.17) | copy-start | bytes 2162692
  42.0 111.9 %all-gather.3.cloned.1.call-start = ((), (), s32[]{:S(2)}) async-start(), calls=%async_computation.4 | async-start | bytes 6488064 | tf_op jit(solution)/shard_map/all_gather | solution.py:125
  43.1 85.0 %all-to-all-start = ((bf16[32,24,2048]{2,1,0:T(8,128)(2,1)}), bf16[32,24,2048]{2,1,0:T(8,128)(2,1)S(1)}, u32[]{:S(2)}, u32[]{:S(2)}) async-start(bf16[32,24,2048]{2,1,0:T(8,128)(2,1)} %bitcast.4), calls=%async_computation | async-start | bytes 6291456 | tf_op jit(solution)/shard_map/all_to_all | solution.py:114
  54.4 167.0 %reduce-scatter.5.cloned.1.call-start = ((), (), s32[]{:S(2)}) async-start(), calls=%async_computation.7 | async-start | bytes 6488064 | tf_op jit(solution)/shard_map/reduce_scatter | solution.py:168
  54.5 99.5 %collective-permute-start.2 = (bf16[2,256,1408]{2,1,0:T(8,128)(2,1)}, bf16[2,256,1408]{2,1,0:T(8,128)(2,1)}, u32[]{:S(2)}, u32[]{:S(2)}) collective-permute-start(bf16[2,256,1408]{2,1,0:T(8,128)(2,1)} %pad_maximum_fusion), channel_id=1, source_target_pairs={{0,1},{1,0},{2,3},{3,2},{4,5},{5,4},{6,7},{7,6},{8,9},{9,8},{10,11... | collective-permute-start | bytes 4325384 | tf_op jit(solution)/shard_map/ppermute | solution.py:18
  133.3 20.7 %copy-start.10 = (bf16[384,2048]{1,0:T(8,128)(2,1)S(1)}, bf16[384,2048]{1,0:T(8,128)(2,1)}, u32[]{:S(2)}) copy-start(bf16[384,2048]{1,0:T(8,128)(2,1)} %convolution_convert_fusion.2) | copy-start | bytes 4718596
  140.6 18.4 %copy-start.11 = (bf16[384,1408]{1,0:T(8,128)(2,1)}, bf16[384,1408]{1,0:T(8,128)(2,1)S(1)}, u32[]{:S(2)}) copy-start(bf16[384,1408]{1,0:T(8,128)(2,1)S(1)} %get-tuple-element.35) | copy-start | bytes 3244036
  159.0 86.8 %reduce-scatter.3.cloned.1.call-start = ((), (), s32[]{:S(2)}) async-start(), calls=%async_computation.6 | async-start | bytes 6488064 | tf_op jit(solution)/shard_map/reduce_scatter | solution.py:162
  159.2 7.3 %copy-start.9 = (bf16[384,2048]{1,0:T(8,128)(2,1)S(1)}, bf16[384,2048]{1,0:T(8,128)(2,1)}, u32[]{:S(2)}) copy-start(bf16[384,2048]{1,0:T(8,128)(2,1)} %convolution_convert_fusion.3) | copy-start | bytes 4718596
  166.5 5.2 %copy-start.12 = (bf16[384,1408]{1,0:T(8,128)(2,1)}, bf16[384,1408]{1,0:T(8,128)(2,1)S(1)}, u32[]{:S(2)}) copy-start(bf16[384,1408]{1,0:T(8,128)(2,1)S(1)} %fusion.4) | copy-start | bytes 3244036
  171.7 32.8 %collective-permute-start.3 = (bf16[2,176,2048]{2,1,0:T(8,128)(2,1)}, bf16[2,176,2048]{2,1,0:T(8,128)(2,1)S(1)}, u32[]{:S(2)}, u32[]{:S(2)}) collective-permute-start(bf16[2,176,2048]{2,1,0:T(8,128)(2,1)} %pad_maximum_fusion.1), channel_id=1, source_target_pairs={{0,1},{1,0},{2,3},{3,2},{4,5},{5,4},{6,7},{7,6},{8,9},{9,8},{10,11... | collective-permute-start | bytes 4325384 | tf_op jit(solution)/shard_map/ppermute | solution.py:18
  204.5 6.9 %copy-start.4 = (bf16[2,176,2048]{2,1,0:T(8,128)(2,1)}, bf16[2,176,2048]{2,1,0:T(8,128)(2,1)S(1)}, u32[]{:S(2)}) copy-start(bf16[2,176,2048]{2,1,0:T(8,128)(2,1)S(1)} %collective-permute-done.3) | copy-start | bytes 4325380
  211.5 83.6 %all-to-all-start.1 = ((bf16[32,24,2048]{2,1,0:T(8,128)(2,1)}), bf16[32,24,2048]{2,1,0:T(8,128)(2,1)S(1)}, u32[]{:S(2)}, u32[]{:S(2)}) async-start(bf16[32,24,2048]{2,1,0:T(8,128)(2,1)} %bitcast.87), calls=%async_computation.1 | async-start | bytes 6291456 | tf_op jit(solution)/shard_map/all_to_all | solution.py:153
Sparse Core Ops, SparseCore 0:
  42.2 42.1 all-gather.4
  86.7 41.3 all-gather.2
  159.1 40.9 reduce-scatter.4
  202.5 43.2 reduce-scatter.2

commit v9 on v8

--- a/solution.py
+++ b/solution.py
@@ -141,8 +141,10 @@
     )
     up_act = jnp.dot(expert_rows, up_full, preferred_element_type=jnp.float32)
     hidden = jax.nn.silu(up_act).astype(jnp.bfloat16)
-    down_full, hidden, up_moments, down_local = lax.optimization_barrier(
-        (down_full, hidden, up_moments, down_local)
+    down_full, hidden = lax.optimization_barrier((down_full, hidden))
+    down_part = contract_rows(hidden, grad_rows).astype(jnp.bfloat16)
+    down_part, up_moments, down_local = lax.optimization_barrier(
+        (down_part, up_moments, down_local)
     )
     down_moments = partner(down_local, "expert", 0)
     expert_out = jnp.dot(hidden, down_full, preferred_element_type=jnp.float32).astype(jnp.bfloat16)
@@ -166,7 +168,7 @@
         tiled=True,
     ).astype(jnp.float32)
     down_gradient = lax.psum_scatter(
-        contract_rows(hidden, grad_rows).astype(jnp.bfloat16),
+        down_part,
         "dp",
         scatter_dimension=0,
         tiled=True,

time: 306 us -> 301 us (0.984)
  waiting for transfers between devices: 185 us -> 180 us
    ppermute x4, waiting for transfers between devices: 49.2 us -> 44.2 us  [partner(): return lax.ppermute(value, axis, pairs)]
  transfers between devices with their start and end apart: 10 -> 10, of which waited for: 7 -> 7; matrix products, arithmetic and copies ran while one was open for 23% -> 25% of each run, Pallas kernels for 0% -> 0%
where the time goes in v9:
time: 301 us; the launch traced here: 300 us
  waiting for transfers between devices  180 us (60%)
  matrix products  59 us (20%)
  starting transfers between devices  26 us (9%)
  other arithmetic  17.3 us (6%)
  between operations  14.7 us (5%)
  local copies, waits for them, and re-layouts  3.05 us (1%)
    all_to_all x1, waiting for transfers between devices, body(): lax.all_to_all(send_both.reshape(experts, 2 * capacity, model_width), 'ex...  71.7 us
    all_to_all x1, waiting for transfers between devices, body(): lax.all_to_all((contract_rows(take_token, expert_out) + contract_rows(tak...  44.6 us
    ppermute x4, waiting for transfers between devices, partner(): return lax.ppermute(value, axis, pairs)  44.2 us
    dot_general x4, matrix products, contract_rows(): lax.dot_general(left, right, (((0,), (0,)), ((), ())), preferred_element_...  27.1 us
    reduce_scatter x1, waiting for transfers between devices, body(): lax.psum_scatter(contract_rows(expert_rows, up_grad).astype(jnp.bfloat16)...  19.7 us
    dot_general x2, matrix products, contract_cols(): lax.dot_general(left, right, (((1,), (1,)), ((), ())), preferred_element_...  12.9 us
    all_to_all x1, starting transfers between devices, body(): lax.all_to_all(send_both.reshape(experts, 2 * capacity, model_width), 'ex...  11.3 us
    all_to_all x1, starting transfers between devices, body(): lax.all_to_all((contract_rows(take_token, expert_out) + contract_rows(tak...  9.92 us
  transfers between devices with their start and end apart: 10, of which 7 were waited for; matrix products, arithmetic and copies ran while one was open for 25% of the time, Pallas kernels for 0%

profile of v9, /device:TPU:6, one launch (start us, length us, event | category | flops | bytes accessed | tf_op | source)
XLA Modules:
  0.0 300.4 jit_solution(7027428484316237911)
XLA Ops:
  7.2 2.0 collective-permute-start
  11.6 0.9 reduce-window.6
  13.1 1.3 dynamic_slice.3
  14.8 1.1 select_reduce_fusion
  16.5 1.3 pad_maximum_fusion.1
  17.9 1.3 pad_maximum_fusion
  19.2 2.7 multiply_convert_fusion
  21.9 4.7 %collective-permute-done = bf16[1,256,1408]{2,1,0:T(8,128)(2,1)S(1)} collective-permute-done((bf16[1,256,1408]{2,1,0:T(8,128)(2,1)}, bf16[1,256,1408]{2,1,0:T(8,128)(2,1)S(1)}, u32[]{:S(2)}, u32[]{:S(2)}) %collective-permute-start) | collective-permute-done | bytes 720928 | tf_op jit(solution)/shard_map/ppermute | solution.py:18
  26.5 14.5 %collective-permute-done.1 = bf16[1,176,2048]{2,1,0:T(8,128)(2,1)S(1)} collective-permute-done((bf16[1,176,2048]{2,1,0:T(8,128)(2,1)}, bf16[1,176,2048]{2,1,0:T(8,128)(2,1)S(1)}, u32[]{:S(2)}, u32[]{:S(2)}) %collective-permute-start.1) | collective-permute-done | bytes 720928 | tf_op jit(solution)/shard_map/ppermute | solution.py:18
  41.0 1.0 broadcast_select_fusion
  42.1 0.9 broadcast_select_fusion.1
  43.1 11.3 %all-to-all-start = ((bf16[32,24,2048]{2,1,0:T(8,128)(2,1)}), bf16[32,24,2048]{2,1,0:T(8,128)(2,1)S(1)}, u32[]{:S(2)}, u32[]{:S(2)}) async-start(bf16[32,24,2048]{2,1,0:T(8,128)(2,1)} %bitcast.4), calls=%async_computation | async-start | bytes 6291456 | tf_op jit(solution)/shard_map/all_to_all | solution.py:114
  54.5 1.9 collective-permute-start.2
  56.3 71.7 %all-to-all-done = bf16[32,24,2048]{2,1,0:T(8,128)(2,1)S(1)} async-done(((bf16[32,24,2048]{2,1,0:T(8,128)(2,1)}), bf16[32,24,2048]{2,1,0:T(8,128)(2,1)S(1)}, u32[]{:S(2)}, u32[]{:S(2)}) %all-to-all-start) | async-done | bytes 3145760 | tf_op jit(solution)/shard_map/all_to_all | solution.py:114
  128.1 2.7 convolution_convert_fusion.2
  130.7 2.6 convolution_convert_fusion.3
  133.3 7.3 %multiply_convert_fusion.1 = (bf16[384,1408]{1,0:T(8,128)(2,1)S(1)}, f32[384,1408]{1,0:T(8,128)}) fusion(bf16[384,2048]{1,0:T(8,128)(2,1)} %convolution_convert_fusion.3, bf16[1,2048,1408]{2,1,0:T(8,128)(2,1)} %all-gather.5.cloned.1.call-done), kind=kOutput, calls=%fused_computation.16 | convolution fusion | flops 2217295872 | bytes 10584064 | tf_op jit(solution)/shard_map/dot_general | solution.py:142
  140.6 5.0 %convolution_convert_fusion.1 = bf16[1408,2048]{1,0:T(8,128)(2,1)} fusion(bf16[384,1408]{1,0:T(8,128)(2,1)S(1)} %get-tuple-element.34, bf16[384,2048]{1,0:T(8,128)(2,1)S(1)} %copy-done.10), kind=kOutput, calls=%fused_computation.1 | convolution fusion | flops 2217476096 | bytes 8421376 | tf_op jit(solution)/shard_map/dot_general | solution.py:44
  145.6 8.4 %collective-permute-done.2 = bf16[2,256,1408]{2,1,0:T(8,128)(2,1)} collective-permute-done((bf16[2,256,1408]{2,1,0:T(8,128)(2,1)}, bf16[2,256,1408]{2,1,0:T(8,128)(2,1)}, u32[]{:S(2)}, u32[]{:S(2)}) %collective-permute-start.2) | collective-permute-done | bytes 1441824 | tf_op jit(solution)/shard_map/ppermute | solution.py:18
  154.2 7.2 %fusion.4 = bf16[384,1408]{1,0:T(8,128)(2,1)S(1)} fusion(bf16[384,2048]{1,0:T(8,128)(2,1)S(1)} %copy-done.10, bf16[1408,2048]{1,0:T(8,128)(2,1)} %bitcast.97, f32[384,1408]{1,0:T(8,128)} %get-tuple-element.61), kind=kOutput, calls=%fused_computation.9 | convolution fusion | flops 2219458560 | bytes 10584064 | tf_op jit(solution)/shard_map/dot_general | solution.py:50
  161.5 5.2 %convolution_convert_fusion = bf16[2048,1408]{1,0:T(8,128)(2,1)} fusion(bf16[384,2048]{1,0:T(8,128)(2,1)S(1)} %copy-done.9, bf16[384,1408]{1,0:T(8,128)(2,1)S(1)} %fusion.4), kind=kOutput, calls=%fused_computation | convolution fusion | flops 2217476096 | bytes 8421376 | tf_op jit(solution)/shard_map/dot_general | solution.py:44
  167.2 5.7 %fusion.5 = bf16[384,2048]{1,0:T(8,128)(2,1)S(1)} fusion(bf16[384,1408]{1,0:T(8,128)(2,1)} %copy-done.12, bf16[1,2048,1408]{2,1,0:T(8,128)(2,1)} %all-gather.5.cloned.1.call-done), kind=kOutput, calls=%fused_computation.12 | convolution fusion | flops 2215378944 | bytes 8421376 | tf_op jit(solution)/shard_map/dot_general | solution.py:50
  172.9 10.0 %fusion.10 = f32[768,2048]{1,0:T(8,128)} fusion(bf16[384,1408]{1,0:T(8,128)(2,1)} %copy-done.11, bf16[1408,2048]{1,0:T(8,128)(2,1)} %bitcast.98, s32[768]{0:T(1024)S(1)} %iota.33, s32[384]{0:T(512)S(1)} %get-tuple-element.53), kind=kOutput, calls=%fused_computation.24 | convolution fusion | flops 3423633408 | bytes 13144576 | tf_op jit(solution)/shard_map/dot_general | solution.py:44
  182.9 16.7 %collective-permute-done.3 = bf16[2,176,2048]{2,1,0:T(8,128)(2,1)S(1)} collective-permute-done((bf16[2,176,2048]{2,1,0:T(8,128)(2,1)}, bf16[2,176,2048]{2,1,0:T(8,128)(2,1)S(1)}, u32[]{:S(2)}, u32[]{:S(2)}) %collective-permute-start.3) | collective-permute-done | bytes 1441824 | tf_op jit(solution)/shard_map/ppermute | solution.py:18
  199.6 6.9 %add_convert_fusion = bf16[768,2048]{1,0:T(8,128)(2,1)} fusion(f32[768,2048]{1,0:T(8,128)} %fusion.10, bf16[384,2048]{1,0:T(8,128)(2,1)S(1)} %fusion.5, s32[768]{0:T(1024)S(1)} %iota.33, s32[384]{0:T(512)S(1)} %get-tuple-element.52), kind=kOutput, calls=%fused_computation.2 | convolution fusion | flops 1211400192 | bytes 11014656 | tf_op jit(solution)/shard_map/dot_general | solution.py:44
  206.5 9.9 %all-to-all-start.1 = ((bf16[32,24,2048]{2,1,0:T(8,128)(2,1)}), bf16[32,24,2048]{2,1,0:T(8,128)(2,1)S(1)}, u32[]{:S(2)}, u32[]{:S(2)}) async-start(bf16[32,24,2048]{2,1,0:T(8,128)(2,1)} %bitcast.87), calls=%async_computation.1 | async-start | bytes 6291456 | tf_op jit(solution)/shard_map/all_to_all | solution.py:155
  216.5 4.7 %fusion.21 = (bf16[176,2048]{1,0:T(8,128)(2,1)}, bf16[176,2048]{1,0:T(8,128)(2,1)}, bf16[176,2048]{1,0:T(8,128)(2,1)}) fusion(bf16[176,2048]{1,0:T(8,128)(2,1)} %reduce-scatter.5.cloned.1.call-done, bf16[1,176,2048]{2,1,0:T(8,128)(2,1)} %param.21, bf16[2,176,2048]{2,1,0:T(8,128)(2,1)} %copy-done.4, pred[]{:T(512)} %bitcast.2, ...), kind=kLoop, calls=%fused_computation.39 | loop fusion | flops 7569408 | bytes 6488065 | tf_op jit(solution)/shard_map/convert_element_type | solution.py:39
  221.1 19.7 %reduce-scatter.3.cloned.1.call-done = bf16[256,1408]{1,0:T(8,128)(2,1)} async-done(((bf16[2048,1408]{1,0:T(8,128)(2,1)}), bf16[256,1408]{1,0:T(8,128)(2,1)}) %reduce-scatter.3.cloned.1.call-update) | async-done | bytes 720912 | tf_op jit(solution)/shard_map/reduce_scatter | solution.py:164
  240.9 4.7 %fusion.22 = (bf16[256,1408]{1,0:T(8,128)(2,1)}, bf16[256,1408]{1,0:T(8,128)(2,1)}, bf16[256,1408]{1,0:T(8,128)(2,1)}) fusion(bf16[256,1408]{1,0:T(8,128)(2,1)} %reduce-scatter.3.cloned.1.call-done, bf16[1,256,1408]{2,1,0:T(8,128)(2,1)} %param.19, bf16[2,256,1408]{2,1,0:T(8,128)(2,1)} %collective-permute-done.2, pred[]{:T(512)} %bitcast.2, ...), kind=kLoop, calls=%fused_computation.40 | loop fusion | flops 7569408 | bytes 6488065 | tf_op jit(solution)/shard_map/convert_element_type | solution.py:39
  245.6 44.6 %all-to-all-done.1 = bf16[32,24,2048]{2,1,0:T(8,128)(2,1)S(1)} async-done(((bf16[32,24,2048]{2,1,0:T(8,128)(2,1)}), bf16[32,24,2048]{2,1,0:T(8,128)(2,1)S(1)}, u32[]{:S(2)}, u32[]{:S(2)}) %all-to-all-start.1) | async-done | bytes 3145760 | tf_op jit(solution)/shard_map/all_to_all | solution.py:155
  290.2 1.3 convolution_convert_fusion.5
  291.5 2.4 convolution_convert_fusion.6
  (65 shorter events, 4.3 us)
Async XLA Ops:
  7.2 9.3 %copy-start = (bf16[1,176,2048]{2,1,0:T(8,128)(2,1)S(1)}, bf16[1,176,2048]{2,1,0:T(8,128)(2,1)}, u32[]{:S(2)}) copy-start(bf16[1,176,2048]{2,1,0:T(8,128)(2,1)} %param.21) | copy-start | bytes 2162692
  7.2 9.3 %copy-start.1 = (bf16[1,176,2048]{2,1,0:T(8,128)(2,1)S(1)}, bf16[1,176,2048]{2,1,0:T(8,128)(2,1)}, u32[]{:S(2)}) copy-start(bf16[1,176,2048]{2,1,0:T(8,128)(2,1)} %param.20) | copy-start | bytes 2162692
  7.2 126.1 %all-gather.5.cloned.1.call-start = ((), (), s32[]{:S(2)}) async-start(), calls=%async_computation.5 | async-start | bytes 6488064 | tf_op jit(solution)/shard_map/all_gather | solution.py:124
  7.2 19.3 %collective-permute-start = (bf16[1,256,1408]{2,1,0:T(8,128)(2,1)}, bf16[1,256,1408]{2,1,0:T(8,128)(2,1)S(1)}, u32[]{:S(2)}, u32[]{:S(2)}) collective-permute-start(bf16[1,256,1408]{2,1,0:T(8,128)(2,1)} %param.16), channel_id=1, source_target_pairs={{0,1},{1,0},{2,3},{3,2},{4,5},{5,4},{6,7},{7,6},{8,9},{9,8},{10,11... | collective-permute-start | bytes 2162696 | tf_op jit(solution)/shard_map/ppermute | solution.py:18
  9.2 31.8 %collective-permute-start.1 = (bf16[1,176,2048]{2,1,0:T(8,128)(2,1)}, bf16[1,176,2048]{2,1,0:T(8,128)(2,1)S(1)}, u32[]{:S(2)}, u32[]{:S(2)}) collective-permute-start(bf16[1,176,2048]{2,1,0:T(8,128)(2,1)} %param.17), channel_id=1, source_target_pairs={{0,1},{1,0},{2,3},{3,2},{4,5},{5,4},{6,7},{7,6},{8,9},{9,8},{10,11... | collective-permute-start | bytes 2162696 | tf_op jit(solution)/shard_map/ppermute | solution.py:18
  14.7 3.1 %copy-start.2 = (bf16[1,256,1408]{2,1,0:T(8,128)(2,1)S(1)}, bf16[1,256,1408]{2,1,0:T(8,128)(2,1)}, u32[]{:S(2)}) copy-start(bf16[1,256,1408]{2,1,0:T(8,128)(2,1)} %param.19) | copy-start | bytes 2162692
  14.7 3.1 %copy-start.3 = (bf16[1,256,1408]{2,1,0:T(8,128)(2,1)S(1)}, bf16[1,256,1408]{2,1,0:T(8,128)(2,1)}, u32[]{:S(2)}) copy-start(bf16[1,256,1408]{2,1,0:T(8,128)(2,1)} %param.18) | copy-start | bytes 2162692
  17.9 1.3 copy-start.7
  17.9 1.3 copy-start.8
  19.2 21.9 %copy-start.5 = (bf16[1,256,1408]{2,1,0:T(8,128)(2,1)S(1)}, bf16[1,256,1408]{2,1,0:T(8,128)(2,1)}, u32[]{:S(2)}) copy-start(bf16[1,256,1408]{2,1,0:T(8,128)(2,1)} %param.16) | copy-start | bytes 2162692
  21.9 20.2 %copy-start.6 = (bf16[1,176,2048]{2,1,0:T(8,128)(2,1)S(1)}, bf16[1,176,2048]{2,1,0:T(8,128)(2,1)}, u32[]{:S(2)}) copy-start(bf16[1,176,2048]{2,1,0:T(8,128)(2,1)} %param.17) | copy-start | bytes 2162692
  42.0 98.5 %all-gather.3.cloned.1.call-start = ((), (), s32[]{:S(2)}) async-start(), calls=%async_computation.4 | async-start | bytes 6488064 | tf_op jit(solution)/shard_map/all_gather | solution.py:125
  43.1 85.0 %all-to-all-start = ((bf16[32,24,2048]{2,1,0:T(8,128)(2,1)}), bf16[32,24,2048]{2,1,0:T(8,128)(2,1)S(1)}, u32[]{:S(2)}, u32[]{:S(2)}) async-start(bf16[32,24,2048]{2,1,0:T(8,128)(2,1)} %bitcast.4), calls=%async_computation | async-start | bytes 6291456 | tf_op jit(solution)/shard_map/all_to_all | solution.py:114
  54.4 162.1 %reduce-scatter.5.cloned.1.call-start = ((), (), s32[]{:S(2)}) async-start(), calls=%async_computation.7 | async-start | bytes 6488064 | tf_op jit(solution)/shard_map/reduce_scatter | solution.py:170
  54.5 99.5 %collective-permute-start.2 = (bf16[2,256,1408]{2,1,0:T(8,128)(2,1)}, bf16[2,256,1408]{2,1,0:T(8,128)(2,1)}, u32[]{:S(2)}, u32[]{:S(2)}) collective-permute-start(bf16[2,256,1408]{2,1,0:T(8,128)(2,1)} %pad_maximum_fusion), channel_id=1, source_target_pairs={{0,1},{1,0},{2,3},{3,2},{4,5},{5,4},{6,7},{7,6},{8,9},{9,8},{10,11... | collective-permute-start | bytes 4325384 | tf_op jit(solution)/shard_map/ppermute | solution.py:18
  133.3 7.3 %copy-start.10 = (bf16[384,2048]{1,0:T(8,128)(2,1)S(1)}, bf16[384,2048]{1,0:T(8,128)(2,1)}, u32[]{:S(2)}) copy-start(bf16[384,2048]{1,0:T(8,128)(2,1)} %convolution_convert_fusion.2) | copy-start | bytes 4718596
  140.6 5.0 %copy-start.11 = (bf16[384,1408]{1,0:T(8,128)(2,1)}, bf16[384,1408]{1,0:T(8,128)(2,1)S(1)}, u32[]{:S(2)}) copy-start(bf16[384,1408]{1,0:T(8,128)(2,1)S(1)} %get-tuple-element.34) | copy-start | bytes 3244036
  154.0 86.9 %reduce-scatter.3.cloned.1.call-start = ((), (), s32[]{:S(2)}) async-start(), calls=%async_computation.6 | async-start | bytes 6488064 | tf_op jit(solution)/shard_map/reduce_scatter | solution.py:164
  154.2 7.3 %copy-start.9 = (bf16[384,2048]{1,0:T(8,128)(2,1)S(1)}, bf16[384,2048]{1,0:T(8,128)(2,1)}, u32[]{:S(2)}) copy-start(bf16[384,2048]{1,0:T(8,128)(2,1)} %convolution_convert_fusion.3) | copy-start | bytes 4718596
  161.5 5.2 %copy-start.12 = (bf16[384,1408]{1,0:T(8,128)(2,1)}, bf16[384,1408]{1,0:T(8,128)(2,1)S(1)}, u32[]{:S(2)}) copy-start(bf16[384,1408]{1,0:T(8,128)(2,1)S(1)} %fusion.4) | copy-start | bytes 3244036
  166.7 32.8 %collective-permute-start.3 = (bf16[2,176,2048]{2,1,0:T(8,128)(2,1)}, bf16[2,176,2048]{2,1,0:T(8,128)(2,1)S(1)}, u32[]{:S(2)}, u32[]{:S(2)}) collective-permute-start(bf16[2,176,2048]{2,1,0:T(8,128)(2,1)} %pad_maximum_fusion.1), channel_id=1, source_target_pairs={{0,1},{1,0},{2,3},{3,2},{4,5},{5,4},{6,7},{7,6},{8,9},{9,8},{10,11... | collective-permute-start | bytes 4325384 | tf_op jit(solution)/shard_map/ppermute | solution.py:18
  199.6 6.9 %copy-start.4 = (bf16[2,176,2048]{2,1,0:T(8,128)(2,1)}, bf16[2,176,2048]{2,1,0:T(8,128)(2,1)S(1)}, u32[]{:S(2)}) copy-start(bf16[2,176,2048]{2,1,0:T(8,128)(2,1)S(1)} %collective-permute-done.3) | copy-start | bytes 4325380
  206.5 83.7 %all-to-all-start.1 = ((bf16[32,24,2048]{2,1,0:T(8,128)(2,1)}), bf16[32,24,2048]{2,1,0:T(8,128)(2,1)S(1)}, u32[]{:S(2)}, u32[]{:S(2)}) async-start(bf16[32,24,2048]{2,1,0:T(8,128)(2,1)} %bitcast.87), calls=%async_computation.1 | async-start | bytes 6291456 | tf_op jit(solution)/shard_map/all_to_all | solution.py:155
Sparse Core Ops, SparseCore 0:
  42.2 42.1 all-gather.4
  86.7 41.3 all-gather.2
  154.1 40.9 reduce-scatter.4
  197.5 43.2 reduce-scatter.2

commit v10 on v9

--- a/solution.py
+++ b/solution.py
@@ -182,10 +182,14 @@
     both_back, up_new, down_new = lax.optimization_barrier((both_back, up_new, down_new))
     back_rows = both_back.reshape(2 * row_total, model_width)
     out_hit = send_row[:, :, None] == row_ids[None, None, :]
+    gate_rows = jnp.sum(jnp.where(out_hit, gates[:, :, None], 0.0), axis=1)
+    gate_hi = gate_rows.astype(jnp.bfloat16)
+    gate_rest = gate_rows - gate_hi.astype(jnp.float32)
+    gate_mid = gate_rest.astype(jnp.bfloat16)
+    gate_lo = (gate_rest - gate_mid.astype(jnp.float32)).astype(jnp.bfloat16)
     mixed = jnp.dot(
-        jnp.sum(jnp.where(out_hit, gates[:, :, None], 0.0), axis=1),
-        back_rows.astype(jnp.float32),
-        precision=lax.Precision.HIGHEST,
+        jnp.concatenate([gate_hi, gate_mid, gate_lo], axis=1),
+        jnp.concatenate([back_rows, back_rows, back_rows], axis=0),
         preferred_element_type=jnp.float32,
     ).astype(jnp.bfloat16)
     input_grad = jnp.dot(

time: 301 us -> 301 us (level)
  no operation moved by 1% of the time
where the time goes in v10:
time: 301 us; the launch traced here: 300 us
  waiting for transfers between devices  180 us (60%)
  matrix products  59 us (20%)
  starting transfers between devices  26 us (9%)
  other arithmetic  18 us (6%)
  between operations  14.7 us (5%)
  local copies, waits for them, and re-layouts  3.06 us (1%)
    all_to_all x1, waiting for transfers between devices, body(): lax.all_to_all(send_both.reshape(experts, 2 * capacity, model_width), 'ex...  71.7 us
    all_to_all x1, waiting for transfers between devices, body(): lax.all_to_all((contract_rows(take_token, expert_out) + contract_rows(tak...  44.7 us
    ppermute x4, waiting for transfers between devices, partner(): return lax.ppermute(value, axis, pairs)  44.2 us
    dot_general x4, matrix products, contract_rows(): lax.dot_general(left, right, (((0,), (0,)), ((), ())), preferred_element_...  27.1 us
    reduce_scatter x1, waiting for transfers between devices, body(): lax.psum_scatter(contract_rows(expert_rows, up_grad).astype(jnp.bfloat16)...  19 us
    dot_general x2, matrix products, contract_cols(): lax.dot_general(left, right, (((1,), (1,)), ((), ())), preferred_element_...  12.9 us
    all_to_all x1, starting transfers between devices, body(): lax.all_to_all(send_both.reshape(experts, 2 * capacity, model_width), 'ex...  11.3 us
    all_to_all x1, starting transfers between devices, body(): lax.all_to_all((contract_rows(take_token, expert_out) + contract_rows(tak...  9.92 us
  transfers between devices with their start and end apart: 10, of which 7 were waited for; matrix products, arithmetic and copies ran while one was open for 25% of the time, Pallas kernels for 0%

profile of v10, /device:TPU:6, one launch (start us, length us, event | category | flops | bytes accessed | tf_op | source)
XLA Modules:
  0.0 300.5 jit_solution(4899460581713251717)
XLA Ops:
  7.2 2.0 collective-permute-start
  11.6 0.9 reduce-window.6
  13.1 1.3 dynamic_slice.3
  14.8 1.1 select_reduce_fusion.1
  16.5 1.3 pad_maximum_fusion.1
  17.9 1.3 pad_maximum_fusion
  19.2 2.7 multiply_convert_fusion
  21.9 4.7 %collective-permute-done = bf16[1,256,1408]{2,1,0:T(8,128)(2,1)S(1)} collective-permute-done((bf16[1,256,1408]{2,1,0:T(8,128)(2,1)}, bf16[1,256,1408]{2,1,0:T(8,128)(2,1)S(1)}, u32[]{:S(2)}, u32[]{:S(2)}) %collective-permute-start) | collective-permute-done | bytes 720928 | tf_op jit(solution)/shard_map/ppermute | solution.py:18
  26.5 14.5 %collective-permute-done.1 = bf16[1,176,2048]{2,1,0:T(8,128)(2,1)S(1)} collective-permute-done((bf16[1,176,2048]{2,1,0:T(8,128)(2,1)}, bf16[1,176,2048]{2,1,0:T(8,128)(2,1)S(1)}, u32[]{:S(2)}, u32[]{:S(2)}) %collective-permute-start.1) | collective-permute-done | bytes 720928 | tf_op jit(solution)/shard_map/ppermute | solution.py:18
  41.0 1.0 broadcast_select_fusion
  42.1 0.9 broadcast_select_fusion.1
  43.1 11.3 %all-to-all-start = ((bf16[32,24,2048]{2,1,0:T(8,128)(2,1)}), bf16[32,24,2048]{2,1,0:T(8,128)(2,1)S(1)}, u32[]{:S(2)}, u32[]{:S(2)}) async-start(bf16[32,24,2048]{2,1,0:T(8,128)(2,1)} %bitcast.4), calls=%async_computation | async-start | bytes 6291456 | tf_op jit(solution)/shard_map/all_to_all | solution.py:114
  54.5 1.9 collective-permute-start.2
  56.3 71.7 %all-to-all-done = bf16[32,24,2048]{2,1,0:T(8,128)(2,1)S(1)} async-done(((bf16[32,24,2048]{2,1,0:T(8,128)(2,1)}), bf16[32,24,2048]{2,1,0:T(8,128)(2,1)S(1)}, u32[]{:S(2)}, u32[]{:S(2)}) %all-to-all-start) | async-done | bytes 3145760 | tf_op jit(solution)/shard_map/all_to_all | solution.py:114
  128.1 2.6 convolution_convert_fusion.2
  130.7 2.6 convolution_convert_fusion.3
  133.3 7.3 %multiply_convert_fusion.1 = (bf16[384,1408]{1,0:T(8,128)(2,1)S(1)}, f32[384,1408]{1,0:T(8,128)}) fusion(bf16[384,2048]{1,0:T(8,128)(2,1)} %convolution_convert_fusion.3, bf16[1,2048,1408]{2,1,0:T(8,128)(2,1)} %all-gather.5.cloned.1.call-done), kind=kOutput, calls=%fused_computation.22 | convolution fusion | flops 2217295872 | bytes 10584064 | tf_op jit(solution)/shard_map/dot_general | solution.py:142
  140.6 5.0 %convolution_convert_fusion.1 = bf16[1408,2048]{1,0:T(8,128)(2,1)} fusion(bf16[384,1408]{1,0:T(8,128)(2,1)S(1)} %get-tuple-element.34, bf16[384,2048]{1,0:T(8,128)(2,1)S(1)} %copy-done.11), kind=kOutput, calls=%fused_computation.7 | convolution fusion | flops 2217476096 | bytes 8421376 | tf_op jit(solution)/shard_map/dot_general | solution.py:44
  145.6 8.4 %collective-permute-done.2 = bf16[2,256,1408]{2,1,0:T(8,128)(2,1)} collective-permute-done((bf16[2,256,1408]{2,1,0:T(8,128)(2,1)}, bf16[2,256,1408]{2,1,0:T(8,128)(2,1)}, u32[]{:S(2)}, u32[]{:S(2)}) %collective-permute-start.2) | collective-permute-done | bytes 1441824 | tf_op jit(solution)/shard_map/ppermute | solution.py:18
  154.2 7.2 %fusion.10 = bf16[384,1408]{1,0:T(8,128)(2,1)S(1)} fusion(bf16[384,2048]{1,0:T(8,128)(2,1)S(1)} %copy-done.11, bf16[1408,2048]{1,0:T(8,128)(2,1)} %bitcast.95, f32[384,1408]{1,0:T(8,128)} %get-tuple-element.64), kind=kOutput, calls=%fused_computation.15 | convolution fusion | flops 2219458560 | bytes 10584064 | tf_op jit(solution)/shard_map/dot_general | solution.py:50
  161.5 5.2 %convolution_convert_fusion = bf16[2048,1408]{1,0:T(8,128)(2,1)} fusion(bf16[384,2048]{1,0:T(8,128)(2,1)S(1)} %copy-done.10, bf16[384,1408]{1,0:T(8,128)(2,1)S(1)} %fusion.10), kind=kOutput, calls=%fused_computation.6 | convolution fusion | flops 2217476096 | bytes 8421376 | tf_op jit(solution)/shard_map/dot_general | solution.py:44
  167.2 5.7 %fusion.11 = bf16[384,2048]{1,0:T(8,128)(2,1)S(1)} fusion(bf16[384,1408]{1,0:T(8,128)(2,1)} %copy-done.13, bf16[1,2048,1408]{2,1,0:T(8,128)(2,1)} %all-gather.5.cloned.1.call-done), kind=kOutput, calls=%fused_computation.18 | convolution fusion | flops 2215378944 | bytes 8421376 | tf_op jit(solution)/shard_map/dot_general | solution.py:50
  172.9 10.0 %fusion.19 = f32[768,2048]{1,0:T(8,128)} fusion(bf16[384,1408]{1,0:T(8,128)(2,1)} %copy-done.12, bf16[1408,2048]{1,0:T(8,128)(2,1)} %bitcast.96, s32[768]{0:T(1024)S(1)} %iota.33, s32[384]{0:T(512)S(1)} %get-tuple-element.53), kind=kOutput, calls=%fused_computation.30 | convolution fusion | flops 3423633408 | bytes 13144576 | tf_op jit(solution)/shard_map/dot_general | solution.py:44
  182.9 16.6 %collective-permute-done.3 = bf16[2,176,2048]{2,1,0:T(8,128)(2,1)S(1)} collective-permute-done((bf16[2,176,2048]{2,1,0:T(8,128)(2,1)}, bf16[2,176,2048]{2,1,0:T(8,128)(2,1)S(1)}, u32[]{:S(2)}, u32[]{:S(2)}) %collective-permute-start.3) | collective-permute-done | bytes 1441824 | tf_op jit(solution)/shard_map/ppermute | solution.py:18
  199.6 6.9 %add_convert_fusion = bf16[768,2048]{1,0:T(8,128)(2,1)} fusion(f32[768,2048]{1,0:T(8,128)} %fusion.19, bf16[384,2048]{1,0:T(8,128)(2,1)S(1)} %fusion.11, s32[768]{0:T(1024)S(1)} %iota.33, s32[384]{0:T(512)S(1)} %get-tuple-element.52), kind=kOutput, calls=%fused_computation.8 | convolution fusion | flops 1211400192 | bytes 11014656 | tf_op jit(solution)/shard_map/dot_general | solution.py:44
  206.5 9.9 %all-to-all-start.1 = ((bf16[32,24,2048]{2,1,0:T(8,128)(2,1)}), bf16[32,24,2048]{2,1,0:T(8,128)(2,1)S(1)}, u32[]{:S(2)}, u32[]{:S(2)}) async-start(bf16[32,24,2048]{2,1,0:T(8,128)(2,1)} %bitcast.85), calls=%async_computation.1 | async-start | bytes 6291456 | tf_op jit(solution)/shard_map/all_to_all | solution.py:155
  217.1 4.7 %fusion.30 = (bf16[176,2048]{1,0:T(8,128)(2,1)}, bf16[176,2048]{1,0:T(8,128)(2,1)}, bf16[176,2048]{1,0:T(8,128)(2,1)}) fusion(bf16[176,2048]{1,0:T(8,128)(2,1)} %reduce-scatter.5.cloned.1.call-done, bf16[1,176,2048]{2,1,0:T(8,128)(2,1)} %param.21, bf16[2,176,2048]{2,1,0:T(8,128)(2,1)} %copy-done.4, pred[]{:T(512)} %bitcast.2, ...), kind=kLoop, calls=%fused_computation.45 | loop fusion | flops 7569408 | bytes 6488065 | tf_op jit(solution)/shard_map/convert_element_type | solution.py:39
  221.8 19.0 %reduce-scatter.3.cloned.1.call-done = bf16[256,1408]{1,0:T(8,128)(2,1)} async-done(((bf16[2048,1408]{1,0:T(8,128)(2,1)}), bf16[256,1408]{1,0:T(8,128)(2,1)}) %reduce-scatter.3.cloned.1.call-update) | async-done | bytes 720912 | tf_op jit(solution)/shard_map/reduce_scatter | solution.py:164
  240.8 4.7 %fusion.31 = (bf16[256,1408]{1,0:T(8,128)(2,1)}, bf16[256,1408]{1,0:T(8,128)(2,1)}, bf16[256,1408]{1,0:T(8,128)(2,1)}) fusion(bf16[256,1408]{1,0:T(8,128)(2,1)} %reduce-scatter.3.cloned.1.call-done, bf16[1,256,1408]{2,1,0:T(8,128)(2,1)} %param.19, bf16[2,256,1408]{2,1,0:T(8,128)(2,1)} %collective-permute-done.2, pred[]{:T(512)} %bitcast.2, ...), kind=kLoop, calls=%fused_computation.46 | loop fusion | flops 7569408 | bytes 6488065 | tf_op jit(solution)/shard_map/convert_element_type | solution.py:39
  245.5 44.7 %all-to-all-done.1 = bf16[32,24,2048]{2,1,0:T(8,128)(2,1)S(1)} async-done(((bf16[32,24,2048]{2,1,0:T(8,128)(2,1)}), bf16[32,24,2048]{2,1,0:T(8,128)(2,1)S(1)}, u32[]{:S(2)}, u32[]{:S(2)}) %all-to-all-start.1) | async-done | bytes 3145760 | tf_op jit(solution)/shard_map/all_to_all | solution.py:155
  290.2 1.3 convolution_convert_fusion.5
  291.5 2.5 fusion.14
  (68 shorter events, 4.9 us)
Async XLA Ops:
  7.2 9.3 %copy-start = (bf16[1,176,2048]{2,1,0:T(8,128)(2,1)S(1)}, bf16[1,176,2048]{2,1,0:T(8,128)(2,1)}, u32[]{:S(2)}) copy-start(bf16[1,176,2048]{2,1,0:T(8,128)(2,1)} %param.21) | copy-start | bytes 2162692
  7.2 9.3 %copy-start.1 = (bf16[1,176,2048]{2,1,0:T(8,128)(2,1)S(1)}, bf16[1,176,2048]{2,1,0:T(8,128)(2,1)}, u32[]{:S(2)}) copy-start(bf16[1,176,2048]{2,1,0:T(8,128)(2,1)} %param.20) | copy-start | bytes 2162692
  7.2 126.1 %all-gather.5.cloned.1.call-start = ((), (), s32[]{:S(2)}) async-start(), calls=%async_computation.5 | async-start | bytes 6488064 | tf_op jit(solution)/shard_map/all_gather | solution.py:124
  7.2 19.3 %collective-permute-start = (bf16[1,256,1408]{2,1,0:T(8,128)(2,1)}, bf16[1,256,1408]{2,1,0:T(8,128)(2,1)S(1)}, u32[]{:S(2)}, u32[]{:S(2)}) collective-permute-start(bf16[1,256,1408]{2,1,0:T(8,128)(2,1)} %param.16), channel_id=1, source_target_pairs={{0,1},{1,0},{2,3},{3,2},{4,5},{5,4},{6,7},{7,6},{8,9},{9,8},{10,11... | collective-permute-start | bytes 2162696 | tf_op jit(solution)/shard_map/ppermute | solution.py:18
  9.2 31.8 %collective-permute-start.1 = (bf16[1,176,2048]{2,1,0:T(8,128)(2,1)}, bf16[1,176,2048]{2,1,0:T(8,128)(2,1)S(1)}, u32[]{:S(2)}, u32[]{:S(2)}) collective-permute-start(bf16[1,176,2048]{2,1,0:T(8,128)(2,1)} %param.17), channel_id=1, source_target_pairs={{0,1},{1,0},{2,3},{3,2},{4,5},{5,4},{6,7},{7,6},{8,9},{9,8},{10,11... | collective-permute-start | bytes 2162696 | tf_op jit(solution)/shard_map/ppermute | solution.py:18
  14.7 3.1 %copy-start.2 = (bf16[1,256,1408]{2,1,0:T(8,128)(2,1)S(1)}, bf16[1,256,1408]{2,1,0:T(8,128)(2,1)}, u32[]{:S(2)}) copy-start(bf16[1,256,1408]{2,1,0:T(8,128)(2,1)} %param.19) | copy-start | bytes 2162692
  14.7 3.1 %copy-start.3 = (bf16[1,256,1408]{2,1,0:T(8,128)(2,1)S(1)}, bf16[1,256,1408]{2,1,0:T(8,128)(2,1)}, u32[]{:S(2)}) copy-start(bf16[1,256,1408]{2,1,0:T(8,128)(2,1)} %param.18) | copy-start | bytes 2162692
  17.9 1.3 copy-start.7
  17.9 1.3 copy-start.8
  19.2 21.9 %copy-start.5 = (bf16[1,256,1408]{2,1,0:T(8,128)(2,1)S(1)}, bf16[1,256,1408]{2,1,0:T(8,128)(2,1)}, u32[]{:S(2)}) copy-start(bf16[1,256,1408]{2,1,0:T(8,128)(2,1)} %param.16) | copy-start | bytes 2162692
  21.9 20.2 %copy-start.6 = (bf16[1,176,2048]{2,1,0:T(8,128)(2,1)S(1)}, bf16[1,176,2048]{2,1,0:T(8,128)(2,1)}, u32[]{:S(2)}) copy-start(bf16[1,176,2048]{2,1,0:T(8,128)(2,1)} %param.17) | copy-start | bytes 2162692
  42.0 98.5 %all-gather.3.cloned.1.call-start = ((), (), s32[]{:S(2)}) async-start(), calls=%async_computation.4 | async-start | bytes 6488064 | tf_op jit(solution)/shard_map/all_gather | solution.py:125
  43.1 85.0 %all-to-all-start = ((bf16[32,24,2048]{2,1,0:T(8,128)(2,1)}), bf16[32,24,2048]{2,1,0:T(8,128)(2,1)S(1)}, u32[]{:S(2)}, u32[]{:S(2)}) async-start(bf16[32,24,2048]{2,1,0:T(8,128)(2,1)} %bitcast.4), calls=%async_computation | async-start | bytes 6291456 | tf_op jit(solution)/shard_map/all_to_all | solution.py:114
  54.4 162.7 %reduce-scatter.5.cloned.1.call-start = ((), (), s32[]{:S(2)}) async-start(), calls=%async_computation.7 | async-start | bytes 6488064 | tf_op jit(solution)/shard_map/reduce_scatter | solution.py:170
  54.5 99.5 %collective-permute-start.2 = (bf16[2,256,1408]{2,1,0:T(8,128)(2,1)}, bf16[2,256,1408]{2,1,0:T(8,128)(2,1)}, u32[]{:S(2)}, u32[]{:S(2)}) collective-permute-start(bf16[2,256,1408]{2,1,0:T(8,128)(2,1)} %pad_maximum_fusion), channel_id=1, source_target_pairs={{0,1},{1,0},{2,3},{3,2},{4,5},{5,4},{6,7},{7,6},{8,9},{9,8},{10,11... | collective-permute-start | bytes 4325384 | tf_op jit(solution)/shard_map/ppermute | solution.py:18
  133.3 7.3 %copy-start.11 = (bf16[384,2048]{1,0:T(8,128)(2,1)S(1)}, bf16[384,2048]{1,0:T(8,128)(2,1)}, u32[]{:S(2)}) copy-start(bf16[384,2048]{1,0:T(8,128)(2,1)} %convolution_convert_fusion.2) | copy-start | bytes 4718596
  140.6 5.0 %copy-start.12 = (bf16[384,1408]{1,0:T(8,128)(2,1)}, bf16[384,1408]{1,0:T(8,128)(2,1)S(1)}, u32[]{:S(2)}) copy-start(bf16[384,1408]{1,0:T(8,128)(2,1)S(1)} %get-tuple-element.34) | copy-start | bytes 3244036
  154.0 86.8 %reduce-scatter.3.cloned.1.call-start = ((), (), s32[]{:S(2)}) async-start(), calls=%async_computation.6 | async-start | bytes 6488064 | tf_op jit(solution)/shard_map/reduce_scatter | solution.py:164
  154.2 7.3 %copy-start.10 = (bf16[384,2048]{1,0:T(8,128)(2,1)S(1)}, bf16[384,2048]{1,0:T(8,128)(2,1)}, u32[]{:S(2)}) copy-start(bf16[384,2048]{1,0:T(8,128)(2,1)} %convolution_convert_fusion.3) | copy-start | bytes 4718596
  161.5 5.2 %copy-start.13 = (bf16[384,1408]{1,0:T(8,128)(2,1)}, bf16[384,1408]{1,0:T(8,128)(2,1)S(1)}, u32[]{:S(2)}) copy-start(bf16[384,1408]{1,0:T(8,128)(2,1)S(1)} %fusion.10) | copy-start | bytes 3244036
  166.7 32.8 %collective-permute-start.3 = (bf16[2,176,2048]{2,1,0:T(8,128)(2,1)}, bf16[2,176,2048]{2,1,0:T(8,128)(2,1)S(1)}, u32[]{:S(2)}, u32[]{:S(2)}) collective-permute-start(bf16[2,176,2048]{2,1,0:T(8,128)(2,1)} %pad_maximum_fusion.1), channel_id=1, source_target_pairs={{0,1},{1,0},{2,3},{3,2},{4,5},{5,4},{6,7},{7,6},{8,9},{9,8},{10,11... | collective-permute-start | bytes 4325384 | tf_op jit(solution)/shard_map/ppermute | solution.py:18
  199.6 6.9 %copy-start.4 = (bf16[2,176,2048]{2,1,0:T(8,128)(2,1)}, bf16[2,176,2048]{2,1,0:T(8,128)(2,1)S(1)}, u32[]{:S(2)}) copy-start(bf16[2,176,2048]{2,1,0:T(8,128)(2,1)S(1)} %collective-permute-done.3) | copy-start | bytes 4325380
  206.5 83.7 %all-to-all-start.1 = ((bf16[32,24,2048]{2,1,0:T(8,128)(2,1)}), bf16[32,24,2048]{2,1,0:T(8,128)(2,1)S(1)}, u32[]{:S(2)}, u32[]{:S(2)}) async-start(bf16[32,24,2048]{2,1,0:T(8,128)(2,1)} %bitcast.85), calls=%async_computation.1 | async-start | bytes 6291456 | tf_op jit(solution)/shard_map/all_to_all | solution.py:155
  290.2 1.3 copy-start.9
Sparse Core Ops, SparseCore 0:
  42.2 42.1 all-gather.4
  86.7 41.3 all-gather.2
  154.1 40.9 reduce-scatter.4
  197.5 43.1 reduce-scatter.2

commit v11 on v9

--- a/solution.py
+++ b/solution.py
@@ -108,7 +108,7 @@
             w_down_in,
             send_both,
             jnp.concatenate([m_up, v_up], axis=0),
-            jnp.concatenate([m_down, v_down], axis=0),
+            m_down,
         )
     )
     got_both = lax.all_to_all(
@@ -119,6 +119,7 @@
         tiled=True,
     )
     up_moments = partner(up_local, "expert", 0)
+    v_down_in = partner(v_down, "expert", 0)
     w_up_use = jnp.where(swapped, w_up_in, w_up)
     w_down_use = jnp.where(swapped, w_down_in, w_down)
     up_full = lax.all_gather(w_up_use, "dp", axis=1, tiled=True)[0]
@@ -143,8 +144,8 @@
     hidden = jax.nn.silu(up_act).astype(jnp.bfloat16)
     down_full, hidden = lax.optimization_barrier((down_full, hidden))
     down_part = contract_rows(hidden, grad_rows).astype(jnp.bfloat16)
-    down_part, up_moments, down_local = lax.optimization_barrier(
-        (down_part, up_moments, down_local)
+    down_part, up_moments, v_down_in, down_local = lax.optimization_barrier(
+        (down_part, up_moments, v_down_in, down_local)
     )
     down_moments = partner(down_local, "expert", 0)
     expert_out = jnp.dot(hidden, down_full, preferred_element_type=jnp.float32).astype(jnp.bfloat16)
@@ -175,8 +176,8 @@
     ).astype(jnp.float32)
     m_up_use = jnp.where(swapped, up_moments[0:1], m_up)
     v_up_use = jnp.where(swapped, up_moments[1:2], v_up)
-    m_down_use = jnp.where(swapped, down_moments[0:1], m_down)
-    v_down_use = jnp.where(swapped, down_moments[1:2], v_down)
+    m_down_use = jnp.where(swapped, down_moments, m_down)
+    v_down_use = jnp.where(swapped, v_down_in, v_down)
     up_new = adam_update(w_up_use[0], m_up_use[0], v_up_use[0], up_gradient)
     down_new = adam_update(w_down_use[0], m_down_use[0], v_down_use[0], down_gradient)
     both_back, up_new, down_new = lax.optimization_barrier((both_back, up_new, down_new))

time: 301 us -> 299 us (level)
  matrix products: 59 us -> 55.5 us
    reduce_scatter x1, waiting for transfers between devices: 19.7 us -> 36.7 us  [body(): lax.psum_scatter(contract_rows(expert_rows, up_grad).astype(jnp.bfloat16)...]
    all_to_all x1, waiting for transfers between devices: 44.6 us -> 27.7 us  [body(): lax.all_to_all((contract_rows(take_token, expert_out) + contract_rows(tak...]
    dot_general x4, matrix products: 27.1 us -> 23.5 us  [contract_rows(): lax.dot_general(left, right, (((0,), (0,)), ((), ())), preferred_element_...]
    ppermute x4 -> x5, waiting for transfers between devices: 44.2 us -> 45.6 us  [partner(): return lax.ppermute(value, axis, pairs)]
  transfers between devices with their start and end apart: 10 -> 11, of which waited for: 7 -> 7; matrix products, arithmetic and copies ran while one was open for 25% -> 23% of each run, Pallas kernels for 0% -> 0%
where the time goes in v11:
time: 299 us
  waiting for transfers between devices  182 us (61%)
  matrix products  55.5 us (19%)
  starting transfers between devices  26.3 us (9%)
  other arithmetic  15.8 us (5%)
  between operations  14.7 us (5%)
  local copies, waits for them, and re-layouts  5.1 us (2%)
    all_to_all x1, waiting for transfers between devices, body(): lax.all_to_all(send_both.reshape(experts, 2 * capacity, model_width), 'ex...  71.4 us
    ppermute x5, waiting for transfers between devices, partner(): return lax.ppermute(value, axis, pairs)  45.6 us
    reduce_scatter x1, waiting for transfers between devices, body(): lax.psum_scatter(contract_rows(expert_rows, up_grad).astype(jnp.bfloat16)...  36.7 us
    all_to_all x1, waiting for transfers between devices, body(): lax.all_to_all((contract_rows(take_token, expert_out) + contract_rows(tak...  27.7 us
    dot_general x4, matrix products, contract_rows(): lax.dot_general(left, right, (((0,), (0,)), ((), ())), preferred_element_...  23.5 us
    dot_general x2, matrix products, contract_cols(): lax.dot_general(left, right, (((1,), (1,)), ((), ())), preferred_element_...  13.1 us
    all_to_all x1, starting transfers between devices, body(): lax.all_to_all(send_both.reshape(experts, 2 * capacity, model_width), 'ex...  11.3 us
    all_to_all x1, starting transfers between devices, body(): lax.all_to_all((contract_rows(take_token, expert_out) + contract_rows(tak...  9.91 us
  transfers between devices with their start and end apart: 11, of which 7 were waited for; matrix products, arithmetic and copies ran while one was open for 23% of the time, Pallas kernels for 0%

profile of v11, /device:TPU:6, one launch (start us, length us, event | category | flops | bytes accessed | tf_op | source)
XLA Modules:
  0.0 299.0 jit_solution(10046775398895021749)
XLA Ops:
  7.2 2.0 collective-permute-start
  13.1 1.3 dynamic_slice.3
  15.5 1.0 select_reduce_fusion
  16.5 1.3 pad_maximum_fusion
  17.8 2.7 multiply_convert_fusion
  20.4 6.1 %collective-permute-done = bf16[1,256,1408]{2,1,0:T(8,128)(2,1)S(1)} collective-permute-done((bf16[1,256,1408]{2,1,0:T(8,128)(2,1)}, bf16[1,256,1408]{2,1,0:T(8,128)(2,1)S(1)}, u32[]{:S(2)}, u32[]{:S(2)}) %collective-permute-start) | collective-permute-done | bytes 720928 | tf_op jit(solution)/shard_map/ppermute | solution.py:18
  26.5 14.5 %collective-permute-done.1 = bf16[1,176,2048]{2,1,0:T(8,128)(2,1)S(1)} collective-permute-done((bf16[1,176,2048]{2,1,0:T(8,128)(2,1)}, bf16[1,176,2048]{2,1,0:T(8,128)(2,1)S(1)}, u32[]{:S(2)}, u32[]{:S(2)}) %collective-permute-start.1) | collective-permute-done | bytes 720928 | tf_op jit(solution)/shard_map/ppermute | solution.py:18
  41.0 1.0 broadcast_select_fusion
  42.1 0.9 broadcast_select_fusion.3
  43.1 11.3 %all-to-all-start = ((bf16[32,24,2048]{2,1,0:T(8,128)(2,1)}), bf16[32,24,2048]{2,1,0:T(8,128)(2,1)S(1)}, u32[]{:S(2)}, u32[]{:S(2)}) async-start(bf16[32,24,2048]{2,1,0:T(8,128)(2,1)} %bitcast.4), calls=%async_computation | async-start | bytes 6291456 | tf_op jit(solution)/shard_map/all_to_all | solution.py:114
  54.4 1.9 collective-permute-start.3
  56.7 71.4 %all-to-all-done = bf16[32,24,2048]{2,1,0:T(8,128)(2,1)S(1)} async-done(((bf16[32,24,2048]{2,1,0:T(8,128)(2,1)}), bf16[32,24,2048]{2,1,0:T(8,128)(2,1)S(1)}, u32[]{:S(2)}, u32[]{:S(2)}) %all-to-all-start) | async-done | bytes 3145760 | tf_op jit(solution)/shard_map/all_to_all | solution.py:114
  128.1 2.6 convolution_convert_fusion.2
  130.6 2.6 convolution_convert_fusion.3
  133.2 7.3 %multiply_convert_fusion.1 = (bf16[384,1408]{1,0:T(8,128)(2,1)S(1)}, f32[384,1408]{1,0:T(8,128)}) fusion(bf16[384,2048]{1,0:T(8,128)(2,1)} %convolution_convert_fusion.3, bf16[1,2048,1408]{2,1,0:T(8,128)(2,1)} %all-gather.5.cloned.1.call-done), kind=kOutput, calls=%fused_computation.16 | convolution fusion | flops 2217295872 | bytes 10584064 | tf_op jit(solution)/shard_map/dot_general | solution.py:143
  140.5 5.0 %convolution_convert_fusion.1 = bf16[1408,2048]{1,0:T(8,128)(2,1)} fusion(bf16[384,1408]{1,0:T(8,128)(2,1)S(1)} %get-tuple-element.35, bf16[384,2048]{1,0:T(8,128)(2,1)S(1)} %copy-done.10), kind=kOutput, calls=%fused_computation.1 | convolution fusion | flops 2217476096 | bytes 8421376 | tf_op jit(solution)/shard_map/dot_general | solution.py:44
  145.6 23.9 %collective-permute-done.2 = bf16[2,256,1408]{2,1,0:T(8,128)(2,1)} collective-permute-done((bf16[2,256,1408]{2,1,0:T(8,128)(2,1)}, bf16[2,256,1408]{2,1,0:T(8,128)(2,1)}, u32[]{:S(2)}, u32[]{:S(2)}) %collective-permute-start.2) | collective-permute-done | bytes 1441824 | tf_op jit(solution)/shard_map/ppermute | solution.py:18
  169.7 7.2 %fusion.4 = bf16[384,1408]{1,0:T(8,128)(2,1)S(1)} fusion(bf16[384,2048]{1,0:T(8,128)(2,1)S(1)} %copy-done.10, bf16[1408,2048]{1,0:T(8,128)(2,1)} %bitcast.97, f32[384,1408]{1,0:T(8,128)} %get-tuple-element.63), kind=kOutput, calls=%fused_computation.9 | convolution fusion | flops 2219458560 | bytes 10584064 | tf_op jit(solution)/shard_map/dot_general | solution.py:50
  177.0 1.0 copy-done.11
  177.9 5.1 %convolution_convert_fusion = bf16[2048,1408]{1,0:T(8,128)(2,1)} fusion(bf16[384,2048]{1,0:T(8,128)(2,1)S(1)} %copy-done.9, bf16[384,1408]{1,0:T(8,128)(2,1)S(1)} %fusion.4), kind=kOutput, calls=%fused_computation | convolution fusion | flops 2217476096 | bytes 8421376 | tf_op jit(solution)/shard_map/dot_general | solution.py:44
  183.1 1.1 copy-done.3
  184.6 9.6 %fusion.10 = f32[768,2048]{1,0:T(8,128)} fusion(bf16[384,1408]{1,0:T(8,128)(2,1)S(1)} %get-tuple-element.35, bf16[1408,2048]{1,0:T(8,128)(2,1)} %bitcast.98, s32[768]{0:T(1024)S(1)} %iota.33, s32[384]{0:T(512)S(1)} %get-tuple-element.55), kind=kOutput, calls=%fused_computation.24 | convolution fusion | flops 3423633408 | bytes 13144576 | tf_op jit(solution)/shard_map/dot_general | solution.py:44
  194.2 5.9 %fusion.5 = bf16[384,2048]{1,0:T(8,128)(2,1)S(1)} fusion(bf16[384,1408]{1,0:T(8,128)(2,1)} %copy-done.11, bf16[1,2048,1408]{2,1,0:T(8,128)(2,1)} %all-gather.5.cloned.1.call-done), kind=kOutput, calls=%fused_computation.12 | convolution fusion | flops 2215378944 | bytes 8421376 | tf_op jit(solution)/shard_map/dot_general | solution.py:50
  200.1 1.2 collective-permute-done.4
  201.3 3.7 %add_convert_fusion = bf16[768,2048]{1,0:T(8,128)(2,1)} fusion(f32[768,2048]{1,0:T(8,128)S(1)} %copy-done, bf16[384,2048]{1,0:T(8,128)(2,1)S(1)} %fusion.5, s32[768]{0:T(1024)S(1)} %iota.33, s32[384]{0:T(512)S(1)} %get-tuple-element.54), kind=kOutput, calls=%fused_computation.2 | convolution fusion | flops 1211400192 | bytes 11014656 | tf_op jit(solution)/shard_map/dot_general | solution.py:44
  205.0 9.9 %all-to-all-start.1 = ((bf16[32,24,2048]{2,1,0:T(8,128)(2,1)}), bf16[32,24,2048]{2,1,0:T(8,128)(2,1)S(1)}, u32[]{:S(2)}, u32[]{:S(2)}) async-start(bf16[32,24,2048]{2,1,0:T(8,128)(2,1)} %bitcast.87), calls=%async_computation.1 | async-start | bytes 6291456 | tf_op jit(solution)/shard_map/all_to_all | solution.py:156
  214.9 4.6 %fusion.21 = (bf16[176,2048]{1,0:T(8,128)(2,1)}, bf16[176,2048]{1,0:T(8,128)(2,1)}, bf16[176,2048]{1,0:T(8,128)(2,1)}) fusion(bf16[176,2048]{1,0:T(8,128)(2,1)} %reduce-scatter.5.cloned.1.call-done, bf16[1,176,2048]{2,1,0:T(8,128)(2,1)} %collective-permute-done.3, bf16[1,176,2048]{2,1,0:T(8,128)(2,1)} %param.21, pred[]{:T(512)} %bitcast.2, ...), kind=kLoop, calls=%fused_computation.38 | loop fusion | flops 7569408 | bytes 6488065 | tf_op jit(solution)/shard_map/convert_element_type | solution.py:39
  219.5 36.7 %reduce-scatter.3.cloned.1.call-done = bf16[256,1408]{1,0:T(8,128)(2,1)} async-done(((bf16[2048,1408]{1,0:T(8,128)(2,1)}), bf16[256,1408]{1,0:T(8,128)(2,1)}) %reduce-scatter.3.cloned.1.call-update) | async-done | bytes 720912 | tf_op jit(solution)/shard_map/reduce_scatter | solution.py:165
  256.3 4.7 %fusion.22 = (bf16[256,1408]{1,0:T(8,128)(2,1)}, bf16[256,1408]{1,0:T(8,128)(2,1)}, bf16[256,1408]{1,0:T(8,128)(2,1)}) fusion(bf16[256,1408]{1,0:T(8,128)(2,1)} %reduce-scatter.3.cloned.1.call-done, bf16[1,256,1408]{2,1,0:T(8,128)(2,1)} %param.19, bf16[2,256,1408]{2,1,0:T(8,128)(2,1)} %collective-permute-done.2, pred[]{:T(512)} %bitcast.2, ...), kind=kLoop, calls=%fused_computation.39 | loop fusion | flops 7569408 | bytes 6488065 | tf_op jit(solution)/shard_map/convert_element_type | solution.py:39
  261.0 27.7 %all-to-all-done.1 = bf16[32,24,2048]{2,1,0:T(8,128)(2,1)S(1)} async-done(((bf16[32,24,2048]{2,1,0:T(8,128)(2,1)}), bf16[32,24,2048]{2,1,0:T(8,128)(2,1)S(1)}, u32[]{:S(2)}, u32[]{:S(2)}) %all-to-all-start.1) | async-done | bytes 3145760 | tf_op jit(solution)/shard_map/all_to_all | solution.py:156
  288.7 1.3 convolution_convert_fusion.5
  290.1 2.4 convolution_convert_fusion.6
  (64 shorter events, 5.4 us)
Async XLA Ops:
  7.2 9.3 %copy-start.1 = (bf16[1,256,1408]{2,1,0:T(8,128)(2,1)S(1)}, bf16[1,256,1408]{2,1,0:T(8,128)(2,1)}, u32[]{:S(2)}) copy-start(bf16[1,256,1408]{2,1,0:T(8,128)(2,1)} %param.19) | copy-start | bytes 2162692
  7.2 9.3 %copy-start.2 = (bf16[1,256,1408]{2,1,0:T(8,128)(2,1)S(1)}, bf16[1,256,1408]{2,1,0:T(8,128)(2,1)}, u32[]{:S(2)}) copy-start(bf16[1,256,1408]{2,1,0:T(8,128)(2,1)} %param.18) | copy-start | bytes 2162692
  7.2 126.0 %all-gather.5.cloned.1.call-start = ((), (), s32[]{:S(2)}) async-start(), calls=%async_computation.5 | async-start | bytes 6488064 | tf_op jit(solution)/shard_map/all_gather | solution.py:125
  7.2 19.3 %collective-permute-start = (bf16[1,256,1408]{2,1,0:T(8,128)(2,1)}, bf16[1,256,1408]{2,1,0:T(8,128)(2,1)S(1)}, u32[]{:S(2)}, u32[]{:S(2)}) collective-permute-start(bf16[1,256,1408]{2,1,0:T(8,128)(2,1)} %param.16), channel_id=1, source_target_pairs={{0,1},{1,0},{2,3},{3,2},{4,5},{5,4},{6,7},{7,6},{8,9},{9,8},{10,11... | collective-permute-start | bytes 2162696 | tf_op jit(solution)/shard_map/ppermute | solution.py:18
  9.2 31.8 %collective-permute-start.1 = (bf16[1,176,2048]{2,1,0:T(8,128)(2,1)}, bf16[1,176,2048]{2,1,0:T(8,128)(2,1)S(1)}, u32[]{:S(2)}, u32[]{:S(2)}) collective-permute-start(bf16[1,176,2048]{2,1,0:T(8,128)(2,1)} %param.17), channel_id=1, source_target_pairs={{0,1},{1,0},{2,3},{3,2},{4,5},{5,4},{6,7},{7,6},{8,9},{9,8},{10,11... | collective-permute-start | bytes 2162696 | tf_op jit(solution)/shard_map/ppermute | solution.py:18
  14.7 3.0 %copy-start.7 = (bf16[48,2048]{1,0:T(8,128)(2,1)S(1)}, bf16[48,2048]{1,0:T(8,128)(2,1)}, u32[]{:S(2)}) copy-start(bf16[48,2048]{1,0:T(8,128)(2,1)} %param.14) | copy-start | bytes 589828
  14.7 3.0 %copy-start.8 = (bf16[48,2048]{1,0:T(8,128)(2,1)S(1)}, bf16[48,2048]{1,0:T(8,128)(2,1)}, u32[]{:S(2)}) copy-start(bf16[48,2048]{1,0:T(8,128)(2,1)} %param.11) | copy-start | bytes 589828
  17.8 23.3 %copy-start.5 = (bf16[1,256,1408]{2,1,0:T(8,128)(2,1)S(1)}, bf16[1,256,1408]{2,1,0:T(8,128)(2,1)}, u32[]{:S(2)}) copy-start(bf16[1,256,1408]{2,1,0:T(8,128)(2,1)} %param.16) | copy-start | bytes 2162692
  20.4 21.7 %copy-start.6 = (bf16[1,176,2048]{2,1,0:T(8,128)(2,1)S(1)}, bf16[1,176,2048]{2,1,0:T(8,128)(2,1)}, u32[]{:S(2)}) copy-start(bf16[1,176,2048]{2,1,0:T(8,128)(2,1)} %param.17) | copy-start | bytes 2162692
  42.0 98.5 %all-gather.3.cloned.1.call-start = ((), (), s32[]{:S(2)}) async-start(), calls=%async_computation.4 | async-start | bytes 6488064 | tf_op jit(solution)/shard_map/all_gather | solution.py:126
  43.1 85.0 %all-to-all-start = ((bf16[32,24,2048]{2,1,0:T(8,128)(2,1)}), bf16[32,24,2048]{2,1,0:T(8,128)(2,1)S(1)}, u32[]{:S(2)}, u32[]{:S(2)}) async-start(bf16[32,24,2048]{2,1,0:T(8,128)(2,1)} %bitcast.4), calls=%async_computation | async-start | bytes 6291456 | tf_op jit(solution)/shard_map/all_to_all | solution.py:114
  54.4 160.5 %reduce-scatter.5.cloned.1.call-start = ((), (), s32[]{:S(2)}) async-start(), calls=%async_computation.7 | async-start | bytes 6488064 | tf_op jit(solution)/shard_map/reduce_scatter | solution.py:171
  54.4 91.1 %collective-permute-start.3 = (bf16[1,176,2048]{2,1,0:T(8,128)(2,1)}, bf16[1,176,2048]{2,1,0:T(8,128)(2,1)}, u32[]{:S(2)}, u32[]{:S(2)}) collective-permute-start(bf16[1,176,2048]{2,1,0:T(8,128)(2,1)} %param.21), channel_id=1, source_target_pairs={{0,1},{1,0},{2,3},{3,2},{4,5},{5,4},{6,7},{7,6},{8,9},{9,8},{10,11... | collective-permute-start | bytes 2162696 | tf_op jit(solution)/shard_map/ppermute | solution.py:18
  56.3 113.1 %collective-permute-start.2 = (bf16[2,256,1408]{2,1,0:T(8,128)(2,1)}, bf16[2,256,1408]{2,1,0:T(8,128)(2,1)}, u32[]{:S(2)}, u32[]{:S(2)}) collective-permute-start(bf16[2,256,1408]{2,1,0:T(8,128)(2,1)} %pad_maximum_fusion), channel_id=1, source_target_pairs={{0,1},{1,0},{2,3},{3,2},{4,5},{5,4},{6,7},{7,6},{8,9},{9,8},{10,11... | collective-permute-start | bytes 4325384 | tf_op jit(solution)/shard_map/ppermute | solution.py:18
  133.2 7.3 %copy-start.10 = (bf16[384,2048]{1,0:T(8,128)(2,1)S(1)}, bf16[384,2048]{1,0:T(8,128)(2,1)}, u32[]{:S(2)}) copy-start(bf16[384,2048]{1,0:T(8,128)(2,1)} %convolution_convert_fusion.2) | copy-start | bytes 4718596
  169.5 86.8 %reduce-scatter.3.cloned.1.call-start = ((), (), s32[]{:S(2)}) async-start(), calls=%async_computation.6 | async-start | bytes 6488064 | tf_op jit(solution)/shard_map/reduce_scatter | solution.py:165
  169.7 8.2 %copy-start.9 = (bf16[384,2048]{1,0:T(8,128)(2,1)S(1)}, bf16[384,2048]{1,0:T(8,128)(2,1)}, u32[]{:S(2)}) copy-start(bf16[384,2048]{1,0:T(8,128)(2,1)} %convolution_convert_fusion.3) | copy-start | bytes 4718596
  176.9 1.0 copy-start.11
  183.1 1.1 copy-start.3
  184.2 17.1 %collective-permute-start.4 = (bf16[1,176,2048]{2,1,0:T(8,128)(2,1)S(1)}, bf16[1,176,2048]{2,1,0:T(8,128)(2,1)S(1)}, u32[]{:S(2)}, u32[]{:S(2)}) collective-permute-start(bf16[1,176,2048]{2,1,0:T(8,128)(2,1)S(1)} %copy-done.3), channel_id=1, source_target_pairs={{0,1},{1,0},{2,3},{3,2},{4,5},{5,4},{6,7},{7,6},{8,9},{9,8},{10,11... | collective-permute-start | bytes 2162696 | tf_op jit(solution)/shard_map/ppermute | solution.py:18
  194.2 7.1 %copy-start = (f32[768,2048]{1,0:T(8,128)S(1)}, f32[768,2048]{1,0:T(8,128)}, u32[]{:S(2)}) copy-start(f32[768,2048]{1,0:T(8,128)} %fusion.10) | copy-start | bytes 18874372
  201.3 3.7 %copy-start.4 = (bf16[1,176,2048]{2,1,0:T(8,128)(2,1)}, bf16[1,176,2048]{2,1,0:T(8,128)(2,1)S(1)}, u32[]{:S(2)}) copy-start(bf16[1,176,2048]{2,1,0:T(8,128)(2,1)S(1)} %collective-permute-done.4) | copy-start | bytes 2162692
  205.0 83.8 %all-to-all-start.1 = ((bf16[32,24,2048]{2,1,0:T(8,128)(2,1)}), bf16[32,24,2048]{2,1,0:T(8,128)(2,1)S(1)}, u32[]{:S(2)}, u32[]{:S(2)}) async-start(bf16[32,24,2048]{2,1,0:T(8,128)(2,1)} %bitcast.87), calls=%async_computation.1 | async-start | bytes 6291456 | tf_op jit(solution)/shard_map/all_to_all | solution.py:156
Sparse Core Ops, SparseCore 0:
  42.2 42.1 all-gather.4
  86.7 41.3 all-gather.2
  169.6 40.9 reduce-scatter.4
  213.0 43.2 reduce-scatter.2

commit v12 on v11

--- a/solution.py
+++ b/solution.py
@@ -152,9 +152,12 @@
     hidden_grad = contract_cols(grad_rows, down_full)
     up_grad = (hidden_grad * silu_slope(up_act)).astype(jnp.bfloat16)
     input_part = contract_cols(up_grad, up_full).astype(jnp.bfloat16)
-    input_part, down_moments = lax.optimization_barrier((input_part, down_moments))
+    out_rows = contract_rows(take_token, expert_out).astype(jnp.bfloat16)
+    input_part, down_moments, out_rows = lax.optimization_barrier(
+        (input_part, down_moments, out_rows)
+    )
     both_back = lax.all_to_all(
-        (contract_rows(take_token, expert_out) + contract_rows(take_grad, input_part))
+        (out_rows.astype(jnp.float32) + contract_rows(take_grad, input_part))
         .astype(jnp.bfloat16)
         .reshape(experts, 2 * capacity, model_width),
         "expert",

time: 299 us -> 299 us (level)
  no operation moved by 1% of the time
where the time goes in v12:
time: 299 us
  waiting for transfers between devices  182 us (61%)
  matrix products  54.6 us (18%)
  starting transfers between devices  26.3 us (9%)
  other arithmetic  15.9 us (5%)
  between operations  14.7 us (5%)
  local copies, waits for them, and re-layouts  5.1 us (2%)
    all_to_all x1, waiting for transfers between devices, body(): lax.all_to_all(send_both.reshape(experts, 2 * capacity, model_width), 'ex...  71.4 us
    ppermute x5, waiting for transfers between devices, partner(): return lax.ppermute(value, axis, pairs)  46.5 us
    reduce_scatter x1, waiting for transfers between devices, body(): lax.psum_scatter(contract_rows(expert_rows, up_grad).astype(jnp.bfloat16)...  36.7 us
    all_to_all x1, waiting for transfers between devices, body(): lax.all_to_all((out_rows.astype(jnp.float32) + contract_rows(take_grad, i...  27.7 us
    dot_general x4, matrix products, contract_rows(): lax.dot_general(left, right, (((0,), (0,)), ((), ())), preferred_element_...  22.5 us
    dot_general x2, matrix products, contract_cols(): lax.dot_general(left, right, (((1,), (1,)), ((), ())), preferred_element_...  13.1 us
    all_to_all x1, starting transfers between devices, body(): lax.all_to_all(send_both.reshape(experts, 2 * capacity, model_width), 'ex...  11.3 us
    all_to_all x1, starting transfers between devices, body(): lax.all_to_all((out_rows.astype(jnp.float32) + contract_rows(take_grad, i...  9.91 us
  transfers between devices with their start and end apart: 11, of which 7 were waited for; matrix products, arithmetic and copies ran while one was open for 23% of the time, Pallas kernels for 0%

profile of v12, /device:TPU:6, one launch (start us, length us, event | category | flops | bytes accessed | tf_op | source)
XLA Modules:
  0.0 299.0 jit_solution(8840741779881835881)
XLA Ops:
  7.2 2.0 collective-permute-start
  13.1 1.3 dynamic_slice.3
  15.5 1.0 select_reduce_fusion
  16.5 1.3 pad_maximum_fusion
  17.8 2.7 multiply_convert_fusion
  20.5 6.0 %collective-permute-done = bf16[1,256,1408]{2,1,0:T(8,128)(2,1)S(1)} collective-permute-done((bf16[1,256,1408]{2,1,0:T(8,128)(2,1)}, bf16[1,256,1408]{2,1,0:T(8,128)(2,1)S(1)}, u32[]{:S(2)}, u32[]{:S(2)}) %collective-permute-start) | collective-permute-done | bytes 720928 | tf_op jit(solution)/shard_map/ppermute | solution.py:18
  26.5 14.5 %collective-permute-done.1 = bf16[1,176,2048]{2,1,0:T(8,128)(2,1)S(1)} collective-permute-done((bf16[1,176,2048]{2,1,0:T(8,128)(2,1)}, bf16[1,176,2048]{2,1,0:T(8,128)(2,1)S(1)}, u32[]{:S(2)}, u32[]{:S(2)}) %collective-permute-start.1) | collective-permute-done | bytes 720928 | tf_op jit(solution)/shard_map/ppermute | solution.py:18
  41.0 1.0 broadcast_select_fusion
  42.1 0.9 broadcast_select_fusion.3
  43.1 11.3 %all-to-all-start = ((bf16[32,24,2048]{2,1,0:T(8,128)(2,1)}), bf16[32,24,2048]{2,1,0:T(8,128)(2,1)S(1)}, u32[]{:S(2)}, u32[]{:S(2)}) async-start(bf16[32,24,2048]{2,1,0:T(8,128)(2,1)} %bitcast.2), calls=%async_computation | async-start | bytes 6291456 | tf_op jit(solution)/shard_map/all_to_all | solution.py:114
  54.4 1.9 collective-permute-start.3
  56.7 71.4 %all-to-all-done = bf16[32,24,2048]{2,1,0:T(8,128)(2,1)S(1)} async-done(((bf16[32,24,2048]{2,1,0:T(8,128)(2,1)}), bf16[32,24,2048]{2,1,0:T(8,128)(2,1)S(1)}, u32[]{:S(2)}, u32[]{:S(2)}) %all-to-all-start) | async-done | bytes 3145760 | tf_op jit(solution)/shard_map/all_to_all | solution.py:114
  128.1 2.6 convolution_convert_fusion.3
  130.6 2.6 convolution_convert_fusion.4
  133.3 7.3 %multiply_convert_fusion.1 = (bf16[384,1408]{1,0:T(8,128)(2,1)S(1)}, f32[384,1408]{1,0:T(8,128)}) fusion(bf16[384,2048]{1,0:T(8,128)(2,1)} %convolution_convert_fusion.3, bf16[1,2048,1408]{2,1,0:T(8,128)(2,1)} %all-gather.5.cloned.1.call-done), kind=kOutput, calls=%fused_computation.17 | convolution fusion | flops 2217295872 | bytes 10584064 | tf_op jit(solution)/shard_map/dot_general | solution.py:143
  140.6 5.0 %convolution_convert_fusion.1 = bf16[1408,2048]{1,0:T(8,128)(2,1)} fusion(bf16[384,1408]{1,0:T(8,128)(2,1)S(1)} %get-tuple-element.37, bf16[384,2048]{1,0:T(8,128)(2,1)S(1)} %copy-done.10), kind=kOutput, calls=%fused_computation.1 | convolution fusion | flops 2217476096 | bytes 8421376 | tf_op jit(solution)/shard_map/dot_general | solution.py:44
  145.6 23.9 %collective-permute-done.2 = bf16[2,256,1408]{2,1,0:T(8,128)(2,1)} collective-permute-done((bf16[2,256,1408]{2,1,0:T(8,128)(2,1)}, bf16[2,256,1408]{2,1,0:T(8,128)(2,1)}, u32[]{:S(2)}, u32[]{:S(2)}) %collective-permute-start.2) | collective-permute-done | bytes 1441824 | tf_op jit(solution)/shard_map/ppermute | solution.py:18
  169.7 7.2 %fusion.4 = bf16[384,1408]{1,0:T(8,128)(2,1)S(1)} fusion(bf16[384,2048]{1,0:T(8,128)(2,1)S(1)} %copy-done.10, bf16[1408,2048]{1,0:T(8,128)(2,1)} %bitcast.97, f32[384,1408]{1,0:T(8,128)} %get-tuple-element.65), kind=kOutput, calls=%fused_computation.10 | convolution fusion | flops 2219458560 | bytes 10584064 | tf_op jit(solution)/shard_map/dot_general | solution.py:50
  177.0 1.0 copy-done.11
  177.9 5.2 %convolution_convert_fusion = bf16[2048,1408]{1,0:T(8,128)(2,1)} fusion(bf16[384,2048]{1,0:T(8,128)(2,1)S(1)} %copy-done.9, bf16[384,1408]{1,0:T(8,128)(2,1)S(1)} %fusion.4), kind=kOutput, calls=%fused_computation | convolution fusion | flops 2217476096 | bytes 8421376 | tf_op jit(solution)/shard_map/dot_general | solution.py:44
  183.1 1.1 copy-done.2
  184.6 8.7 %convolution_convert_fusion.2 = bf16[768,2048]{1,0:T(8,128)(2,1)} fusion(bf16[384,1408]{1,0:T(8,128)(2,1)S(1)} %get-tuple-element.37, bf16[1408,2048]{1,0:T(8,128)(2,1)} %bitcast.98, s32[768]{0:T(1024)S(1)} %iota.33, s32[384]{0:T(512)S(1)} %get-tuple-element.57), kind=kOutput, calls=%fused_computation.8 | convolution fusion | flops 3425206272 | bytes 9998848 | tf_op jit(solution)/shard_map/dot_general | solution.py:44
  193.3 5.9 %fusion.5 = bf16[384,2048]{1,0:T(8,128)(2,1)S(1)} fusion(bf16[384,1408]{1,0:T(8,128)(2,1)} %copy-done.11, bf16[1,2048,1408]{2,1,0:T(8,128)(2,1)} %all-gather.5.cloned.1.call-done), kind=kOutput, calls=%fused_computation.13 | convolution fusion | flops 2215378944 | bytes 8421376 | tf_op jit(solution)/shard_map/dot_general | solution.py:50
  199.2 2.1 collective-permute-done.4
  201.3 3.6 %add_convert_fusion = bf16[768,2048]{1,0:T(8,128)(2,1)} fusion(bf16[768,2048]{1,0:T(8,128)(2,1)S(1)} %copy-done.8, bf16[384,2048]{1,0:T(8,128)(2,1)S(1)} %fusion.5, s32[768]{0:T(1024)S(1)} %iota.33, s32[384]{0:T(512)S(1)} %get-tuple-element.56), kind=kOutput, calls=%fused_computation.2 | convolution fusion | flops 1212973056 | bytes 7868928 | tf_op jit(solution)/shard_map/dot_general | solution.py:44
  205.0 9.9 %all-to-all-start.1 = ((bf16[32,24,2048]{2,1,0:T(8,128)(2,1)}), bf16[32,24,2048]{2,1,0:T(8,128)(2,1)S(1)}, u32[]{:S(2)}, u32[]{:S(2)}) async-start(bf16[32,24,2048]{2,1,0:T(8,128)(2,1)} %bitcast.87), calls=%async_computation.1 | async-start | bytes 6291456 | tf_op jit(solution)/shard_map/all_to_all | solution.py:159
  214.9 4.6 %fusion.23 = (bf16[176,2048]{1,0:T(8,128)(2,1)}, bf16[176,2048]{1,0:T(8,128)(2,1)}, bf16[176,2048]{1,0:T(8,128)(2,1)}) fusion(bf16[176,2048]{1,0:T(8,128)(2,1)} %reduce-scatter.5.cloned.1.call-done, bf16[1,176,2048]{2,1,0:T(8,128)(2,1)} %collective-permute-done.3, bf16[1,176,2048]{2,1,0:T(8,128)(2,1)} %param.21, pred[]{:T(512)} %bitcast.4, ...), kind=kLoop, calls=%fused_computation.39 | loop fusion | flops 7569408 | bytes 6488065 | tf_op jit(solution)/shard_map/convert_element_type | solution.py:39
  219.5 36.7 %reduce-scatter.3.cloned.1.call-done = bf16[256,1408]{1,0:T(8,128)(2,1)} async-done(((bf16[2048,1408]{1,0:T(8,128)(2,1)}), bf16[256,1408]{1,0:T(8,128)(2,1)}) %reduce-scatter.3.cloned.1.call-update) | async-done | bytes 720912 | tf_op jit(solution)/shard_map/reduce_scatter | solution.py:168
  256.3 4.7 %fusion.24 = (bf16[256,1408]{1,0:T(8,128)(2,1)}, bf16[256,1408]{1,0:T(8,128)(2,1)}, bf16[256,1408]{1,0:T(8,128)(2,1)}) fusion(bf16[256,1408]{1,0:T(8,128)(2,1)} %reduce-scatter.3.cloned.1.call-done, bf16[1,256,1408]{2,1,0:T(8,128)(2,1)} %param.19, bf16[2,256,1408]{2,1,0:T(8,128)(2,1)} %collective-permute-done.2, pred[]{:T(512)} %bitcast.4, ...), kind=kLoop, calls=%fused_computation.40 | loop fusion | flops 7569408 | bytes 6488065 | tf_op jit(solution)/shard_map/convert_element_type | solution.py:39
  261.0 27.7 %all-to-all-done.1 = bf16[32,24,2048]{2,1,0:T(8,128)(2,1)S(1)} async-done(((bf16[32,24,2048]{2,1,0:T(8,128)(2,1)}), bf16[32,24,2048]{2,1,0:T(8,128)(2,1)S(1)}, u32[]{:S(2)}, u32[]{:S(2)}) %all-to-all-start.1) | async-done | bytes 3145760 | tf_op jit(solution)/shard_map/all_to_all | solution.py:159
  288.7 1.3 convolution_convert_fusion.6
  290.0 2.4 convolution_convert_fusion.7
  (64 shorter events, 5.4 us)
Async XLA Ops:
  7.2 9.3 %copy-start = (bf16[1,256,1408]{2,1,0:T(8,128)(2,1)S(1)}, bf16[1,256,1408]{2,1,0:T(8,128)(2,1)}, u32[]{:S(2)}) copy-start(bf16[1,256,1408]{2,1,0:T(8,128)(2,1)} %param.19) | copy-start | bytes 2162692
  7.2 9.3 %copy-start.1 = (bf16[1,256,1408]{2,1,0:T(8,128)(2,1)S(1)}, bf16[1,256,1408]{2,1,0:T(8,128)(2,1)}, u32[]{:S(2)}) copy-start(bf16[1,256,1408]{2,1,0:T(8,128)(2,1)} %param.18) | copy-start | bytes 2162692
  7.2 126.1 %all-gather.5.cloned.1.call-start = ((), (), s32[]{:S(2)}) async-start(), calls=%async_computation.5 | async-start | bytes 6488064 | tf_op jit(solution)/shard_map/all_gather | solution.py:125
  7.2 19.3 %collective-permute-start = (bf16[1,256,1408]{2,1,0:T(8,128)(2,1)}, bf16[1,256,1408]{2,1,0:T(8,128)(2,1)S(1)}, u32[]{:S(2)}, u32[]{:S(2)}) collective-permute-start(bf16[1,256,1408]{2,1,0:T(8,128)(2,1)} %param.16), channel_id=1, source_target_pairs={{0,1},{1,0},{2,3},{3,2},{4,5},{5,4},{6,7},{7,6},{8,9},{9,8},{10,11... | collective-permute-start | bytes 2162696 | tf_op jit(solution)/shard_map/ppermute | solution.py:18
  9.2 31.8 %collective-permute-start.1 = (bf16[1,176,2048]{2,1,0:T(8,128)(2,1)}, bf16[1,176,2048]{2,1,0:T(8,128)(2,1)S(1)}, u32[]{:S(2)}, u32[]{:S(2)}) collective-permute-start(bf16[1,176,2048]{2,1,0:T(8,128)(2,1)} %param.17), channel_id=1, source_target_pairs={{0,1},{1,0},{2,3},{3,2},{4,5},{5,4},{6,7},{7,6},{8,9},{9,8},{10,11... | collective-permute-start | bytes 2162696 | tf_op jit(solution)/shard_map/ppermute | solution.py:18
  14.7 3.0 %copy-start.6 = (bf16[48,2048]{1,0:T(8,128)(2,1)S(1)}, bf16[48,2048]{1,0:T(8,128)(2,1)}, u32[]{:S(2)}) copy-start(bf16[48,2048]{1,0:T(8,128)(2,1)} %param.14) | copy-start | bytes 589828
  14.7 3.0 %copy-start.7 = (bf16[48,2048]{1,0:T(8,128)(2,1)S(1)}, bf16[48,2048]{1,0:T(8,128)(2,1)}, u32[]{:S(2)}) copy-start(bf16[48,2048]{1,0:T(8,128)(2,1)} %param.11) | copy-start | bytes 589828
  17.8 23.3 %copy-start.4 = (bf16[1,256,1408]{2,1,0:T(8,128)(2,1)S(1)}, bf16[1,256,1408]{2,1,0:T(8,128)(2,1)}, u32[]{:S(2)}) copy-start(bf16[1,256,1408]{2,1,0:T(8,128)(2,1)} %param.16) | copy-start | bytes 2162692
  20.5 21.6 %copy-start.5 = (bf16[1,176,2048]{2,1,0:T(8,128)(2,1)S(1)}, bf16[1,176,2048]{2,1,0:T(8,128)(2,1)}, u32[]{:S(2)}) copy-start(bf16[1,176,2048]{2,1,0:T(8,128)(2,1)} %param.17) | copy-start | bytes 2162692
  42.0 98.5 %all-gather.3.cloned.1.call-start = ((), (), s32[]{:S(2)}) async-start(), calls=%async_computation.4 | async-start | bytes 6488064 | tf_op jit(solution)/shard_map/all_gather | solution.py:126
  43.1 85.0 %all-to-all-start = ((bf16[32,24,2048]{2,1,0:T(8,128)(2,1)}), bf16[32,24,2048]{2,1,0:T(8,128)(2,1)S(1)}, u32[]{:S(2)}, u32[]{:S(2)}) async-start(bf16[32,24,2048]{2,1,0:T(8,128)(2,1)} %bitcast.2), calls=%async_computation | async-start | bytes 6291456 | tf_op jit(solution)/shard_map/all_to_all | solution.py:114
  54.4 160.5 %reduce-scatter.5.cloned.1.call-start = ((), (), s32[]{:S(2)}) async-start(), calls=%async_computation.7 | async-start | bytes 6488064 | tf_op jit(solution)/shard_map/reduce_scatter | solution.py:174
  54.4 91.1 %collective-permute-start.3 = (bf16[1,176,2048]{2,1,0:T(8,128)(2,1)}, bf16[1,176,2048]{2,1,0:T(8,128)(2,1)}, u32[]{:S(2)}, u32[]{:S(2)}) collective-permute-start(bf16[1,176,2048]{2,1,0:T(8,128)(2,1)} %param.21), channel_id=1, source_target_pairs={{0,1},{1,0},{2,3},{3,2},{4,5},{5,4},{6,7},{7,6},{8,9},{9,8},{10,11... | collective-permute-start | bytes 2162696 | tf_op jit(solution)/shard_map/ppermute | solution.py:18
  56.3 113.1 %collective-permute-start.2 = (bf16[2,256,1408]{2,1,0:T(8,128)(2,1)}, bf16[2,256,1408]{2,1,0:T(8,128)(2,1)}, u32[]{:S(2)}, u32[]{:S(2)}) collective-permute-start(bf16[2,256,1408]{2,1,0:T(8,128)(2,1)} %pad_maximum_fusion), channel_id=1, source_target_pairs={{0,1},{1,0},{2,3},{3,2},{4,5},{5,4},{6,7},{7,6},{8,9},{9,8},{10,11... | collective-permute-start | bytes 4325384 | tf_op jit(solution)/shard_map/ppermute | solution.py:18
  133.3 7.3 %copy-start.10 = (bf16[384,2048]{1,0:T(8,128)(2,1)S(1)}, bf16[384,2048]{1,0:T(8,128)(2,1)}, u32[]{:S(2)}) copy-start(bf16[384,2048]{1,0:T(8,128)(2,1)} %convolution_convert_fusion.4) | copy-start | bytes 4718596
  169.5 86.8 %reduce-scatter.3.cloned.1.call-start = ((), (), s32[]{:S(2)}) async-start(), calls=%async_computation.6 | async-start | bytes 6488064 | tf_op jit(solution)/shard_map/reduce_scatter | solution.py:168
  169.7 8.2 %copy-start.9 = (bf16[384,2048]{1,0:T(8,128)(2,1)S(1)}, bf16[384,2048]{1,0:T(8,128)(2,1)}, u32[]{:S(2)}) copy-start(bf16[384,2048]{1,0:T(8,128)(2,1)} %convolution_convert_fusion.3) | copy-start | bytes 4718596
  176.9 1.0 copy-start.11
  183.1 1.1 copy-start.2
  184.2 17.1 %collective-permute-start.4 = (bf16[1,176,2048]{2,1,0:T(8,128)(2,1)S(1)}, bf16[1,176,2048]{2,1,0:T(8,128)(2,1)S(1)}, u32[]{:S(2)}, u32[]{:S(2)}) collective-permute-start(bf16[1,176,2048]{2,1,0:T(8,128)(2,1)S(1)} %copy-done.2), channel_id=1, source_target_pairs={{0,1},{1,0},{2,3},{3,2},{4,5},{5,4},{6,7},{7,6},{8,9},{9,8},{10,11... | collective-permute-start | bytes 2162696 | tf_op jit(solution)/shard_map/ppermute | solution.py:18
  193.3 8.0 %copy-start.8 = (bf16[768,2048]{1,0:T(8,128)(2,1)S(1)}, bf16[768,2048]{1,0:T(8,128)(2,1)}, u32[]{:S(2)}) copy-start(bf16[768,2048]{1,0:T(8,128)(2,1)} %convolution_convert_fusion.2) | copy-start | bytes 9437188
  201.3 3.6 %copy-start.3 = (bf16[1,176,2048]{2,1,0:T(8,128)(2,1)}, bf16[1,176,2048]{2,1,0:T(8,128)(2,1)S(1)}, u32[]{:S(2)}) copy-start(bf16[1,176,2048]{2,1,0:T(8,128)(2,1)S(1)} %collective-permute-done.4) | copy-start | bytes 2162692
  205.0 83.8 %all-to-all-start.1 = ((bf16[32,24,2048]{2,1,0:T(8,128)(2,1)}), bf16[32,24,2048]{2,1,0:T(8,128)(2,1)S(1)}, u32[]{:S(2)}, u32[]{:S(2)}) async-start(bf16[32,24,2048]{2,1,0:T(8,128)(2,1)} %bitcast.87), calls=%async_computation.1 | async-start | bytes 6291456 | tf_op jit(solution)/shard_map/all_to_all | solution.py:159
Sparse Core Ops, SparseCore 0:
  42.2 42.1 all-gather.4
  86.7 41.3 all-gather.2
  169.6 40.9 reduce-scatter.4
  213.0 43.2 reduce-scatter.2
